TPU v7x, 256 devices: a whole 4x4x8 slice. The times are simulated.
256 devices in a mesh: space: 16 (over x, z_hi), snap: 16 (over y, z_lo, core).
Axes of the slice: x: 4, y: 4, z: 8 (z_hi: 4, z_lo: 2; z = z_hi * 2 + z_lo), core: 2. Of those that a mesh axis runs over, the one named last changes fastest.
Arguments:
- velocity: bfloat16 [256, 3, 128, 32, 128], P('snap', None, 'space'), may hold values from -40 to 40
- phase_bins: int32 [256], replicated, may hold values from 0 to 23, as said below
- tile_owner: int32 [16], replicated, may hold values from 0 to 15, each once
Outputs:
- gram_tiles: float32 [16, 16, 256], P('space', None, 'snap')
Inputs may be any that keep to these rules, and one draw needn't show every extreme that they name: `phase_bins`: every bin holds at least one snapshot. `tile_owner`: each tile has exactly one owner.
All inputs are finite; a program needn't handle non-finite values.
Results may differ from a plain program's by a relative error of at most 0.0003.
Values may be sent and summed in bfloat16 or wider, within the bound.
No kernel may reach another device: no remote copies, remote signals or barrier semaphores. Data moves between devices by JAX's collectives and lax.ppermute only.
A program may use at most 128 MiB of HBM per device.

v0:
```python
import jax
import jax.numpy as jnp
from jax import lax
from jax.sharding import PartitionSpec as P

NB = 24


def with_halo(block, sides, width):
    for axis, dim in sides:
        count = lax.axis_size(axis)
        forward = [(i, i + 1) for i in range(count - 1)]
        backward = [(target, source) for source, target in forward]
        low = lax.ppermute(
            lax.slice_in_dim(block, block.shape[dim] - width, None, axis=dim), axis, forward
        )
        high = lax.ppermute(lax.slice_in_dim(block, 0, width, axis=dim), axis, backward)
        block = jnp.concatenate([low, block, high], axis=dim)
    return block


def widen(field_in, direction):
    widths = [(0, 0)] * field_in.ndim
    widths[direction] = (2, 2)
    return jnp.pad(field_in, widths)


def derivative(padded_field, direction):
    length = padded_field.shape[direction] - 4

    def window_at(offset):
        return lax.slice_in_dim(padded_field, offset, offset + length, axis=direction)

    return (8.0 * (window_at(3) - window_at(1)) - (window_at(4) - window_at(0))) / 12.0


def curl_field(u_field, v_field, w_field, v_wide, w_wide, first):
    second = first + 1
    third = first + 2
    omega_x = derivative(widen(w_field, second), second) - derivative(widen(v_field, third), third)
    omega_y = derivative(widen(u_field, third), third) - derivative(w_wide, first)
    omega_z = derivative(v_wide, first) - derivative(widen(u_field, second), second)
    return jnp.stack([omega_x, omega_y, omega_z], axis=first)


def per_device(velocity, phase_bins, tile_owner):
    widened = with_halo(velocity, (("space", 2),), 2).astype(jnp.float32)
    v_wide = widened[:, 1]
    w_wide = widened[:, 2]
    frame_float = velocity.astype(jnp.float32)
    vortex = curl_field(
        frame_float[:, 0], frame_float[:, 1], frame_float[:, 2], v_wide, w_wide, 1
    ).astype(jnp.bfloat16)
    snaps_dev, _, cells_x, cells_y, cells_z = vortex.shape
    flattened = vortex.reshape(snaps_dev, 3, cells_x * cells_y * cells_z)
    arranged = lax.all_to_all(flattened, "snap", split_axis=2, concat_axis=0, tiled=True)
    total_snaps = arranged.shape[0]
    columns = arranged.reshape(total_snaps, -1)
    onehot = (phase_bins[None, :] == jnp.arange(NB, dtype=jnp.int32)[:, None]).astype(jnp.bfloat16)
    bin_counts = jnp.sum(onehot.astype(jnp.float32), axis=1)
    bin_sums = jnp.dot(onehot, columns, preferred_element_type=jnp.float32)
    bin_means = bin_sums / bin_counts[:, None]
    fluctuation = (columns.astype(jnp.float32) - jnp.take(bin_means, phase_bins, axis=0)).astype(
        jnp.bfloat16
    )
    voxel_total = lax.axis_size("space") * cells_x * cells_y * cells_z
    partial_gram = (
        lax.dot_general(
            fluctuation, fluctuation, (((1,), (1,)), ((), ())), preferred_element_type=jnp.float32
        )
        / voxel_total
    )
    tile_count = lax.axis_size("space")
    tile_ids = jnp.arange(tile_count, dtype=jnp.int32)
    inverse = jnp.sum(
        tile_ids[None, :] * (tile_owner[None, :] == tile_ids[:, None]).astype(jnp.int32), axis=1
    )
    blocks = jnp.take(
        partial_gram.reshape(tile_count, total_snaps // tile_count, total_snaps), inverse, axis=0
    )
    rows_done = lax.psum_scatter(blocks, "space", scatter_dimension=0, tiled=True)
    return lax.psum_scatter(rows_done, "snap", scatter_dimension=2, tiled=True)


def solution(mesh):
    return jax.shard_map(
        per_device,
        mesh=mesh,
        in_specs=(P("snap", None, "space", None, None), P(), P()),
        out_specs=P("space", None, "snap"),
        check_vma=False,
    )
```

profile of v0, /device:TPU:1, one launch (start us, length us, event | category | flops | bytes accessed | tf_op | source)
XLA Modules:
  0.0 428.7 jit_solution(14037773328832607324)
XLA Ops:
  6.5 0.0 slice-start
  6.5 0.0 copy-start.2
  6.5 1.1 slice-done
  7.7 1.0 copy.77
  8.6 1.3 collective-permute-start.1
  9.9 2.1 slice.108
  12.0 7.2 %collective-permute-start = (bf16[16,3,2,32,128]{4,3,2,1,0:T(8,128)(2,1)}, bf16[16,3,2,32,128]{4,3,2,1,0:T(8,128)(2,1)}, u32[]{:S(2)}, u32[]{:S(2)}) collective-permute-start(bf16[16,3,2,32,128]{4,3,2,1,0:T(8,128)(2,1)} %slice.108), channel_id=1, source_target_pairs={{0,16},{16,32},{32,48},{48,64},{64,80},{80,96},{96,112},{112,128},... | collective-permute-start | bytes 2359304 | tf_op jit(solution)/shard_map/ppermute | solution.py:14
  19.3 0.0 copy-done.2
  19.3 0.8 convert_element_type.33
  20.1 2.4 slice_bitcast_fusion.1
  22.5 0.0 copy-start.3
  22.5 3.1 fusion.7
  25.6 2.3 stack.12
  27.9 0.0 copy-start.4
  27.9 20.2 %collective-permute-done.1 = bf16[16,3,2,32,128]{4,3,2,0,1:T(8,128)(2,1)} collective-permute-done((bf16[16,3,2,32,128]{4,3,2,0,1:T(8,128)(2,1)}, bf16[16,3,2,32,128]{4,3,2,0,1:T(8,128)(2,1)}, u32[]{:S(2)}, u32[]{:S(2)}) %collective-permute-start.1) | collective-permute-done | bytes 786464 | tf_op jit(solution)/shard_map/ppermute | solution.py:17
  48.2 0.0 collective-permute-done
  48.2 0.0 copy-done.3
  48.2 2.0 convert_bitcast_fusion
  50.2 0.0 copy-done.4
  50.2 4.2 fusion.26
  54.4 1.3 stack.13
  55.7 1.2 stack.14
  56.9 2.2 pad_maximum_fusion
  59.1 31.0 %copy.55 = bf16[16,3,32768]{0,1,2:T(4,128)(2,1)} copy(bf16[16,3,32768]{2,0,1:T(8,128)(2,1)S(1)} %pad_maximum_fusion) | data formatting | bytes 6291456 | tf_op jit(solution)/shard_map/stack | solution.py:43
  90.1 29.5 %reshape.77 = bf16[16,2,49152]{2,1,0:T(2,128)(2,1)} reshape(bf16[32768,3,16]{2,1,0:T(4,128)(2,1)} %bitcast.45) | data formatting | bytes 6291456
  119.6 0.0 copy-start.5
  119.6 0.0 copy-start.6
  119.6 10.7 %all-to-all-start = ((bf16[16,2,49152]{2,1,0:T(2,128)(2,1)}), bf16[16,2,49152]{2,1,0:T(2,128)(2,1)S(1)}, u32[]{:S(2)}, u32[]{:S(2)}) async-start(bf16[16,2,49152]{2,1,0:T(2,128)(2,1)} %reshape.77), calls=%async_computation | async-start | bytes 6291456 | tf_op jit(solution)/shard_map/all_to_all | solution.py:56
  130.2 0.0 reduce-scatter.5.cloned.1.call-start
  130.3 0.0 copy-done.5
  130.3 0.1 broadcast_in_dim.31
  130.4 0.1 copy.57
  130.5 0.0 copy-done.6
  130.5 0.1 select_reduce_fusion
  130.6 0.1 convert_reduce_fusion
  130.8 37.6 %all-to-all-done = bf16[16,2,49152]{2,1,0:T(2,128)(2,1)S(1)} async-done(((bf16[16,2,49152]{2,1,0:T(2,128)(2,1)}), bf16[16,2,49152]{2,1,0:T(2,128)(2,1)S(1)}, u32[]{:S(2)}, u32[]{:S(2)}) %all-to-all-start) | async-done | bytes 3145760 | tf_op jit(solution)/shard_map/all_to_all | solution.py:56
  168.4 32.7 %reshape.78 = bf16[32768,3,16]{2,1,0:T(4,128)(2,1)} reshape(bf16[16,2,49152]{2,1,0:T(2,128)(2,1)S(1)} %all-to-all-done) | data formatting | bytes 6291456
  201.2 30.1 %copy.61 = bf16[16,3,16,2048]{3,2,0,1:T(8,128)(2,1)S(1)} copy(bf16[16,3,16,2048]{0,1,3,2:T(4,128)(2,1)} %bitcast.46) | data formatting | bytes 6291456 | tf_op jit(solution)/shard_map/all_to_all | solution.py:56
  231.2 0.0 copy-start
  231.2 2.7 copy.58
  233.9 0.0 copy-done
  234.0 3.3 copy.66
  237.3 0.5 convolution_divide_fusion
  237.8 5.2 %gather_fusion = f32[256,6144]{1,0:T(8,128)} fusion(f32[24,6144]{1,0:T(8,128)S(1)} %convolution_divide_fusion, s32[1024]{0:T(1024)S(1)} %pad_clamp_fusion.1), kind=kCustom, calls=%fused_computation | custom fusion | bytes 12583936 | tf_op jit(solution)/shard_map/jit(_take)/gather | solution.py:63
  243.0 0.0 copy-start.1
  243.0 11.5 %gather.11 = f32[16,16,3,2048]{3,2,1,0:T(4,128)} reshape(f32[256,6144]{1,0:T(8,128)} %gather_fusion) | data formatting | bytes 12582912 | tf_op jit(solution)/shard_map/jit(_take)/gather | solution.py:63
  254.5 0.0 copy-done.1
  254.5 7.4 %fusion.1 = bf16[16,16,3,2048]{3,0,1,2:T(8,128)(2,1)S(1)} fusion(f32[16,16,3,2048]{3,2,1,0:T(4,128)} %gather.11, pred[16,16]{0,1:T(8,128)(4,1)S(1)} %copy.57, bf16[16,3,16,2048]{3,2,0,1:T(8,128)(2,1)S(1)} %copy-done.1), kind=kLoop, calls=%fused_computation.13 | loop fusion | flops 6291456 | bytes 12583168 | tf_op jit(solution)/shard_map/convert_element_type | solution.py:63
  261.9 2.7 copy.60
  264.6 3.3 copy.67
  267.9 1.0 convolution_multiply_fusion
  268.9 0.6 gather_fusion.1
  269.5 0.8 broadcast_select_fusion
  270.3 0.0 reduce-scatter.5.cloned.1.call-update
  270.3 0.0 reduce-scatter.7.cloned.1.call-start
  270.4 87.7 %reduce-scatter.5.cloned.1.call-done = f32[1,16,256]{2,1,0:T(8,128)} async-done(((f32[16,16,256]{2,1,0:T(8,128)}), f32[1,16,256]{2,1,0:T(8,128)}) %reduce-scatter.5.cloned.1.call-update) | async-done | bytes 16400 | tf_op jit(solution)/shard_map/reduce_scatter | solution.py:81
  358.0 1.5 copy.62
  359.5 0.0 reduce-scatter.7.cloned.1.call-update
  359.5 60.9 %reduce-scatter.7.cloned.1.call-done = f32[16,16]{1,0:T(8,128)} async-done(((f32[256,16]{1,0:T(8,128)}), f32[16,16]{1,0:T(8,128)}) %reduce-scatter.7.cloned.1.call-update) | async-done | bytes 1040
  420.5 1.4 copy.63
  (6 shorter events, 0.0 us)
Async XLA Ops:
  6.5 1.1 slice-start
  6.5 12.7 %copy-start.2 = (bf16[16,3,8,32,128]{4,3,2,1,0:T(8,128)(2,1)S(1)}, bf16[16,3,8,32,128]{4,3,2,1,0:T(8,128)(2,1)}, u32[]{:S(2)}) copy-start(bf16[16,3,8,32,128]{4,3,2,1,0:T(8,128)(2,1)} %param.3) | copy-start | bytes 9437188
  8.6 39.5 %collective-permute-start.1 = (bf16[16,3,2,32,128]{4,3,2,0,1:T(8,128)(2,1)}, bf16[16,3,2,32,128]{4,3,2,0,1:T(8,128)(2,1)}, u32[]{:S(2)}, u32[]{:S(2)}) collective-permute-start(bf16[16,3,2,32,128]{4,3,2,0,1:T(8,128)(2,1)} %copy.77), channel_id=1, source_target_pairs={{16,0},{32,16},{48,32},{64,48},{80,64},{96,80},{112,96},{128,112},... | collective-permute-start | bytes 2359304 | tf_op jit(solution)/shard_map/ppermute | solution.py:17
  12.0 36.1 %collective-permute-start = (bf16[16,3,2,32,128]{4,3,2,1,0:T(8,128)(2,1)}, bf16[16,3,2,32,128]{4,3,2,1,0:T(8,128)(2,1)}, u32[]{:S(2)}, u32[]{:S(2)}) collective-permute-start(bf16[16,3,2,32,128]{4,3,2,1,0:T(8,128)(2,1)} %slice.108), channel_id=1, source_target_pairs={{0,16},{16,32},{32,48},{48,64},{64,80},{80,96},{96,112},{112,128},... | collective-permute-start | bytes 2359304 | tf_op jit(solution)/shard_map/ppermute | solution.py:14
  22.5 25.7 %copy-start.3 = (bf16[16,3,8,32,128]{4,3,2,1,0:T(8,128)(2,1)S(1)}, bf16[16,3,8,32,128]{4,3,2,1,0:T(8,128)(2,1)}, u32[]{:S(2)}) copy-start(bf16[16,3,8,32,128]{4,3,2,1,0:T(8,128)(2,1)} %param.3) | copy-start | bytes 9437188
  27.9 22.2 %copy-start.4 = (f32[16,8,32,128]{3,2,1,0:T(8,128)S(1)}, f32[16,8,32,128]{3,2,1,0:T(8,128)}, u32[]{:S(2)}) copy-start(f32[16,8,32,128]{3,2,1,0:T(8,128)} %get-tuple-element.7) | copy-start | bytes 6291460
  119.6 10.7 %copy-start.5 = (s32[256]{0:T(256)S(1)}, s32[256]{0:T(256)}, u32[]{:S(2)}) copy-start(s32[256]{0:T(256)} %param.4) | copy-start | bytes 3076
  119.6 10.9 %copy-start.6 = (s32[16]{0:T(128)S(1)}, s32[16]{0:T(128)}, u32[]{:S(2)}) copy-start(s32[16]{0:T(128)} %param.5) | copy-start | bytes 196
  119.6 48.8 %all-to-all-start = ((bf16[16,2,49152]{2,1,0:T(2,128)(2,1)}), bf16[16,2,49152]{2,1,0:T(2,128)(2,1)S(1)}, u32[]{:S(2)}, u32[]{:S(2)}) async-start(bf16[16,2,49152]{2,1,0:T(2,128)(2,1)} %reshape.77), calls=%async_computation | async-start | bytes 6291456 | tf_op jit(solution)/shard_map/all_to_all | solution.py:56
  130.2 227.8 %reduce-scatter.5.cloned.1.call-start = ((), (), s32[]{:S(2)}) async-start(), calls=%async_computation.3 | async-start | bytes 278528 | tf_op jit(solution)/shard_map/reduce_scatter | solution.py:81
  231.2 2.7 copy-start
  243.0 11.5 %copy-start.1 = (bf16[16,3,16,2048]{3,2,0,1:T(8,128)(2,1)S(1)}, bf16[16,3,16,2048]{3,2,0,1:T(8,128)(2,1)}, u32[]{:S(2)}) copy-start(bf16[16,3,16,2048]{3,2,0,1:T(8,128)(2,1)} %copy-done) | copy-start | bytes 9437188
  270.3 150.1 %reduce-scatter.7.cloned.1.call-start = ((), (), s32[]{:S(2)}) async-start(), calls=%async_computation.4 | async-start | bytes 139264
Sparse Core Ops, SparseCore 0:
  270.4 87.5 reduce-scatter.4
  360.5 59.8 reduce-scatter.6
where the time goes:
time: 433 us; the launch traced here: 429 us
  waiting for transfers between devices  207 us (48%)
  local copies, waits for them, and re-layouts  167 us (39%)
  other arithmetic  20.8 us (5%)
  starting transfers between devices  19.3 us (4%)
  between operations  13.6 us (3%)
    reduce_scatter x1, waiting for transfers between devices, per_device(): lax.psum_scatter(blocks, 'space', scatter_dimension=0, tiled=True)  87.7 us
    unnamed x21, local copies, waits for them, and re-layouts  72.7 us
    unnamed x3, waiting for transfers between devices  61 us
    all_to_all x1, waiting for transfers between devices, per_device(): lax.all_to_all(flattened, 'snap', split_axis=2, concat_axis=0, tiled=True)  37.6 us
    another operation x4, local copies, waits for them, and re-layouts, curl_field(): return jnp.stack([omega_x, omega_y, omega_z], axis=first)  35.8 us
    all_to_all x2, local copies, waits for them, and re-layouts, per_device(): lax.all_to_all(flattened, 'snap', split_axis=2, concat_axis=0, tiled=True)  32.8 us
    ppermute x1, waiting for transfers between devices, with_halo(): lax.ppermute(lax.slice_in_dim(block, 0, width, axis=dim), axis, backward)  20.2 us
    gather x2, local copies, waits for them, and re-layouts, per_device(): jnp.take(bin_means, phase_bins, axis=0)  16.7 us
  transfers between devices with their start and end apart: 5, of which 4 were waited for; matrix products, arithmetic and copies ran while one was open for 3% of the time, Pallas kernels for 0%

commit v1 on v0

v1 whole, which is shorter than its diff:
```python
import jax
import jax.numpy as jnp
from jax import lax
from jax.sharding import PartitionSpec as P

NB = 24


def x_halo(block, width):
    count = lax.axis_size("space")
    forward = [(i, i + 1) for i in range(count - 1)]
    backward = [(target, source) for source, target in forward]
    low = lax.ppermute(block[:, :, block.shape[2] - width :], "space", forward)
    high = lax.ppermute(block[:, :, :width], "space", backward)
    return jnp.concatenate([low, block, high], axis=2)


def stencil(window_at):
    return (8.0 * (window_at(3) - window_at(1)) - (window_at(4) - window_at(0))) / 12.0


def d_padded(field, axis):
    widths = [(0, 0)] * field.ndim
    widths[axis] = (2, 2)
    padded = jnp.pad(field, widths)
    length = field.shape[axis]
    return stencil(lambda o: lax.slice_in_dim(padded, o, o + length, axis=axis))


def d_wide(wide, axis):
    length = wide.shape[axis] - 4
    return stencil(lambda o: lax.slice_in_dim(wide, o, o + length, axis=axis))


def all_to_all_sum(x, axis):
    got = lax.all_to_all(x, axis, split_axis=0, concat_axis=0, tiled=True)
    return jnp.sum(got, axis=0)


def per_device(velocity, phase_bins, tile_owner):
    snaps_dev, _, cells_x, cells_y, cells_z = velocity.shape
    vw_wide = x_halo(velocity[:, 1:3], 2).astype(jnp.float32)
    frame = velocity.astype(jnp.float32)
    u, v, w = frame[:, 0], frame[:, 1], frame[:, 2]
    v_wide, w_wide = vw_wide[:, 0], vw_wide[:, 1]
    omega_x = d_padded(w, 2) - d_padded(v, 3)
    omega_y = d_padded(u, 3) - d_wide(w_wide, 1)
    omega_z = d_wide(v_wide, 1) - d_padded(u, 2)
    vortex = jnp.stack([omega_x, omega_y, omega_z], axis=1).astype(jnp.bfloat16)

    n_snap = lax.axis_size("snap")
    halves = n_snap // cells_x
    rows = cells_y // halves
    parts = vortex.reshape(snaps_dev, 3, cells_x, halves, rows, cells_z)
    parts = jnp.transpose(parts, (2, 3, 0, 1, 4, 5)).reshape(n_snap, snaps_dev, 3, rows, cells_z)
    arranged = lax.all_to_all(parts, "snap", split_axis=0, concat_axis=0, tiled=True)
    total_snaps = n_snap * snaps_dev
    columns = arranged.reshape(total_snaps, 3 * rows, cells_z)

    onehot = (phase_bins[None, :] == jnp.arange(NB, dtype=jnp.int32)[:, None])
    bin_counts = jnp.sum(onehot.astype(jnp.float32), axis=1)
    bin_sums = jnp.einsum(
        "bs,skz->bkz", onehot.astype(jnp.bfloat16), columns, preferred_element_type=jnp.float32
    )
    bin_means = bin_sums / bin_counts[:, None, None]
    selected = jnp.einsum(
        "sb,bkz->skz",
        onehot.T.astype(jnp.float32),
        bin_means,
        precision=lax.Precision.HIGHEST,
        preferred_element_type=jnp.float32,
    )
    fluctuation = (columns.astype(jnp.float32) - selected).astype(jnp.bfloat16)
    voxel_total = lax.axis_size("space") * cells_x * cells_y * cells_z
    partial_gram = (
        jnp.einsum("skz,tkz->st", fluctuation, fluctuation, preferred_element_type=jnp.float32)
        / voxel_total
    )

    row_blocks = partial_gram.reshape(n_snap, total_snaps // n_snap, total_snaps)
    col_sum = all_to_all_sum(row_blocks, "snap")
    tile_count = lax.axis_size("space")
    tile_ids = jnp.arange(tile_count, dtype=jnp.int32)
    inverse = jnp.sum(
        tile_ids[None, :] * (tile_owner[None, :] == tile_ids[:, None]).astype(jnp.int32), axis=1
    )
    tiles = col_sum.reshape(col_sum.shape[0], tile_count, total_snaps // tile_count)
    tiles = jnp.transpose(jnp.take(tiles, inverse, axis=1), (1, 2, 0))
    mine = all_to_all_sum(tiles, "space")
    return mine[None]


def solution(mesh):
    return jax.shard_map(
        per_device,
        mesh=mesh,
        in_specs=(P("snap", None, "space", None, None), P(), P()),
        out_specs=P("space", None, "snap"),
        check_vma=False,
    )
```

time: 433 us -> 127 us (0.29)
  local copies, waits for them, and re-layouts: 167 us -> 8.3 us
  waiting for transfers between devices: 207 us -> 60.5 us
  blocking collectives: 0 us -> 20.5 us
  between operations: 13.6 us -> 0.22 us
  other arithmetic: 20.8 us -> 11.3 us
    reduce_scatter x1 -> x0, waiting for transfers between devices: 87.7 us -> none  [per_device(): lax.psum_scatter(blocks, 'space', scatter_dimension=0, tiled=True)]
    unnamed x21 -> x9, local copies, waits for them, and re-layouts: 72.7 us -> 0.25 us
    unnamed x3 -> x0, waiting for transfers between devices: 61 us -> none
    another operation x4 -> x3, local copies, waits for them, and re-layouts: 35.8 us -> 2.04 us  [per_device(): vortex = jnp.stack([omega_x, omega_y, omega_z], axis=1).astype(jnp.bfloat16)]
    all_to_all x2, local copies, waits for them, and re-layouts: 32.8 us -> 1.41 us  [the longest x1 0.9 us: per_device(): lax.all_to_all(parts, 'snap', split_axis=0, concat_axis=0, tiled=True)]
    all_to_all x0 -> x1, blocking collectives: none -> 20.5 us  [all_to_all_sum(): got = lax.all_to_all(x, axis, split_axis=0, concat_axis=0, tiled=True)]
    gather x3 -> x1, local copies, waits for them, and re-layouts: 17.3 us -> 0.57 us  [per_device(): tiles = jnp.transpose(jnp.take(tiles, inverse, axis=1), (1, 2, 0))]
    all_to_all x1 -> x2, waiting for transfers between devices: 37.6 us -> 45.2 us  [the longest x1 37.9 us: per_device(): lax.all_to_all(parts, 'snap', split_axis=0, concat_axis=0, tiled=True)]
  transfers between devices with their start and end apart: 5 -> 4, of which waited for: 4 -> 3; matrix products, arithmetic and copies ran while one was open for 3% -> 4% of each run, Pallas kernels for 0% -> 0%
where the time goes in v1:
time: 127 us; the launch traced here: 126 us
  waiting for transfers between devices  60.5 us (48%)
  starting transfers between devices  20.5 us (16%)
  blocking collectives  20.5 us (16%)
  other arithmetic  11.3 us (9%)
  local copies, waits for them, and re-layouts  8.3 us (7%)
  matrix products  5.08 us (4%)
    all_to_all x1, waiting for transfers between devices, per_device(): lax.all_to_all(parts, 'snap', split_axis=0, concat_axis=0, tiled=True)  37.9 us
    all_to_all x1, blocking collectives, all_to_all_sum(): got = lax.all_to_all(x, axis, split_axis=0, concat_axis=0, tiled=True)  20.5 us
    ppermute x1, waiting for transfers between devices, x_halo(): high = lax.ppermute(block[:, :, :width], 'space', backward)  15.3 us
    all_to_all x1, starting transfers between devices, per_device(): lax.all_to_all(parts, 'snap', split_axis=0, concat_axis=0, tiled=True)  8.59 us
    all_to_all x1, waiting for transfers between devices, all_to_all_sum(): got = lax.all_to_all(x, axis, split_axis=0, concat_axis=0, tiled=True)  7.22 us
    another operation x2, other arithmetic  6.58 us
    ppermute x1, starting transfers between devices, x_halo(): low = lax.ppermute(block[:, :, block.shape[2] - width:], 'space', forward)  6.37 us
    all_to_all x1, starting transfers between devices, all_to_all_sum(): got = lax.all_to_all(x, axis, split_axis=0, concat_axis=0, tiled=True)  4.29 us
  transfers between devices with their start and end apart: 4, of which 3 were waited for; matrix products, arithmetic and copies ran while one was open for 4% of the time, Pallas kernels for 0%

profile of v1, /device:TPU:1, one launch (start us, length us, event | category | flops | bytes accessed | tf_op | source)
XLA Modules:
  0.0 126.5 jit_solution(17841112616173321267)
XLA Ops:
  0.0 0.0 copy-start
  0.0 1.4 %fusion.42 = (bf16[16,2,2,32,128]{4,3,2,1,0:T(8,128)(2,1)S(1)}, bf16[16,2,2,32,128]{4,3,2,1,0:T(8,128)(2,1)S(1)}) fusion(bf16[16,3,8,32,128]{4,3,2,1,0:T(8,128)(2,1)} %param.3), kind=kLoop, calls=%fused_computation.79 | loop fusion | bytes 2097152 | tf_op jit(solution)/shard_map/slice | solution.py:13
  1.5 1.3 %collective-permute-start.1 = (bf16[16,2,2,32,128]{4,3,2,0,1:T(8,128)(2,1)S(1)}, bf16[16,2,2,32,128]{4,3,2,0,1:T(8,128)(2,1)S(1)}, u32[]{:S(2)}, u32[]{:S(2)}) collective-permute-start(bf16[16,2,2,32,128]{4,3,2,0,1:T(8,128)(2,1)S(1)} %copy.48), channel_id=1, source_target_pairs={{16,0},{32,16},{48,32},{64,48},{80,64},{96,80},{112,96},{128,112},... | collective-permute-start | bytes 1572872 | tf_op jit(solution)/shard_map/ppermute | solution.py:14
  2.8 6.4 %collective-permute-start = (bf16[16,2,2,32,128]{4,3,2,1,0:T(8,128)(2,1)S(1)}, bf16[16,2,2,32,128]{4,3,2,1,0:T(8,128)(2,1)S(1)}, u32[]{:S(2)}, u32[]{:S(2)}) collective-permute-start(bf16[16,2,2,32,128]{4,3,2,1,0:T(8,128)(2,1)S(1)} %get-tuple-element.10), channel_id=1, source_target_pairs={{0,16},{16,32},{32,48},{48,64},{64,80},{80,96},{96,112},{112,128},... | collective-permute-start | bytes 1572872 | tf_op jit(solution)/shard_map/ppermute | solution.py:13
  9.2 0.0 copy-done
  9.2 0.8 convert_element_type.26
  10.0 1.0 slice_bitcast_fusion.3
  11.1 2.4 %fusion.6 = bf16[16,8,32,128]{3,2,1,0:T(8,128)(2,1)S(1)} fusion(f32[16,8,32,128]{3,2,1,0:T(8,128)S(1)} %get-tuple-element.6, f32[16,8,32,128]{3,2,1,0:T(8,128)S(1)} %get-tuple-element.5), kind=kLoop, calls=%fused_computation.28 | loop fusion | flops 6291456 | bytes 5242880 | tf_op jit(solution)/shard_map/convert.5
  13.4 0.7 copy.39
  14.1 15.3 %collective-permute-done.1 = bf16[16,2,2,32,128]{4,3,2,0,1:T(8,128)(2,1)S(1)} collective-permute-done((bf16[16,2,2,32,128]{4,3,2,0,1:T(8,128)(2,1)S(1)}, bf16[16,2,2,32,128]{4,3,2,0,1:T(8,128)(2,1)S(1)}, u32[]{:S(2)}, u32[]{:S(2)}) %collective-permute-start.1) | collective-permute-done | bytes 524320 | tf_op jit(solution)/shard_map/ppermute | solution.py:14
  29.5 0.0 collective-permute-done
  29.5 0.9 maximum_convert_fusion
  30.3 0.8 slice_bitcast_fusion.1
  31.1 4.2 %fusion.25 = (bf16[16,8,32,128]{3,2,1,0:T(8,128)(2,1)S(1)}, bf16[16,8,32,128]{3,2,1,0:T(8,128)(2,1)S(1)}) fusion(f32[16,8,32,128]{3,2,1,0:T(8,128)S(1)} %get-tuple-element.7, f32[16,12,32,128]{3,2,1,0:T(8,128)S(1)} %get-tuple-element.8, f32[16,12,32,128]{3,2,1,0:T(8,128)S(1)} %get-tuple-element.9), kind=kLoop, calls=%fused_computation.47 | loop fusion | flops 12582912 | bytes 20971520 | tf_op jit(solution)/shard_map/convert.4
  35.3 0.7 copy.40
  36.0 0.7 copy.41
  36.7 2.0 %pad_maximum_fusion = bf16[16,3,8,2,16,128]{5,0,4,1,3,2:T(8,128)(2,1)} fusion(bf16[16,1,8,2,16,128]{5,0,4,1,3,2:T(8,128)(2,1)S(1)} %copy.41, bf16[16,1,8,2,16,128]{5,0,4,1,3,2:T(8,128)(2,1)S(1)} %copy.40, bf16[16,1,8,2,16,128]{5,0,4,1,3,2:T(8,128)(2,1)S(1)} %copy.39), kind=kLoop, calls=%fused_computation.14 | loop fusion | flops 3145728 | bytes 6291456 | tf_op jit(solution)/shard_map/stack | solution.py:49
  38.7 0.0 copy-start.2
  38.7 0.0 copy-start.1
  38.7 8.6 %all-to-all-start = ((bf16[16,16,3,16,128]{4,1,3,2,0:T(8,128)(2,1)}), bf16[16,16,3,16,128]{4,1,3,2,0:T(8,128)(2,1)S(1)}, u32[]{:S(2)}, u32[]{:S(2)}) async-start(bf16[16,16,3,16,128]{4,1,3,2,0:T(8,128)(2,1)} %bitcast.47), calls=%async_computation | async-start | bytes 6291456 | tf_op jit(solution)/shard_map/all_to_all | solution.py:56
  47.3 0.0 copy-done.2
  47.3 0.1 select_reduce_fusion
  47.4 0.0 copy-done.1
  47.4 0.1 convert_reduce_fusion
  47.5 37.9 %all-to-all-done = bf16[16,16,3,16,128]{4,1,3,2,0:T(8,128)(2,1)S(1)} async-done(((bf16[16,16,3,16,128]{4,1,3,2,0:T(8,128)(2,1)}), bf16[16,16,3,16,128]{4,1,3,2,0:T(8,128)(2,1)S(1)}, u32[]{:S(2)}, u32[]{:S(2)}) %all-to-all-start) | async-done | bytes 3145760 | tf_op jit(solution)/shard_map/all_to_all | solution.py:56
  85.5 0.9 copy.42
  86.4 0.5 convolution_divide_fusion
  86.9 2.7 %fusion.36 = f32[256,48,128]{2,0,1:T(8,128)S(1)} fusion(f32[24,48,128]{2,0,1:T(8,128)S(1)} %convolution_divide_fusion, s32[256]{0:T(256)S(1)} %copy-done.1), kind=kOutput, calls=%fused_computation.69 | convolution fusion | flops 452990976 | bytes 6882304 | tf_op jit(solution)/shard_map/sb,bkz->skz/dot_general | solution.py:66
  89.6 1.9 %fusion.34 = f32[256,256]{1,0:T(8,128)} fusion(f32[256,48,128]{2,0,1:T(8,128)S(1)} %fusion.36, bf16[256,48,128]{2,0,1:T(8,128)(2,1)S(1)} %bitcast.46), kind=kOutput, calls=%fused_computation.64 | convolution fusion | flops 810090496 | bytes 9699328 | tf_op jit(solution)/shard_map/skz,tkz->st/dot_general | solution.py:76
  91.5 4.3 %all-to-all-start.1 = ((f32[16,16,256]{2,1,0:T(8,128)}), f32[16,16,256]{2,1,0:T(8,128)S(1)}, u32[]{:S(2)}, u32[]{:S(2)}) async-start(f32[16,16,256]{2,1,0:T(8,128)} %bitcast.13), calls=%async_computation.1 | async-start | bytes 524288 | tf_op jit(solution)/shard_map/all_to_all | solution.py:36
  95.8 7.2 %all-to-all-done.1 = f32[16,16,256]{2,1,0:T(8,128)S(1)} async-done(((f32[16,16,256]{2,1,0:T(8,128)}), f32[16,16,256]{2,1,0:T(8,128)S(1)}, u32[]{:S(2)}, u32[]{:S(2)}) %all-to-all-start.1) | async-done | bytes 262176 | tf_op jit(solution)/shard_map/all_to_all | solution.py:36
  103.0 0.1 reshape.46
  103.2 0.6 gather_fusion
  103.8 0.1 fusion.43
  103.8 0.1 reshape.57
  104.0 20.5 %all_to_all.15 = f32[16,1,256]{2,1,0:T(1,128)S(1)} all-to-all(f32[16,1,256]{2,1,0:T(1,128)S(1)} %reshape.57), channel_id=1, replica_groups=mesh['space'=16,'snap'=16] {'space'}, dimensions={0} | all-to-all | bytes 32768 | tf_op jit(solution)/shard_map/all_to_all | solution.py:36
  124.5 0.5 broadcast.87
  125.0 0.7 reduce
  125.7 0.1 reshape.58
  125.8 0.7 copy.44
  (7 shorter events, 0.1 us)
Async XLA Ops:
  0.0 9.2 %copy-start = (bf16[16,3,8,32,128]{4,3,2,1,0:T(8,128)(2,1)S(1)}, bf16[16,3,8,32,128]{4,3,2,1,0:T(8,128)(2,1)}, u32[]{:S(2)}) copy-start(bf16[16,3,8,32,128]{4,3,2,1,0:T(8,128)(2,1)} %param.3) | copy-start | bytes 9437188
  1.5 28.0 %collective-permute-start.1 = (bf16[16,2,2,32,128]{4,3,2,0,1:T(8,128)(2,1)S(1)}, bf16[16,2,2,32,128]{4,3,2,0,1:T(8,128)(2,1)S(1)}, u32[]{:S(2)}, u32[]{:S(2)}) collective-permute-start(bf16[16,2,2,32,128]{4,3,2,0,1:T(8,128)(2,1)S(1)} %copy.48), channel_id=1, source_target_pairs={{16,0},{32,16},{48,32},{64,48},{80,64},{96,80},{112,96},{128,112},... | collective-permute-start | bytes 1572872 | tf_op jit(solution)/shard_map/ppermute | solution.py:14
  2.8 26.7 %collective-permute-start = (bf16[16,2,2,32,128]{4,3,2,1,0:T(8,128)(2,1)S(1)}, bf16[16,2,2,32,128]{4,3,2,1,0:T(8,128)(2,1)S(1)}, u32[]{:S(2)}, u32[]{:S(2)}) collective-permute-start(bf16[16,2,2,32,128]{4,3,2,1,0:T(8,128)(2,1)S(1)} %get-tuple-element.10), channel_id=1, source_target_pairs={{0,16},{16,32},{32,48},{48,64},{64,80},{80,96},{96,112},{112,128},... | collective-permute-start | bytes 1572872 | tf_op jit(solution)/shard_map/ppermute | solution.py:13
  38.7 8.6 %copy-start.2 = (s32[16]{0:T(128)S(1)}, s32[16]{0:T(128)}, u32[]{:S(2)}) copy-start(s32[16]{0:T(128)} %param.5) | copy-start | bytes 196
  38.7 8.7 %copy-start.1 = (s32[256]{0:T(256)S(1)}, s32[256]{0:T(256)}, u32[]{:S(2)}) copy-start(s32[256]{0:T(256)} %param.4) | copy-start | bytes 3076
  38.7 46.8 %all-to-all-start = ((bf16[16,16,3,16,128]{4,1,3,2,0:T(8,128)(2,1)}), bf16[16,16,3,16,128]{4,1,3,2,0:T(8,128)(2,1)S(1)}, u32[]{:S(2)}, u32[]{:S(2)}) async-start(bf16[16,16,3,16,128]{4,1,3,2,0:T(8,128)(2,1)} %bitcast.47), calls=%async_computation | async-start | bytes 6291456 | tf_op jit(solution)/shard_map/all_to_all | solution.py:56
  91.5 11.5 %all-to-all-start.1 = ((f32[16,16,256]{2,1,0:T(8,128)}), f32[16,16,256]{2,1,0:T(8,128)S(1)}, u32[]{:S(2)}, u32[]{:S(2)}) async-start(f32[16,16,256]{2,1,0:T(8,128)} %bitcast.13), calls=%async_computation.1 | async-start | bytes 524288 | tf_op jit(solution)/shard_map/all_to_all | solution.py:36

commit v2 on v1

--- a/solution.py
+++ b/solution.py
@@ -37,28 +37,21 @@
     return jnp.sum(got, axis=0)
 
 
-def per_device(velocity, phase_bins, tile_owner):
-    snaps_dev, _, cells_x, cells_y, cells_z = velocity.shape
-    vw_wide = x_halo(velocity[:, 1:3], 2).astype(jnp.float32)
-    frame = velocity.astype(jnp.float32)
-    u, v, w = frame[:, 0], frame[:, 1], frame[:, 2]
-    v_wide, w_wide = vw_wide[:, 0], vw_wide[:, 1]
-    omega_x = d_padded(w, 2) - d_padded(v, 3)
-    omega_y = d_padded(u, 3) - d_wide(w_wide, 1)
-    omega_z = d_wide(v_wide, 1) - d_padded(u, 2)
-    vortex = jnp.stack([omega_x, omega_y, omega_z], axis=1).astype(jnp.bfloat16)
-
-    n_snap = lax.axis_size("snap")
+def to_parts(field, n_snap):
+    snaps_dev, cells_x, cells_y, cells_z = field.shape
     halves = n_snap // cells_x
     rows = cells_y // halves
-    parts = vortex.reshape(snaps_dev, 3, cells_x, halves, rows, cells_z)
-    parts = jnp.transpose(parts, (2, 3, 0, 1, 4, 5)).reshape(n_snap, snaps_dev, 3, rows, cells_z)
+    parts = field.reshape(snaps_dev, cells_x, halves, rows, cells_z)
+    return jnp.transpose(parts, (1, 2, 0, 3, 4)).reshape(n_snap, snaps_dev, rows, cells_z)
+
+
+def exchange(parts):
     arranged = lax.all_to_all(parts, "snap", split_axis=0, concat_axis=0, tiled=True)
-    total_snaps = n_snap * snaps_dev
-    columns = arranged.reshape(total_snaps, 3 * rows, cells_z)
+    count, snaps_dev, comps, rows, cells_z = arranged.shape
+    return arranged.reshape(count * snaps_dev, comps * rows, cells_z)
 
-    onehot = (phase_bins[None, :] == jnp.arange(NB, dtype=jnp.int32)[:, None])
-    bin_counts = jnp.sum(onehot.astype(jnp.float32), axis=1)
+
+def fluctuation_of(columns, onehot, bin_counts):
     bin_sums = jnp.einsum(
         "bs,skz->bkz", onehot.astype(jnp.bfloat16), columns, preferred_element_type=jnp.float32
     )
@@ -70,12 +63,37 @@
         precision=lax.Precision.HIGHEST,
         preferred_element_type=jnp.float32,
     )
-    fluctuation = (columns.astype(jnp.float32) - selected).astype(jnp.bfloat16)
+    fluct = (columns.astype(jnp.float32) - selected).astype(jnp.bfloat16)
+    return jnp.einsum("skz,tkz->st", fluct, fluct, preferred_element_type=jnp.float32)
+
+
+def per_device(velocity, phase_bins, tile_owner):
+    snaps_dev, _, cells_x, cells_y, cells_z = velocity.shape
+    n_snap = lax.axis_size("snap")
+    vw_wide = x_halo(velocity[:, 1:3], 2)
+    frame = velocity.astype(jnp.float32)
+    u, v, w = frame[:, 0], frame[:, 1], frame[:, 2]
+
+    omega_x = (d_padded(w, 2) - d_padded(v, 3)).astype(jnp.bfloat16)
+    cols_x = exchange(to_parts(omega_x, n_snap)[:, :, None])
+
+    vw_wide = vw_wide.astype(jnp.float32)
+    v_wide, w_wide = vw_wide[:, 0], vw_wide[:, 1]
+    omega_y = d_padded(u, 3) - d_wide(w_wide, 1)
+    omega_z = d_wide(v_wide, 1) - d_padded(u, 2)
+    omega_yz = jnp.stack(
+        [to_parts(omega_y.astype(jnp.bfloat16), n_snap), to_parts(omega_z.astype(jnp.bfloat16), n_snap)],
+        axis=2,
+    )
+    cols_yz = exchange(omega_yz)
+    total_snaps = cols_x.shape[0]
+
+    onehot = (phase_bins[None, :] == jnp.arange(NB, dtype=jnp.int32)[:, None])
+    bin_counts = jnp.sum(onehot.astype(jnp.float32), axis=1)
     voxel_total = lax.axis_size("space") * cells_x * cells_y * cells_z
     partial_gram = (
-        jnp.einsum("skz,tkz->st", fluctuation, fluctuation, preferred_element_type=jnp.float32)
-        / voxel_total
-    )
+        fluctuation_of(cols_x, onehot, bin_counts) + fluctuation_of(cols_yz, onehot, bin_counts)
+    ) / voxel_total
 
     row_blocks = partial_gram.reshape(n_snap, total_snaps // n_snap, total_snaps)
     col_sum = all_to_all_sum(row_blocks, "snap")

time: 127 us -> 119 us (0.937)
  waiting for transfers between devices: 60.5 us -> 42.4 us
  local copies, waits for them, and re-layouts: 8.3 us -> 14.2 us
  starting transfers between devices: 20.5 us -> 26.4 us
  blocking collectives: 20.5 us -> 17.4 us
    ppermute x1, waiting for transfers between devices: 15.3 us -> 5.84 us  [x_halo(): high = lax.ppermute(block[:, :, :width], 'space', backward)]
    all_to_all x1 -> x2, waiting for transfers between devices: 37.9 us -> 29.4 us  [exchange(): lax.all_to_all(parts, 'snap', split_axis=0, concat_axis=0, tiled=True)]
    convert_element_type x1 -> x3, other arithmetic: 0.86 us -> 8.48 us  [the longest x1 4.2 us: per_device(): omega_y.astype(jnp.bfloat16)]
    another operation x3 -> x1, other arithmetic: 8.58 us -> 1.53 us  [per_device(): jnp.stack([to_parts(omega_y.astype(jnp.bfloat16), n_snap), to_parts(omega...]
    all_to_all x1 -> x2, starting transfers between devices: 8.59 us -> 13.7 us  [exchange(): lax.all_to_all(parts, 'snap', split_axis=0, concat_axis=0, tiled=True)]
    all_to_all x1, blocking collectives: 20.5 us -> 17.4 us  [all_to_all_sum(): got = lax.all_to_all(x, axis, split_axis=0, concat_axis=0, tiled=True)]
    reshape x0 -> x3, local copies, waits for them, and re-layouts: none -> 3.02 us  [to_parts(): parts = field.reshape(snaps_dev, cells_x, halves, rows, cells_z)]
    another operation x3 -> x0, local copies, waits for them, and re-layouts: 2.04 us -> none  [per_device(): vortex = jnp.stack([omega_x, omega_y, omega_z], axis=1).astype(jnp.bfloat16)]
  transfers between devices with their start and end apart: 4 -> 5, of which waited for: 3 -> 4; matrix products, arithmetic and copies ran while one was open for 4% -> 17% of each run, Pallas kernels for 0% -> 0%
where the time goes in v2:
time: 119 us; the launch traced here: 118 us
  waiting for transfers between devices  42.4 us (36%)
  starting transfers between devices  26.4 us (22%)
  blocking collectives  17.4 us (15%)
  local copies, waits for them, and re-layouts  14.2 us (12%)
  other arithmetic  11.9 us (10%)
  matrix products  5.74 us (5%)
    all_to_all x2, waiting for transfers between devices, exchange(): lax.all_to_all(parts, 'snap', split_axis=0, concat_axis=0, tiled=True)  29.4 us
    all_to_all x1, blocking collectives, all_to_all_sum(): got = lax.all_to_all(x, axis, split_axis=0, concat_axis=0, tiled=True)  17.4 us
    all_to_all x2, starting transfers between devices, exchange(): lax.all_to_all(parts, 'snap', split_axis=0, concat_axis=0, tiled=True)  13.7 us
    all_to_all x1, waiting for transfers between devices, all_to_all_sum(): got = lax.all_to_all(x, axis, split_axis=0, concat_axis=0, tiled=True)  7.22 us
    ppermute x1, starting transfers between devices, x_halo(): low = lax.ppermute(block[:, :, block.shape[2] - width:], 'space', forward)  7.16 us
    ppermute x1, waiting for transfers between devices, x_halo(): high = lax.ppermute(block[:, :, :width], 'space', backward)  5.84 us
    all_to_all x1, starting transfers between devices, all_to_all_sum(): got = lax.all_to_all(x, axis, split_axis=0, concat_axis=0, tiled=True)  4.29 us
    convert_element_type x1, other arithmetic, per_device(): omega_y.astype(jnp.bfloat16)  4.2 us
  transfers between devices with their start and end apart: 5, of which 4 were waited for; matrix products, arithmetic and copies ran while one was open for 17% of the time, Pallas kernels for 0%

profile of v2, /device:TPU:1, one launch (start us, length us, event | category | flops | bytes accessed | tf_op | source)
XLA Modules:
  0.0 118.3 jit_solution(13211669222600232699)
XLA Ops:
  0.0 0.0 copy-start
  0.0 2.2 %fusion.44 = (bf16[16,2,2,32,128]{4,3,2,1,0:T(8,128)(2,1)}, bf16[16,2,2,32,128]{4,3,2,1,0:T(8,128)(2,1)S(1)}) fusion(bf16[16,3,8,32,128]{4,3,2,1,0:T(8,128)(2,1)} %param.3), kind=kLoop, calls=%fused_computation.83 | loop fusion | bytes 2097152 | tf_op jit(solution)/shard_map/slice | solution.py:13
  2.2 0.8 copy.56
  3.1 1.3 %collective-permute-start.1 = (bf16[16,2,2,32,128]{4,3,2,0,1:T(8,128)(2,1)}, bf16[16,2,2,32,128]{4,3,2,0,1:T(8,128)(2,1)}, u32[]{:S(2)}, u32[]{:S(2)}) collective-permute-start(bf16[16,2,2,32,128]{4,3,2,0,1:T(8,128)(2,1)} %copy.56), channel_id=1, source_target_pairs={{16,0},{32,16},{48,32},{64,48},{80,64},{96,80},{112,96},{128,112},... | collective-permute-start | bytes 1572872 | tf_op jit(solution)/shard_map/ppermute | solution.py:14
  4.4 7.2 %collective-permute-start = (bf16[16,2,2,32,128]{4,3,2,1,0:T(8,128)(2,1)}, bf16[16,2,2,32,128]{4,3,2,1,0:T(8,128)(2,1)}, u32[]{:S(2)}, u32[]{:S(2)}) collective-permute-start(bf16[16,2,2,32,128]{4,3,2,1,0:T(8,128)(2,1)} %get-tuple-element.10), channel_id=1, source_target_pairs={{0,16},{16,32},{32,48},{48,64},{64,80},{80,96},{96,112},{112,128},... | collective-permute-start | bytes 1572872 | tf_op jit(solution)/shard_map/ppermute | solution.py:13
  11.5 0.0 copy-done
  11.5 0.8 convert_element_type.41
  12.4 2.4 %slice_bitcast_fusion.3 = (f32[16,8,32,128]{3,2,1,0:T(8,128)S(1)}, f32[16,8,32,128]{3,2,1,0:T(8,128)S(1)}, f32[16,8,32,128]{3,2,1,0:T(8,128)}) fusion(f32[16,3,8,32,128]{4,3,2,1,0:T(8,128)S(1)} %convert_element_type.41), kind=kLoop, calls=%fused_computation.58 | loop fusion | bytes 12582912 | tf_op jit(solution)/shard_map/squeeze | solution.py:75
  14.8 2.3 %fusion.5 = bf16[16,8,32,128]{3,2,1,0:T(8,128)(2,1)S(1)} fusion(f32[16,8,32,128]{3,2,1,0:T(8,128)S(1)} %get-tuple-element.6, f32[16,8,32,128]{3,2,1,0:T(8,128)S(1)} %get-tuple-element.5), kind=kLoop, calls=%fused_computation.26 | loop fusion | flops 6291456 | bytes 5242880 | tf_op jit(solution)/shard_map/convert_element_type | solution.py:77
  17.1 1.7 %copy.43 = bf16[16,8,2,16,128]{4,0,3,2,1:T(8,128)(2,1)} copy(bf16[16,8,2,16,128]{4,3,2,1,0:T(8,128)(2,1)S(1)} %bitcast.70) | data formatting | bytes 2097152 | tf_op jit(solution)/shard_map/reshape | solution.py:44
  18.8 6.8 %all-to-all-start = ((bf16[16,16,1,16,128]{4,1,3,2,0:T(8,128)(2,1)}), bf16[16,16,1,16,128]{4,1,3,2,0:T(8,128)(2,1)}, u32[]{:S(2)}, u32[]{:S(2)}) async-start(bf16[16,16,1,16,128]{4,1,3,2,0:T(8,128)(2,1)} %bitcast.71), calls=%async_computation | async-start | bytes 2097152 | tf_op jit(solution)/shard_map/all_to_all | solution.py:49
  25.6 5.8 %collective-permute-done.1 = bf16[16,2,2,32,128]{4,3,2,0,1:T(8,128)(2,1)} collective-permute-done((bf16[16,2,2,32,128]{4,3,2,0,1:T(8,128)(2,1)}, bf16[16,2,2,32,128]{4,3,2,0,1:T(8,128)(2,1)}, u32[]{:S(2)}, u32[]{:S(2)}) %collective-permute-start.1) | collective-permute-done | bytes 524320 | tf_op jit(solution)/shard_map/ppermute | solution.py:14
  31.4 0.0 collective-permute-done
  31.4 1.9 %maximum_convert_fusion = f32[16,2,12,32,128]{4,3,2,0,1:T(8,128)S(1)} fusion(bf16[16,2,2,32,128]{4,3,2,0,1:T(8,128)(2,1)} %collective-permute-done.1, bf16[16,2,2,32,128]{4,3,2,1,0:T(8,128)(2,1)} %collective-permute-done, bf16[16,3,8,32,128]{4,3,2,1,0:T(8,128)(2,1)S(1)} %copy-done), kind=kLoop, calls=%fused_computation.12 | loop fusion | flops 9437184 | bytes 9437184 | tf_op jit(solution)/shard_map/convert_element_type | solution.py:80
  33.4 0.0 copy-start.1
  33.4 0.8 slice_bitcast_fusion.1
  34.2 0.8 copy-done.1
  34.9 4.2 %fusion.24 = (bf16[16,8,32,128]{3,2,1,0:T(8,128)(2,1)S(1)}, bf16[16,8,32,128]{3,2,1,0:T(8,128)(2,1)S(1)}) fusion(f32[16,8,32,128]{3,2,1,0:T(8,128)S(1)} %copy-done.1, f32[16,12,32,128]{3,2,1,0:T(8,128)S(1)} %get-tuple-element.8, f32[16,12,32,128]{3,2,1,0:T(8,128)S(1)} %get-tuple-element.9), kind=kLoop, calls=%fused_computation.45 | loop fusion | flops 12582912 | bytes 20971520 | tf_op jit(solution)/shard_map/convert_element_type | solution.py:85
  39.2 0.7 copy.48
  39.8 0.7 copy.49
  40.5 1.5 %pad_maximum_fusion = bf16[16,16,2,16,128]{4,1,3,2,0:T(8,128)(2,1)} fusion(bf16[16,16,1,16,128]{4,1,3,2,0:T(8,128)(2,1)S(1)} %bitcast.73, bf16[16,16,1,16,128]{4,1,3,2,0:T(8,128)(2,1)S(1)} %bitcast.72), kind=kLoop, calls=%fused_computation.60 | loop fusion | flops 1048576 | bytes 4194304 | tf_op jit(solution)/shard_map/stack | solution.py:84
  42.1 0.0 copy-start.3
  42.1 0.0 copy-start.2
  42.1 5.5 %all-to-all-done = bf16[16,16,1,16,128]{4,1,3,2,0:T(8,128)(2,1)} async-done(((bf16[16,16,1,16,128]{4,1,3,2,0:T(8,128)(2,1)}), bf16[16,16,1,16,128]{4,1,3,2,0:T(8,128)(2,1)}, u32[]{:S(2)}, u32[]{:S(2)}) %all-to-all-start) | async-done | bytes 1048608 | tf_op jit(solution)/shard_map/all_to_all | solution.py:49
  47.6 6.9 %all-to-all-start.1 = ((bf16[16,16,2,16,128]{4,1,3,2,0:T(8,128)(2,1)}), bf16[16,16,2,16,128]{4,1,3,2,0:T(8,128)(2,1)S(1)}, u32[]{:S(2)}, u32[]{:S(2)}) async-start(bf16[16,16,2,16,128]{4,1,3,2,0:T(8,128)(2,1)} %pad_maximum_fusion), calls=%async_computation.1 | async-start | bytes 4194304 | tf_op jit(solution)/shard_map/all_to_all | solution.py:49
  54.5 0.0 copy-done.3
  54.5 0.1 select_reduce_fusion
  54.6 0.0 copy-done.2
  54.7 0.1 convert_reduce_fusion
  54.8 1.5 %copy.44 = bf16[16,16,1,16,128]{4,1,0,3,2:T(8,128)(2,1)S(1)} copy(bf16[16,16,1,16,128]{4,1,3,2,0:T(8,128)(2,1)} %all-to-all-done) | data formatting | bytes 2097152 | tf_op jit(solution)/shard_map/all_to_all | solution.py:49
  56.3 0.2 convolution_divide_fusion.1
  56.5 1.1 subtract_convert_fusion.1
  57.6 23.8 %all-to-all-done.1 = bf16[16,16,2,16,128]{4,1,3,2,0:T(8,128)(2,1)S(1)} async-done(((bf16[16,16,2,16,128]{4,1,3,2,0:T(8,128)(2,1)}), bf16[16,16,2,16,128]{4,1,3,2,0:T(8,128)(2,1)S(1)}, u32[]{:S(2)}, u32[]{:S(2)}) %all-to-all-start.1) | async-done | bytes 2097184 | tf_op jit(solution)/shard_map/all_to_all | solution.py:49
  81.5 0.6 copy.50
  82.0 0.4 convolution_divide_fusion
  82.4 2.1 %subtract_convert_fusion = bf16[256,32,128]{2,0,1:T(8,128)(2,1)S(1)} fusion(bf16[256,32,128]{2,0,1:T(8,128)(2,1)S(1)} %bitcast.65, f32[24,32,128]{2,0,1:T(8,128)S(1)} %convolution_divide_fusion, s32[256]{0:T(256)S(1)} %copy-done.2), kind=kOutput, calls=%fused_computation.9 | convolution fusion | flops 305141760 | bytes 4588544 | tf_op jit(solution)/shard_map/sb,bkz->skz/dot_general | solution.py:59
  84.5 0.7 convolution_bitcast_fusion
  85.3 1.2 fusion.33
  86.4 4.3 %all-to-all-start.2 = ((f32[16,16,256]{2,1,0:T(8,128)}), f32[16,16,256]{2,1,0:T(8,128)S(1)}, u32[]{:S(2)}, u32[]{:S(2)}) async-start(f32[16,16,256]{2,1,0:T(8,128)} %bitcast.19), calls=%async_computation.2 | async-start | bytes 524288 | tf_op jit(solution)/shard_map/all_to_all | solution.py:36
  90.8 7.2 %all-to-all-done.2 = f32[16,16,256]{2,1,0:T(8,128)S(1)} async-done(((f32[16,16,256]{2,1,0:T(8,128)}), f32[16,16,256]{2,1,0:T(8,128)S(1)}, u32[]{:S(2)}, u32[]{:S(2)}) %all-to-all-start.2) | async-done | bytes 262176 | tf_op jit(solution)/shard_map/all_to_all | solution.py:36
  98.0 0.1 reshape.48
  98.2 0.6 gather_fusion
  98.7 0.1 fusion.45
  98.8 0.1 reshape.60
  98.9 17.4 %all_to_all.20 = f32[16,1,256]{2,1,0:T(1,128)S(1)} all-to-all(f32[16,1,256]{2,1,0:T(1,128)S(1)} %reshape.60), channel_id=1, replica_groups=mesh['space'=16,'snap'=16] {'space'}, dimensions={0} | all-to-all | bytes 32768 | tf_op jit(solution)/shard_map/all_to_all | solution.py:36
  116.3 0.5 broadcast.87
  116.9 0.7 reduce
  117.5 0.1 reshape.61
  117.7 0.7 copy.52
  (6 shorter events, 0.1 us)
Async XLA Ops:
  0.0 11.5 %copy-start = (bf16[16,3,8,32,128]{4,3,2,1,0:T(8,128)(2,1)S(1)}, bf16[16,3,8,32,128]{4,3,2,1,0:T(8,128)(2,1)}, u32[]{:S(2)}) copy-start(bf16[16,3,8,32,128]{4,3,2,1,0:T(8,128)(2,1)} %param.3) | copy-start | bytes 9437188
  3.1 28.3 %collective-permute-start.1 = (bf16[16,2,2,32,128]{4,3,2,0,1:T(8,128)(2,1)}, bf16[16,2,2,32,128]{4,3,2,0,1:T(8,128)(2,1)}, u32[]{:S(2)}, u32[]{:S(2)}) collective-permute-start(bf16[16,2,2,32,128]{4,3,2,0,1:T(8,128)(2,1)} %copy.56), channel_id=1, source_target_pairs={{16,0},{32,16},{48,32},{64,48},{80,64},{96,80},{112,96},{128,112},... | collective-permute-start | bytes 1572872 | tf_op jit(solution)/shard_map/ppermute | solution.py:14
  4.4 27.0 %collective-permute-start = (bf16[16,2,2,32,128]{4,3,2,1,0:T(8,128)(2,1)}, bf16[16,2,2,32,128]{4,3,2,1,0:T(8,128)(2,1)}, u32[]{:S(2)}, u32[]{:S(2)}) collective-permute-start(bf16[16,2,2,32,128]{4,3,2,1,0:T(8,128)(2,1)} %get-tuple-element.10), channel_id=1, source_target_pairs={{0,16},{16,32},{32,48},{48,64},{64,80},{80,96},{96,112},{112,128},... | collective-permute-start | bytes 1572872 | tf_op jit(solution)/shard_map/ppermute | solution.py:13
  18.8 28.8 %all-to-all-start = ((bf16[16,16,1,16,128]{4,1,3,2,0:T(8,128)(2,1)}), bf16[16,16,1,16,128]{4,1,3,2,0:T(8,128)(2,1)}, u32[]{:S(2)}, u32[]{:S(2)}) async-start(bf16[16,16,1,16,128]{4,1,3,2,0:T(8,128)(2,1)} %bitcast.71), calls=%async_computation | async-start | bytes 2097152 | tf_op jit(solution)/shard_map/all_to_all | solution.py:49
  33.4 1.6 %copy-start.1 = (f32[16,8,32,128]{3,2,1,0:T(8,128)S(1)}, f32[16,8,32,128]{3,2,1,0:T(8,128)}, u32[]{:S(2)}) copy-start(f32[16,8,32,128]{3,2,1,0:T(8,128)} %get-tuple-element.7) | copy-start | bytes 6291460
  42.1 12.5 %copy-start.3 = (s32[16]{0:T(128)S(1)}, s32[16]{0:T(128)}, u32[]{:S(2)}) copy-start(s32[16]{0:T(128)} %param.5) | copy-start | bytes 196
  42.1 12.6 %copy-start.2 = (s32[256]{0:T(256)S(1)}, s32[256]{0:T(256)}, u32[]{:S(2)}) copy-start(s32[256]{0:T(256)} %param.4) | copy-start | bytes 3076
  47.6 33.9 %all-to-all-start.1 = ((bf16[16,16,2,16,128]{4,1,3,2,0:T(8,128)(2,1)}), bf16[16,16,2,16,128]{4,1,3,2,0:T(8,128)(2,1)S(1)}, u32[]{:S(2)}, u32[]{:S(2)}) async-start(bf16[16,16,2,16,128]{4,1,3,2,0:T(8,128)(2,1)} %pad_maximum_fusion), calls=%async_computation.1 | async-start | bytes 4194304 | tf_op jit(solution)/shard_map/all_to_all | solution.py:49
  86.4 11.5 %all-to-all-start.2 = ((f32[16,16,256]{2,1,0:T(8,128)}), f32[16,16,256]{2,1,0:T(8,128)S(1)}, u32[]{:S(2)}, u32[]{:S(2)}) async-start(f32[16,16,256]{2,1,0:T(8,128)} %bitcast.19), calls=%async_computation.2 | async-start | bytes 524288 | tf_op jit(solution)/shard_map/all_to_all | solution.py:36

commit v3 on v2

--- a/solution.py
+++ b/solution.py
@@ -2,6 +2,7 @@
 import jax.numpy as jnp
 from jax import lax
 from jax.sharding import PartitionSpec as P
+
 
 NB = 24
 
@@ -27,22 +28,15 @@
     return stencil(lambda o: lax.slice_in_dim(padded, o, o + length, axis=axis))
 
 
-def d_wide(wide, axis):
-    length = wide.shape[axis] - 4
-    return stencil(lambda o: lax.slice_in_dim(wide, o, o + length, axis=axis))
-
-
 def all_to_all_sum(x, axis):
     got = lax.all_to_all(x, axis, split_axis=0, concat_axis=0, tiled=True)
     return jnp.sum(got, axis=0)
 
 
-def to_parts(field, n_snap):
-    snaps_dev, cells_x, cells_y, cells_z = field.shape
-    halves = n_snap // cells_x
-    rows = cells_y // halves
-    parts = field.reshape(snaps_dev, cells_x, halves, rows, cells_z)
-    return jnp.transpose(parts, (1, 2, 0, 3, 4)).reshape(n_snap, snaps_dev, rows, cells_z)
+def pieces(field, count):
+    snaps_dev, cells_z = field.shape[0], field.shape[-1]
+    blocks = field.reshape(snaps_dev, count, -1, cells_z)
+    return jnp.transpose(blocks, (1, 0, 2, 3))
 
 
 def exchange(parts):
@@ -67,32 +61,43 @@
     return jnp.einsum("skz,tkz->st", fluct, fluct, preferred_element_type=jnp.float32)
 
 
-def per_device(velocity, phase_bins, tile_owner):
-    snaps_dev, _, cells_x, cells_y, cells_z = velocity.shape
+def d_x(field, planes):
+    return stencil(lambda o: field[:, planes[0] + o - 2 : planes[-1] + o - 1])
+
+
+def body(velocity, phase_bins, tile_owner):
+    _, _, cells_x, cells_y, cells_z = velocity.shape
     n_snap = lax.axis_size("snap")
-    vw_wide = x_halo(velocity[:, 1:3], 2)
     frame = velocity.astype(jnp.float32)
     u, v, w = frame[:, 0], frame[:, 1], frame[:, 2]
+    inner = list(range(2, cells_x - 2))
 
     omega_x = (d_padded(w, 2) - d_padded(v, 3)).astype(jnp.bfloat16)
-    cols_x = exchange(to_parts(omega_x, n_snap)[:, :, None])
+    u_in = u[:, inner[0] : inner[-1] + 1]
+    omega_y_in = (d_padded(u_in, 3) - d_x(w, inner)).astype(jnp.bfloat16)
+    omega_z_in = (d_x(v, inner) - d_padded(u_in, 2)).astype(jnp.bfloat16)
+    early = jnp.stack(
+        [pieces(omega_x, n_snap), pieces(jnp.stack([omega_y_in, omega_z_in], axis=1), n_snap)], axis=2
+    )
+    cols_a = exchange(early)
 
+    vw_wide = x_halo(velocity[:, 1:3], 2)
     vw_wide = vw_wide.astype(jnp.float32)
     v_wide, w_wide = vw_wide[:, 0], vw_wide[:, 1]
-    omega_y = d_padded(u, 3) - d_wide(w_wide, 1)
-    omega_z = d_wide(v_wide, 1) - d_padded(u, 2)
-    omega_yz = jnp.stack(
-        [to_parts(omega_y.astype(jnp.bfloat16), n_snap), to_parts(omega_z.astype(jnp.bfloat16), n_snap)],
-        axis=2,
-    )
-    cols_yz = exchange(omega_yz)
-    total_snaps = cols_x.shape[0]
+    u_edge = jnp.concatenate([u[:, :2], u[:, cells_x - 2 :]], axis=1)
+    dxw = jnp.concatenate([d_x(w_wide, [2, 3]), d_x(w_wide, [cells_x, cells_x + 1])], axis=1)
+    dxv = jnp.concatenate([d_x(v_wide, [2, 3]), d_x(v_wide, [cells_x, cells_x + 1])], axis=1)
+    omega_y_edge = (d_padded(u_edge, 3) - dxw).astype(jnp.bfloat16)
+    omega_z_edge = (dxv - d_padded(u_edge, 2)).astype(jnp.bfloat16)
+    late = pieces(jnp.stack([omega_y_edge, omega_z_edge], axis=1), n_snap)[:, :, None]
+    cols_b = exchange(late)
+    total_snaps = cols_a.shape[0]
 
     onehot = (phase_bins[None, :] == jnp.arange(NB, dtype=jnp.int32)[:, None])
     bin_counts = jnp.sum(onehot.astype(jnp.float32), axis=1)
     voxel_total = lax.axis_size("space") * cells_x * cells_y * cells_z
     partial_gram = (
-        fluctuation_of(cols_x, onehot, bin_counts) + fluctuation_of(cols_yz, onehot, bin_counts)
+        fluctuation_of(cols_a, onehot, bin_counts) + fluctuation_of(cols_b, onehot, bin_counts)
     ) / voxel_total
 
     row_blocks = partial_gram.reshape(n_snap, total_snaps // n_snap, total_snaps)
@@ -110,7 +115,7 @@
 
 def solution(mesh):
     return jax.shard_map(
-        per_device,
+        body,
         mesh=mesh,
         in_specs=(P("snap", None, "space", None, None), P(), P()),
         out_specs=P("space", None, "snap"),

time: 119 us -> 131 us (1.10)
  waiting for transfers between devices: 42.4 us -> 62.8 us
  starting transfers between devices: 26.4 us -> 21.2 us
  other arithmetic: 11.9 us -> 10.4 us
  blocking collectives: 17.4 us -> 16 us
    ppermute x1, waiting for transfers between devices: 5.84 us -> 15.2 us  [x_halo(): high = lax.ppermute(block[:, :, :width], 'space', backward)]
    ppermute x1, waiting for transfers between devices: 0.01 us -> 8.38 us  [x_halo(): low = lax.ppermute(block[:, :, block.shape[2] - width:], 'space', forward)]
    convert_element_type x4 -> x3, other arithmetic: 9.31 us -> 4.1 us  [the longest x1 2.38 us: body(): omega_x = (d_padded(w, 2) - d_padded(v, 3)).astype(jnp.bfloat16)]
    all_to_all x2, starting transfers between devices: 13.7 us -> 9.91 us  [exchange(): lax.all_to_all(parts, 'snap', split_axis=0, concat_axis=0, tiled=True)]
    reshape x5 -> x2, local copies, waits for them, and re-layouts: 3.15 us -> 0.14 us  [body(): col_sum.reshape(col_sum.shape[0], tile_count, total_snaps // tile_count)]
    another operation x1 -> x5, other arithmetic: 1.53 us -> 4.12 us  [the longest x2 2.2 us: body(): jnp.stack([omega_y_in, omega_z_in], axis=1)]
    all_to_all x2, waiting for transfers between devices: 29.4 us -> 31.9 us  [exchange(): lax.all_to_all(parts, 'snap', split_axis=0, concat_axis=0, tiled=True)]
    another operation x0 -> x2, local copies, waits for them, and re-layouts: none -> 2.03 us  [the longest x1 1.93 us: body(): jnp.stack([pieces(omega_x, n_snap), pieces(jnp.stack([omega_y_in, omega_z...]
  transfers between devices with their start and end apart: 5 -> 5, of which waited for: 4 -> 5; matrix products, arithmetic and copies ran while one was open for 17% -> 10% of each run, Pallas kernels for 0% -> 0%
where the time goes in v3:
time: 131 us
  waiting for transfers between devices  62.8 us (48%)
  starting transfers between devices  21.2 us (16%)
  blocking collectives  16 us (12%)
  local copies, waits for them, and re-layouts  13.7 us (10%)
  other arithmetic  10.4 us (8%)
  matrix products  6.49 us (5%)
    all_to_all x2, waiting for transfers between devices, exchange(): lax.all_to_all(parts, 'snap', split_axis=0, concat_axis=0, tiled=True)  31.9 us
    all_to_all x1, blocking collectives, all_to_all_sum(): got = lax.all_to_all(x, axis, split_axis=0, concat_axis=0, tiled=True)  16 us
    ppermute x1, waiting for transfers between devices, x_halo(): high = lax.ppermute(block[:, :, :width], 'space', backward)  15.2 us
    all_to_all x2, starting transfers between devices, exchange(): lax.all_to_all(parts, 'snap', split_axis=0, concat_axis=0, tiled=True)  9.91 us
    ppermute x1, waiting for transfers between devices, x_halo(): low = lax.ppermute(block[:, :, block.shape[2] - width:], 'space', forward)  8.38 us
    all_to_all x1, waiting for transfers between devices, all_to_all_sum(): got = lax.all_to_all(x, axis, split_axis=0, concat_axis=0, tiled=True)  7.22 us
    ppermute x1, starting transfers between devices, x_halo(): low = lax.ppermute(block[:, :, block.shape[2] - width:], 'space', forward)  5.75 us
    all_to_all x1, starting transfers between devices, all_to_all_sum(): got = lax.all_to_all(x, axis, split_axis=0, concat_axis=0, tiled=True)  4.29 us
  transfers between devices with their start and end apart: 5, of which 5 were waited for; matrix products, arithmetic and copies ran while one was open for 10% of the time, Pallas kernels for 0%

profile of v3, /device:TPU:1, one launch (start us, length us, event | category | flops | bytes accessed | tf_op | source)
XLA Modules:
  0.0 130.9 jit_solution(8245419653087159052)
XLA Ops:
  0.0 0.0 copy-start.1
  0.0 1.4 %fusion.80 = (bf16[16,2,2,32,128]{4,3,2,1,0:T(8,128)(2,1)S(1)}, bf16[16,2,2,32,128]{4,3,2,1,0:T(8,128)(2,1)S(1)}) fusion(bf16[16,3,8,32,128]{4,3,2,1,0:T(8,128)(2,1)} %param.3), kind=kLoop, calls=%fused_computation.136 | loop fusion | bytes 2097152 | tf_op jit(solution)/shard_map/slice | solution.py:14
  1.5 5.7 %collective-permute-start = (bf16[16,2,2,32,128]{4,3,2,0,1:T(8,128)(2,1)S(1)}, bf16[16,2,2,32,128]{4,3,2,0,1:T(8,128)(2,1)S(1)}, u32[]{:S(2)}, u32[]{:S(2)}) collective-permute-start(bf16[16,2,2,32,128]{4,3,2,0,1:T(8,128)(2,1)S(1)} %copy.70), channel_id=1, source_target_pairs={{0,16},{16,32},{32,48},{48,64},{64,80},{80,96},{96,112},{112,128},... | collective-permute-start | bytes 1572872 | tf_op jit(solution)/shard_map/ppermute | solution.py:14
  7.3 1.3 collective-permute-start.1
  8.6 0.0 copy-done.1
  8.6 0.8 copy_convert_fusion
  9.4 2.2 %slice_bitcast_fusion.4 = (f32[16,8,32,128]{3,2,1,0:T(8,128)S(1)}, f32[16,8,32,128]{3,2,1,0:T(8,128)S(1)}, f32[16,8,32,128]{3,2,1,0:T(8,128)}) fusion(f32[16,3,8,32,128]{4,3,2,0,1:T(8,128)S(1)} %copy_convert_fusion), kind=kLoop, calls=%fused_computation.35 | loop fusion | bytes 12582912 | tf_op jit(solution)/shard_map/squeeze | solution.py:72
  11.6 0.0 copy-start.2
  11.6 0.1 fusion.81
  11.7 0.1 pad_maximum_fusion.2
  11.8 1.1 copy-done.2
  12.9 8.4 %collective-permute-done = bf16[16,2,2,32,128]{4,3,2,0,1:T(8,128)(2,1)S(1)} collective-permute-done((bf16[16,2,2,32,128]{4,3,2,0,1:T(8,128)(2,1)S(1)}, bf16[16,2,2,32,128]{4,3,2,0,1:T(8,128)(2,1)S(1)}, u32[]{:S(2)}, u32[]{:S(2)}) %collective-permute-start) | collective-permute-done | bytes 524320 | tf_op jit(solution)/shard_map/ppermute | solution.py:14
  21.3 15.2 %collective-permute-done.1 = bf16[16,2,2,32,128]{4,3,2,0,1:T(8,128)(2,1)S(1)} collective-permute-done((bf16[16,2,2,32,128]{4,3,2,0,1:T(8,128)(2,1)S(1)}, bf16[16,2,2,32,128]{4,3,2,0,1:T(8,128)(2,1)S(1)}, u32[]{:S(2)}, u32[]{:S(2)}) %collective-permute-start.1) | collective-permute-done | bytes 524320 | tf_op jit(solution)/shard_map/ppermute | solution.py:15
  36.5 0.9 maximum_convert_fusion
  37.4 1.1 slice_bitcast_fusion.1
  38.6 1.0 fusion.58
  39.6 1.6 %fusion.67 = (bf16[16,1,4,32,128]{4,3,2,0,1:T(8,128)(2,1)S(1)}, bf16[16,1,4,32,128]{4,3,2,0,1:T(8,128)(2,1)S(1)}) fusion(f32[16,2,32,128]{3,2,1,0:T(8,128)S(1)} %get-tuple-element.22, f32[16,2,32,128]{3,2,1,0:T(8,128)S(1)} %get-tuple-element.23, f32[16,4,32,128]{3,2,1,0:T(8,128)S(1)} %pad_maximum_fusion.2, f32[16,2,32,128]{3,2,1,0:T(8,128)S(1)} %get-tuple-element.13, ...), kind=kLoop, calls=%fused_computation.117 | loop fusion | flops 4194304 | bytes 4194304 | tf_op jit(solution)/shard_map/stack | solution.py:92
  41.2 0.1 pad_maximum_fusion.3
  41.3 0.1 copy.53
  41.4 1.3 copy.54
  42.7 5.4 %all-to-all-start.1 = ((bf16[16,16,1,16,128]{4,3,1,2,0:T(8,128)(2,1)}), bf16[16,16,1,16,128]{4,3,1,2,0:T(8,128)(2,1)S(1)}, u32[]{:S(2)}, u32[]{:S(2)}) async-start(bf16[16,16,1,16,128]{4,3,1,2,0:T(8,128)(2,1)} %copy.54), calls=%async_computation.1 | async-start | bytes 2097152 | tf_op jit(solution)/shard_map/all_to_all | solution.py:43
  48.1 0.0 copy-start
  48.1 1.5 %slice.243 = f32[16,4,32,128]{3,2,1,0:T(8,128)S(1)} slice(f32[16,8,32,128]{3,2,1,0:T(8,128)} %copy-done.2), slice={[0:16], [2:6], [0:32], [0:128]} | slice | bytes 2097152 | tf_op jit(solution)/shard_map/slice | solution.py:76
  49.6 0.4 copy-done
  50.0 2.1 %fusion.69 = (bf16[16,1,4,32,128]{4,3,2,1,0:T(8,128)(2,1)S(1)}, bf16[16,1,4,32,128]{4,3,2,1,0:T(8,128)(2,1)S(1)}) fusion(f32[16,8,32,128]{3,2,1,0:T(8,128)S(1)} %get-tuple-element.5, f32[16,4,32,128]{3,2,1,0:T(8,128)S(1)} %slice.243, f32[16,8,32,128]{3,2,1,0:T(8,128)S(1)} %copy-done), kind=kLoop, calls=%fused_computation.119 | loop fusion | flops 6291456 | bytes 10485760 | tf_op jit(solution)/shard_map/stack | solution.py:80
  52.1 0.1 pad_maximum_fusion.1
  52.3 2.4 %fusion.5 = bf16[16,8,32,128]{3,2,1,0:T(8,128)(2,1)S(1)} fusion(f32[16,8,32,128]{3,2,1,0:T(8,128)S(1)} %get-tuple-element.5, f32[16,8,32,128]{3,2,1,0:T(8,128)S(1)} %copy-done), kind=kLoop, calls=%fused_computation.26 | loop fusion | flops 6291456 | bytes 5242880 | tf_op jit(solution)/shard_map/convert_element_type | solution.py:75
  54.6 0.2 pad_maximum_fusion
  54.8 1.9 %copy.46 = bf16[16,16,2,16,128]{4,3,1,2,0:T(8,128)(2,1)} copy(bf16[16,16,2,16,128]{4,3,0,1,2:T(8,128)(2,1)S(1)} %pad_maximum_fusion) | data formatting | bytes 4194304 | tf_op jit(solution)/shard_map/stack | solution.py:79
  56.8 0.0 copy-start.4
  56.8 0.0 copy-start.3
  56.8 7.0 %all-to-all-done.1 = bf16[16,16,1,16,128]{4,3,1,2,0:T(8,128)(2,1)S(1)} async-done(((bf16[16,16,1,16,128]{4,3,1,2,0:T(8,128)(2,1)}), bf16[16,16,1,16,128]{4,3,1,2,0:T(8,128)(2,1)S(1)}, u32[]{:S(2)}, u32[]{:S(2)}) %all-to-all-start.1) | async-done | bytes 1048608 | tf_op jit(solution)/shard_map/all_to_all | solution.py:43
  63.8 4.5 %all-to-all-start = ((bf16[16,16,2,16,128]{4,3,1,2,0:T(8,128)(2,1)}), bf16[16,16,2,16,128]{4,3,1,2,0:T(8,128)(2,1)S(1)}, u32[]{:S(2)}, u32[]{:S(2)}) async-start(bf16[16,16,2,16,128]{4,3,1,2,0:T(8,128)(2,1)} %copy.46), calls=%async_computation | async-start | bytes 4194304 | tf_op jit(solution)/shard_map/all_to_all | solution.py:43
  68.3 0.0 copy-done.4
  68.3 0.1 select_reduce_fusion
  68.4 0.0 copy-done.3
  68.4 0.1 convert_reduce_fusion
  68.5 0.3 convolution_divide_fusion
  68.8 1.1 subtract_convert_fusion.1
  69.9 0.5 convolution_bitcast_fusion
  70.4 24.9 %all-to-all-done = bf16[16,16,2,16,128]{4,3,1,2,0:T(8,128)(2,1)S(1)} async-done(((bf16[16,16,2,16,128]{4,3,1,2,0:T(8,128)(2,1)}), bf16[16,16,2,16,128]{4,3,1,2,0:T(8,128)(2,1)S(1)}, u32[]{:S(2)}, u32[]{:S(2)}) %all-to-all-start) | async-done | bytes 2097184 | tf_op jit(solution)/shard_map/all_to_all | solution.py:43
  95.3 0.4 copy.47
  95.7 0.7 fusion.14
  96.4 2.5 %subtract_convert_fusion = bf16[256,32,128]{2,0,1:T(8,128)(2,1)S(1)} fusion(f32[24,32,128]{2,0,1:T(8,128)S(1)} %fusion.14, bf16[256,32,128]{2,1,0:T(8,128)(2,1)S(1)} %bitcast.72, s32[256]{0:T(256)S(1)} %copy-done.3), kind=kOutput, calls=%fused_computation.5 | convolution fusion | flops 305141760 | bytes 4588544 | tf_op jit(solution)/shard_map/sb,bkz->skz/dot_general | solution.py:53
  98.9 1.4 %fusion.18 = f32[256,256]{1,0:T(8,128)} fusion(f32[256,256]{1,0:T(8,128)S(1)} %convolution_bitcast_fusion, bf16[256,32,128]{2,0,1:T(8,128)(2,1)S(1)} %subtract_convert_fusion), kind=kOutput, calls=%fused_computation.52 | convolution fusion | flops 537001984 | bytes 2621440 | tf_op jit(solution)/shard_map/skz,tkz->st/dot_general | solution.py:61
  100.4 4.3 %all-to-all-start.2 = ((f32[16,16,256]{2,1,0:T(8,128)}), f32[16,16,256]{2,1,0:T(8,128)S(1)}, u32[]{:S(2)}, u32[]{:S(2)}) async-start(f32[16,16,256]{2,1,0:T(8,128)} %bitcast.24), calls=%async_computation.2 | async-start | bytes 524288 | tf_op jit(solution)/shard_map/all_to_all | solution.py:32
  104.7 7.2 %all-to-all-done.2 = f32[16,16,256]{2,1,0:T(8,128)S(1)} async-done(((f32[16,16,256]{2,1,0:T(8,128)}), f32[16,16,256]{2,1,0:T(8,128)S(1)}, u32[]{:S(2)}, u32[]{:S(2)}) %all-to-all-start.2) | async-done | bytes 262176 | tf_op jit(solution)/shard_map/all_to_all | solution.py:32
  111.9 0.1 reshape.48
  112.1 0.6 gather_fusion
  112.6 0.1 fusion.82
  112.7 0.1 reshape.60
  112.9 16.0 %all_to_all.20 = f32[16,1,256]{2,1,0:T(1,128)S(1)} all-to-all(f32[16,1,256]{2,1,0:T(1,128)S(1)} %reshape.60), channel_id=1, replica_groups=mesh['space'=16,'snap'=16] {'space'}, dimensions={0} | all-to-all | bytes 32768 | tf_op jit(solution)/shard_map/all_to_all | solution.py:32
  128.9 0.5 broadcast.141
  129.4 0.7 reduce
  130.1 0.1 reshape.61
  130.2 0.7 copy.58
  (8 shorter events, 0.2 us)
Async XLA Ops:
  0.0 8.6 %copy-start.1 = (bf16[16,3,8,32,128]{4,3,2,1,0:T(8,128)(2,1)S(1)}, bf16[16,3,8,32,128]{4,3,2,1,0:T(8,128)(2,1)}, u32[]{:S(2)}) copy-start(bf16[16,3,8,32,128]{4,3,2,1,0:T(8,128)(2,1)} %param.3) | copy-start | bytes 9437188
  1.5 19.8 %collective-permute-start = (bf16[16,2,2,32,128]{4,3,2,0,1:T(8,128)(2,1)S(1)}, bf16[16,2,2,32,128]{4,3,2,0,1:T(8,128)(2,1)S(1)}, u32[]{:S(2)}, u32[]{:S(2)}) collective-permute-start(bf16[16,2,2,32,128]{4,3,2,0,1:T(8,128)(2,1)S(1)} %copy.70), channel_id=1, source_target_pairs={{0,16},{16,32},{32,48},{48,64},{64,80},{80,96},{96,112},{112,128},... | collective-permute-start | bytes 1572872 | tf_op jit(solution)/shard_map/ppermute | solution.py:14
  7.3 29.2 %collective-permute-start.1 = (bf16[16,2,2,32,128]{4,3,2,0,1:T(8,128)(2,1)S(1)}, bf16[16,2,2,32,128]{4,3,2,0,1:T(8,128)(2,1)S(1)}, u32[]{:S(2)}, u32[]{:S(2)}) collective-permute-start(bf16[16,2,2,32,128]{4,3,2,0,1:T(8,128)(2,1)S(1)} %copy.68), channel_id=1, source_target_pairs={{16,0},{32,16},{48,32},{64,48},{80,64},{96,80},{112,96},{128,112},... | collective-permute-start | bytes 1572872 | tf_op jit(solution)/shard_map/ppermute | solution.py:15
  11.6 1.3 copy-start.2
  42.7 21.1 %all-to-all-start.1 = ((bf16[16,16,1,16,128]{4,3,1,2,0:T(8,128)(2,1)}), bf16[16,16,1,16,128]{4,3,1,2,0:T(8,128)(2,1)S(1)}, u32[]{:S(2)}, u32[]{:S(2)}) async-start(bf16[16,16,1,16,128]{4,3,1,2,0:T(8,128)(2,1)} %copy.54), calls=%async_computation.1 | async-start | bytes 2097152 | tf_op jit(solution)/shard_map/all_to_all | solution.py:43
  48.1 1.9 %copy-start = (f32[16,8,32,128]{3,2,1,0:T(8,128)S(1)}, f32[16,8,32,128]{3,2,1,0:T(8,128)}, u32[]{:S(2)}) copy-start(f32[16,8,32,128]{3,2,1,0:T(8,128)} %get-tuple-element.7) | copy-start | bytes 6291460
  56.8 11.5 %copy-start.4 = (s32[16]{0:T(128)S(1)}, s32[16]{0:T(128)}, u32[]{:S(2)}) copy-start(s32[16]{0:T(128)} %param.5) | copy-start | bytes 196
  56.8 11.6 %copy-start.3 = (s32[256]{0:T(256)S(1)}, s32[256]{0:T(256)}, u32[]{:S(2)}) copy-start(s32[256]{0:T(256)} %param.4) | copy-start | bytes 3076
  63.8 31.5 %all-to-all-start = ((bf16[16,16,2,16,128]{4,3,1,2,0:T(8,128)(2,1)}), bf16[16,16,2,16,128]{4,3,1,2,0:T(8,128)(2,1)S(1)}, u32[]{:S(2)}, u32[]{:S(2)}) async-start(bf16[16,16,2,16,128]{4,3,1,2,0:T(8,128)(2,1)} %copy.46), calls=%async_computation | async-start | bytes 4194304 | tf_op jit(solution)/shard_map/all_to_all | solution.py:43
  100.4 11.5 %all-to-all-start.2 = ((f32[16,16,256]{2,1,0:T(8,128)}), f32[16,16,256]{2,1,0:T(8,128)S(1)}, u32[]{:S(2)}, u32[]{:S(2)}) async-start(f32[16,16,256]{2,1,0:T(8,128)} %bitcast.24), calls=%async_computation.2 | async-start | bytes 524288 | tf_op jit(solution)/shard_map/all_to_all | solution.py:32

commit v4 on v2

--- a/solution.py
+++ b/solution.py
@@ -1,6 +1,8 @@
 import jax
 import jax.numpy as jnp
 from jax import lax
+from jax.experimental import pallas as pl
+from jax.experimental.pallas import tpu as pltpu
 from jax.sharding import PartitionSpec as P
 
 NB = 24
@@ -30,6 +32,64 @@
 def d_wide(wide, axis):
     length = wide.shape[axis] - 4
     return stencil(lambda o: lax.slice_in_dim(wide, o, o + length, axis=axis))
+
+
+def shifted(f, offset, axis):
+    size = f.shape[axis]
+    rolled = pltpu.roll(f, (-offset) % size, axis)
+    index = lax.broadcasted_iota(jnp.int32, f.shape, axis) + offset
+    return jnp.where((index >= 0) & (index < size), rolled, 0.0)
+
+
+def d_in(f, axis):
+    return stencil(lambda o: shifted(f, o - 2, axis))
+
+
+def curl_x_kernel(vel_ref, out_ref):
+    cells_x, cells_y = vel_ref.shape[2], vel_ref.shape[3]
+    rows = out_ref.shape[3]
+    for x in range(cells_x):
+        v = vel_ref[0, 1, x].astype(jnp.float32)
+        w = vel_ref[0, 2, x].astype(jnp.float32)
+        omega = (d_in(w, 0) - d_in(v, 1)).astype(out_ref.dtype)
+        for h in range(cells_y // rows):
+            out_ref[x * (cells_y // rows) + h, 0, 0] = omega[h * rows : (h + 1) * rows]
+
+
+def curl_yz_kernel(vel_ref, low_ref, high_ref, out_ref):
+    cells_x, cells_y = vel_ref.shape[2], vel_ref.shape[3]
+    rows = out_ref.shape[3]
+
+    def plane(c, x):
+        if x < 0:
+            return low_ref[0, c - 1, x + 2].astype(jnp.float32)
+        if x >= cells_x:
+            return high_ref[0, c - 1, x - cells_x].astype(jnp.float32)
+        return vel_ref[0, c, x].astype(jnp.float32)
+
+    for x in range(cells_x):
+        u = vel_ref[0, 0, x].astype(jnp.float32)
+        dxw = stencil(lambda o: plane(2, x + o - 2))
+        dxv = stencil(lambda o: plane(1, x + o - 2))
+        omega_y = (d_in(u, 1) - dxw).astype(out_ref.dtype)
+        omega_z = (dxv - d_in(u, 0)).astype(out_ref.dtype)
+        for h in range(cells_y // rows):
+            out_ref[x * (cells_y // rows) + h, 0, 0] = omega_y[h * rows : (h + 1) * rows]
+            out_ref[x * (cells_y // rows) + h, 0, 1] = omega_z[h * rows : (h + 1) * rows]
+
+
+def curl_call(kernel, comps, velocity, halos, n_snap):
+    snaps_dev, _, cells_x, cells_y, cells_z = velocity.shape
+    rows = cells_y * cells_x // n_snap
+    vel_spec = pl.BlockSpec((1,) + velocity.shape[1:], lambda s: (s, 0, 0, 0, 0))
+    halo_specs = [pl.BlockSpec((1,) + h.shape[1:], lambda s: (s, 0, 0, 0, 0)) for h in halos]
+    return pl.pallas_call(
+        kernel,
+        grid=(snaps_dev,),
+        in_specs=[vel_spec] + halo_specs,
+        out_specs=pl.BlockSpec((n_snap, 1, comps, rows, cells_z), lambda s: (0, s, 0, 0, 0)),
+        out_shape=jax.ShapeDtypeStruct((n_snap, snaps_dev, comps, rows, cells_z), jnp.bfloat16),
+    )(velocity, *halos)
 
 
 def all_to_all_sum(x, axis):
@@ -70,22 +130,14 @@
 def per_device(velocity, phase_bins, tile_owner):
     snaps_dev, _, cells_x, cells_y, cells_z = velocity.shape
     n_snap = lax.axis_size("snap")
-    vw_wide = x_halo(velocity[:, 1:3], 2)
-    frame = velocity.astype(jnp.float32)
-    u, v, w = frame[:, 0], frame[:, 1], frame[:, 2]
+    count = lax.axis_size("space")
+    forward = [(i, i + 1) for i in range(count - 1)]
+    backward = [(target, source) for source, target in forward]
+    low = lax.ppermute(velocity[:, 1:3, cells_x - 2 :], "space", forward)
+    high = lax.ppermute(velocity[:, 1:3, :2], "space", backward)
 
-    omega_x = (d_padded(w, 2) - d_padded(v, 3)).astype(jnp.bfloat16)
-    cols_x = exchange(to_parts(omega_x, n_snap)[:, :, None])
-
-    vw_wide = vw_wide.astype(jnp.float32)
-    v_wide, w_wide = vw_wide[:, 0], vw_wide[:, 1]
-    omega_y = d_padded(u, 3) - d_wide(w_wide, 1)
-    omega_z = d_wide(v_wide, 1) - d_padded(u, 2)
-    omega_yz = jnp.stack(
-        [to_parts(omega_y.astype(jnp.bfloat16), n_snap), to_parts(omega_z.astype(jnp.bfloat16), n_snap)],
-        axis=2,
-    )
-    cols_yz = exchange(omega_yz)
+    cols_x = exchange(curl_call(curl_x_kernel, 1, velocity, [], n_snap))
+    cols_yz = exchange(curl_call(curl_yz_kernel, 2, velocity, [low, high], n_snap))
     total_snaps = cols_x.shape[0]
 
     onehot = (phase_bins[None, :] == jnp.arange(NB, dtype=jnp.int32)[:, None])

time: 119 us -> 138 us (1.16)
  Pallas kernels: 0 us -> 21.6 us
  waiting for transfers between devices: 42.4 us -> 59 us
  other arithmetic: 11.9 us -> 1.05 us
  local copies, waits for them, and re-layouts: 14.2 us -> 4.96 us
    pallas_call x0 -> x2, Pallas kernels: none -> 21.6 us  [curl_call(): pl.pallas_call(kernel, grid=(snaps_dev,), in_specs=[vel_spec] + halo_spec...]
    ppermute x2, waiting for transfers between devices: 5.84 us -> 26.9 us  [the longest x1 26.9 us: per_device(): low = lax.ppermute(velocity[:, 1:3, cells_x - 2:], 'space', forward)]
    convert_element_type x4 -> x0, other arithmetic: 9.31 us -> none  [the longest x1 4.2 us: per_device(): omega_y.astype(jnp.bfloat16)]
    all_to_all x2, waiting for transfers between devices: 29.4 us -> 24.8 us  [exchange(): lax.all_to_all(parts, 'snap', split_axis=0, concat_axis=0, tiled=True)]
    squeeze x2 -> x0, local copies, waits for them, and re-layouts: 3.18 us -> none  [the longest x1 2.39 us: per_device(): u, v, w = (frame[:, 0], frame[:, 1], frame[:, 2])]
    reshape x3 -> x0, local copies, waits for them, and re-layouts: 3.02 us -> none  [to_parts(): parts = field.reshape(snaps_dev, cells_x, halves, rows, cells_z)]
    all_to_all x2, starting transfers between devices: 13.7 us -> 16.2 us  [exchange(): lax.all_to_all(parts, 'snap', split_axis=0, concat_axis=0, tiled=True)]
    ppermute x2, starting transfers between devices: 8.44 us -> 6.22 us  [the longest x1 4.93 us: per_device(): low = lax.ppermute(velocity[:, 1:3, cells_x - 2:], 'space', forward)]
  transfers between devices with their start and end apart: 5 -> 5, of which waited for: 4 -> 3; matrix products, arithmetic and copies ran while one was open for 17% -> 2% of each run, Pallas kernels for 0% -> 8%
where the time goes in v4:
time: 138 us; the launch traced here: 137 us
  waiting for transfers between devices  59 us (43%)
  starting transfers between devices  26.7 us (19%)
  Pallas kernels  21.6 us (16%)
  blocking collectives  16.7 us (12%)
  matrix products  7.08 us (5%)
  local copies, waits for them, and re-layouts  4.96 us (4%)
    ppermute x1, waiting for transfers between devices, per_device(): low = lax.ppermute(velocity[:, 1:3, cells_x - 2:], 'space', forward)  26.9 us
    all_to_all x2, waiting for transfers between devices, exchange(): lax.all_to_all(parts, 'snap', split_axis=0, concat_axis=0, tiled=True)  24.8 us
    pallas_call x2, Pallas kernels, curl_call(): pl.pallas_call(kernel, grid=(snaps_dev,), in_specs=[vel_spec] + halo_spec...  21.6 us
    all_to_all x1, blocking collectives, all_to_all_sum(): got = lax.all_to_all(x, axis, split_axis=0, concat_axis=0, tiled=True)  16.7 us
    all_to_all x2, starting transfers between devices, exchange(): lax.all_to_all(parts, 'snap', split_axis=0, concat_axis=0, tiled=True)  16.2 us
    all_to_all x1, waiting for transfers between devices, all_to_all_sum(): got = lax.all_to_all(x, axis, split_axis=0, concat_axis=0, tiled=True)  7.22 us
    ppermute x1, starting transfers between devices, per_device(): low = lax.ppermute(velocity[:, 1:3, cells_x - 2:], 'space', forward)  4.93 us
    all_to_all x1, starting transfers between devices, all_to_all_sum(): got = lax.all_to_all(x, axis, split_axis=0, concat_axis=0, tiled=True)  4.29 us
  transfers between devices with their start and end apart: 5, of which 3 were waited for; matrix products, arithmetic and copies ran while one was open for 2% of the time, Pallas kernels for 8%

profile of v4, /device:TPU:1, one launch (start us, length us, event | category | flops | bytes accessed | tf_op | source)
XLA Modules:
  0.0 137.1 jit_solution(13209771447720348745)
XLA Ops:
  0.0 10.4 %shard_map.37 = bf16[16,16,1,16,128]{4,3,2,1,0:T(8,128)(2,1)} custom-call(bf16[16,3,8,32,128]{4,3,2,1,0:T(8,128)(2,1)} %vel_ref.3), custom_call_target="tpu_custom_call" | custom-call | tf_op jit(solution)/shard_map/pallas_call | solution.py:86
  10.4 7.3 %all-to-all-start = ((bf16[16,16,1,16,128]{4,3,2,1,0:T(8,128)(2,1)}), bf16[16,16,1,16,128]{4,3,2,1,0:T(8,128)(2,1)S(1)}, u32[]{:S(2)}, u32[]{:S(2)}) async-start(bf16[16,16,1,16,128]{4,3,2,1,0:T(8,128)(2,1)} %shard_map.37), calls=%async_computation | async-start | bytes 2097152 | tf_op jit(solution)/shard_map/all_to_all | solution.py:109
  17.8 1.3 fusion.22
  19.1 4.9 %collective-permute-start = (bf16[16,2,2,32,128]{4,3,2,1,0:T(8,128)(2,1)S(1)}, bf16[16,2,2,32,128]{4,3,2,1,0:T(8,128)(2,1)S(1)}, u32[]{:S(2)}, u32[]{:S(2)}) collective-permute-start(bf16[16,2,2,32,128]{4,3,2,1,0:T(8,128)(2,1)S(1)} %get-tuple-element.6), channel_id=1, source_target_pairs={{0,16},{16,32},{32,48},{48,64},{64,80},{80,96},{96,112},{112,128},... | collective-permute-start | bytes 1572872 | tf_op jit(solution)/shard_map/ppermute | solution.py:136
  24.0 1.3 collective-permute-start.1
  25.3 26.9 %collective-permute-done.low_ref = bf16[16,2,2,32,128]{4,3,2,1,0:T(8,128)(2,1)S(1)} collective-permute-done((bf16[16,2,2,32,128]{4,3,2,1,0:T(8,128)(2,1)S(1)}, bf16[16,2,2,32,128]{4,3,2,1,0:T(8,128)(2,1)S(1)}, u32[]{:S(2)}, u32[]{:S(2)}) %collective-permute-start) | collective-permute-done | bytes 524320 | tf_op jit(solution)/shard_map/ppermute | solution.py:136
  52.2 0.0 copy-start
  52.2 0.0 collective-permute-done.1.high_ref
  52.2 0.8 copy-done
  53.0 0.0 copy-start.1
  53.0 0.8 copy-done.1
  53.8 11.1 %shard_map.38 = bf16[16,16,2,16,128]{4,3,2,1,0:T(8,128)(2,1)} custom-call(bf16[16,3,8,32,128]{4,3,2,1,0:T(8,128)(2,1)} %vel_ref.3, bf16[16,2,2,32,128]{4,3,2,1,0:T(8,128)(2,1)} %copy-done, bf16[16,2,2,32,128]{4,3,2,1,0:T(8,128)(2,1)} %copy-done.1), custom_call_target="tpu_custom_call" | custom-call | tf_op jit(solution)/shard_map/pallas_call | solution.py:86
  64.9 0.0 copy-start.3
  64.9 0.0 copy-start.2
  64.9 0.0 all-to-all-done
  64.9 8.8 %all-to-all-start.1 = ((bf16[16,16,2,16,128]{4,3,2,1,0:T(8,128)(2,1)}), bf16[16,16,2,16,128]{4,3,2,1,0:T(8,128)(2,1)S(1)}, u32[]{:S(2)}, u32[]{:S(2)}) async-start(bf16[16,16,2,16,128]{4,3,2,1,0:T(8,128)(2,1)} %shard_map.38), calls=%async_computation.1 | async-start | bytes 4194304 | tf_op jit(solution)/shard_map/all_to_all | solution.py:109
  73.8 0.0 copy-done.3
  73.8 0.1 select_reduce_fusion
  73.9 0.0 copy-done.2
  73.9 0.1 convert_reduce_fusion
  74.0 0.3 convolution_divide_fusion
  74.3 1.1 subtract_convert_fusion.2
  75.4 0.5 convolution_bitcast_fusion
  75.9 24.8 %all-to-all-done.1 = bf16[16,16,2,16,128]{4,3,2,1,0:T(8,128)(2,1)S(1)} async-done(((bf16[16,16,2,16,128]{4,3,2,1,0:T(8,128)(2,1)}), bf16[16,16,2,16,128]{4,3,2,1,0:T(8,128)(2,1)S(1)}, u32[]{:S(2)}, u32[]{:S(2)}) %all-to-all-start.1) | async-done | bytes 2097184 | tf_op jit(solution)/shard_map/all_to_all | solution.py:109
  100.7 0.7 fusion.4
  101.4 1.8 %fusion.12 = f32[256,32,128]{2,0,1:T(8,128)S(1)} fusion(f32[24,32,128]{2,0,1:T(8,128)S(1)} %fusion.4, s32[256]{0:T(256)S(1)} %copy-done.2), kind=kOutput, calls=%fused_computation.18 | convolution fusion | flops 301996032 | bytes 4588544 | tf_op jit(solution)/shard_map/sb,bkz->skz/dot_general | solution.py:119
  103.3 2.7 %fusion.9 = f32[256,256]{1,0:T(8,128)} fusion(f32[256,256]{1,0:T(8,128)S(1)} %convolution_bitcast_fusion, f32[256,32,128]{2,0,1:T(8,128)S(1)} %fusion.12, bf16[256,32,128]{2,1,0:T(8,128)(2,1)S(1)} %bitcast.35), kind=kOutput, calls=%fused_computation.11 | convolution fusion | flops 540147712 | bytes 6815744 | tf_op jit(solution)/shard_map/skz,tkz->st/dot_general | solution.py:127
  105.9 4.3 %all-to-all-start.2 = ((f32[16,16,256]{2,1,0:T(8,128)}), f32[16,16,256]{2,1,0:T(8,128)S(1)}, u32[]{:S(2)}, u32[]{:S(2)}) async-start(f32[16,16,256]{2,1,0:T(8,128)} %bitcast.5), calls=%async_computation.2 | async-start | bytes 524288 | tf_op jit(solution)/shard_map/all_to_all | solution.py:96
  110.3 7.2 %all-to-all-done.2 = f32[16,16,256]{2,1,0:T(8,128)S(1)} async-done(((f32[16,16,256]{2,1,0:T(8,128)}), f32[16,16,256]{2,1,0:T(8,128)S(1)}, u32[]{:S(2)}, u32[]{:S(2)}) %all-to-all-start.2) | async-done | bytes 262176 | tf_op jit(solution)/shard_map/all_to_all | solution.py:96
  117.5 0.1 reshape.36
  117.7 0.6 gather_fusion
  118.2 0.1 fusion.23
  118.3 0.1 reshape.48
  118.4 16.7 %all_to_all.20 = f32[16,1,256]{2,1,0:T(1,128)S(1)} all-to-all(f32[16,1,256]{2,1,0:T(1,128)S(1)} %reshape.48), channel_id=1, replica_groups=mesh['space'=16,'snap'=16] {'space'}, dimensions={0} | all-to-all | bytes 32768 | tf_op jit(solution)/shard_map/all_to_all | solution.py:96
  135.1 0.5 broadcast.59
  135.7 0.7 reduce
  136.3 0.1 reshape.49
  136.5 0.7 copy.24
  (6 shorter events, 0.1 us)
Async XLA Ops:
  10.4 54.5 %all-to-all-start = ((bf16[16,16,1,16,128]{4,3,2,1,0:T(8,128)(2,1)}), bf16[16,16,1,16,128]{4,3,2,1,0:T(8,128)(2,1)S(1)}, u32[]{:S(2)}, u32[]{:S(2)}) async-start(bf16[16,16,1,16,128]{4,3,2,1,0:T(8,128)(2,1)} %shard_map.37), calls=%async_computation | async-start | bytes 2097152 | tf_op jit(solution)/shard_map/all_to_all | solution.py:109
  19.1 33.1 %collective-permute-start = (bf16[16,2,2,32,128]{4,3,2,1,0:T(8,128)(2,1)S(1)}, bf16[16,2,2,32,128]{4,3,2,1,0:T(8,128)(2,1)S(1)}, u32[]{:S(2)}, u32[]{:S(2)}) collective-permute-start(bf16[16,2,2,32,128]{4,3,2,1,0:T(8,128)(2,1)S(1)} %get-tuple-element.6), channel_id=1, source_target_pairs={{0,16},{16,32},{32,48},{48,64},{64,80},{80,96},{96,112},{112,128},... | collective-permute-start | bytes 1572872 | tf_op jit(solution)/shard_map/ppermute | solution.py:136
  24.0 28.2 %collective-permute-start.1 = (bf16[16,2,2,32,128]{4,3,2,1,0:T(8,128)(2,1)S(1)}, bf16[16,2,2,32,128]{4,3,2,1,0:T(8,128)(2,1)S(1)}, u32[]{:S(2)}, u32[]{:S(2)}) collective-permute-start(bf16[16,2,2,32,128]{4,3,2,1,0:T(8,128)(2,1)S(1)} %get-tuple-element.5), channel_id=1, source_target_pairs={{16,0},{32,16},{48,32},{64,48},{80,64},{96,80},{112,96},{128,112},... | collective-permute-start | bytes 1572872 | tf_op jit(solution)/shard_map/ppermute | solution.py:137
  52.2 0.8 copy-start
  53.0 0.8 copy-start.1
  64.9 8.9 %copy-start.3 = (s32[16]{0:T(128)S(1)}, s32[16]{0:T(128)}, u32[]{:S(2)}) copy-start(s32[16]{0:T(128)} %param.5) | copy-start | bytes 196
  64.9 9.0 %copy-start.2 = (s32[256]{0:T(256)S(1)}, s32[256]{0:T(256)}, u32[]{:S(2)}) copy-start(s32[256]{0:T(256)} %param.4) | copy-start | bytes 3076
  64.9 35.8 %all-to-all-start.1 = ((bf16[16,16,2,16,128]{4,3,2,1,0:T(8,128)(2,1)}), bf16[16,16,2,16,128]{4,3,2,1,0:T(8,128)(2,1)S(1)}, u32[]{:S(2)}, u32[]{:S(2)}) async-start(bf16[16,16,2,16,128]{4,3,2,1,0:T(8,128)(2,1)} %shard_map.38), calls=%async_computation.1 | async-start | bytes 4194304 | tf_op jit(solution)/shard_map/all_to_all | solution.py:109
  105.9 11.5 %all-to-all-start.2 = ((f32[16,16,256]{2,1,0:T(8,128)}), f32[16,16,256]{2,1,0:T(8,128)S(1)}, u32[]{:S(2)}, u32[]{:S(2)}) async-start(f32[16,16,256]{2,1,0:T(8,128)} %bitcast.5), calls=%async_computation.2 | async-start | bytes 524288 | tf_op jit(solution)/shard_map/all_to_all | solution.py:96

commit v5 on v2

v5 whole, which is shorter than its diff:
```python
import jax
import jax.numpy as jnp
from jax import lax
from jax.experimental import pallas as pl
from jax.experimental.pallas import tpu as pltpu
from jax.sharding import PartitionSpec as P


NB = 24


def stencil(window_at):
    return (8.0 * (window_at(3) - window_at(1)) - (window_at(4) - window_at(0))) / 12.0


def shifters(shape):
    masks = {}
    for axis in (0, 1):
        index = lax.broadcasted_iota(jnp.int32, shape, axis)
        for offset in (-2, -1, 1, 2):
            masks[axis, offset] = (index + offset >= 0) & (index + offset < shape[axis])

    def shifted(f, offset, axis):
        rolled = pltpu.roll(f, (-offset) % shape[axis], axis)
        return jnp.where(masks[axis, offset], rolled, 0.0)

    def d_in(f, axis):
        return (8.0 * (shifted(f, 1, axis) - shifted(f, -1, axis)) - (shifted(f, 2, axis) - shifted(f, -2, axis))) / 12.0

    return d_in


def curl_x_kernel(vel_ref, out_ref):
    snaps, _, cells_x, cells_y, _ = vel_ref.shape
    rows = out_ref.shape[3]
    d_in = shifters(vel_ref.shape[3:])
    for s in range(snaps):
        for x in range(cells_x):
            v = vel_ref[s, 1, x].astype(jnp.float32)
            w = vel_ref[s, 2, x].astype(jnp.float32)
            omega = (d_in(w, 0) - d_in(v, 1)).astype(out_ref.dtype)
            for h in range(cells_y // rows):
                out_ref[x * (cells_y // rows) + h, s, 0] = omega[h * rows : (h + 1) * rows]


def curl_yz_kernel(vel_ref, low_ref, high_ref, out_ref):
    snaps, _, cells_x, cells_y, _ = vel_ref.shape
    rows = out_ref.shape[3]
    d_in = shifters(vel_ref.shape[3:])
    for s in range(snaps):
        wide = []
        for c in (1, 2):
            planes = [low_ref[s, c - 1, i] for i in range(2)]
            planes += [vel_ref[s, c, i] for i in range(cells_x)]
            planes += [high_ref[s, c - 1, i] for i in range(2)]
            wide.append([p.astype(jnp.float32) for p in planes])
        v_wide, w_wide = wide
        for x in range(cells_x):
            u = vel_ref[s, 0, x].astype(jnp.float32)
            dxw = stencil(lambda o: w_wide[x + o])
            dxv = stencil(lambda o: v_wide[x + o])
            omega_y = (d_in(u, 1) - dxw).astype(out_ref.dtype)
            omega_z = (dxv - d_in(u, 0)).astype(out_ref.dtype)
            for h in range(cells_y // rows):
                out_ref[x * (cells_y // rows) + h, s, 0] = omega_y[h * rows : (h + 1) * rows]
                out_ref[x * (cells_y // rows) + h, s, 1] = omega_z[h * rows : (h + 1) * rows]


def curl_call(kernel, comps, velocity, halos, n_snap):
    snaps_dev, _, cells_x, cells_y, cells_z = velocity.shape
    rows = cells_y * cells_x // n_snap
    block = 4
    vel_spec = pl.BlockSpec((block,) + velocity.shape[1:], lambda s: (s, 0, 0, 0, 0))
    halo_specs = [pl.BlockSpec((block,) + h.shape[1:], lambda s: (s, 0, 0, 0, 0)) for h in halos]
    return pl.pallas_call(
        kernel,
        grid=(snaps_dev // block,),
        in_specs=[vel_spec] + halo_specs,
        out_specs=pl.BlockSpec((n_snap, block, comps, rows, cells_z), lambda s: (0, s, 0, 0, 0)),
        out_shape=jax.ShapeDtypeStruct((n_snap, snaps_dev, comps, rows, cells_z), jnp.bfloat16),
    )(velocity, *halos)


def all_to_all_sum(x, axis):
    got = lax.all_to_all(x, axis, split_axis=0, concat_axis=0, tiled=True)
    return jnp.sum(got, axis=0)


def exchange(parts):
    arranged = lax.all_to_all(parts, "snap", split_axis=0, concat_axis=0, tiled=True)
    count, snaps_dev, comps, rows, cells_z = arranged.shape
    return arranged.reshape(count * snaps_dev, comps * rows, cells_z)


def fluctuation_of(columns, onehot, bin_counts):
    bin_sums = jnp.einsum(
        "bs,skz->bkz", onehot.astype(jnp.bfloat16), columns, preferred_element_type=jnp.float32
    )
    bin_means = bin_sums / bin_counts[:, None, None]
    selected = jnp.einsum(
        "sb,bkz->skz",
        onehot.T.astype(jnp.float32),
        bin_means,
        precision=lax.Precision.HIGHEST,
        preferred_element_type=jnp.float32,
    )
    fluct = (columns.astype(jnp.float32) - selected).astype(jnp.bfloat16)
    return jnp.einsum("skz,tkz->st", fluct, fluct, preferred_element_type=jnp.float32)


def body(velocity, phase_bins, tile_owner):
    _, _, cells_x, cells_y, cells_z = velocity.shape
    n_snap = lax.axis_size("snap")
    count = lax.axis_size("space")
    forward = [(i, i + 1) for i in range(count - 1)]
    backward = [(target, source) for source, target in forward]
    low = lax.ppermute(velocity[:, 1:3, cells_x - 2 :], "space", forward)
    high = lax.ppermute(velocity[:, 1:3, :2], "space", backward)

    parts_x = curl_call(curl_x_kernel, 1, velocity, [], n_snap)
    cols_x = exchange(parts_x)
    cols_yz = exchange(curl_call(curl_yz_kernel, 2, velocity, [low, high], n_snap))
    total_snaps = cols_x.shape[0]

    onehot = (phase_bins[None, :] == jnp.arange(NB, dtype=jnp.int32)[:, None])
    bin_counts = jnp.sum(onehot.astype(jnp.float32), axis=1)
    voxel_total = lax.axis_size("space") * cells_x * cells_y * cells_z
    partial_gram = (
        fluctuation_of(cols_x, onehot, bin_counts) + fluctuation_of(cols_yz, onehot, bin_counts)
    ) / voxel_total

    row_blocks = partial_gram.reshape(n_snap, total_snaps // n_snap, total_snaps)
    col_sum = all_to_all_sum(row_blocks, "snap")
    tile_count = lax.axis_size("space")
    tile_ids = jnp.arange(tile_count, dtype=jnp.int32)
    inverse = jnp.sum(
        tile_ids[None, :] * (tile_owner[None, :] == tile_ids[:, None]).astype(jnp.int32), axis=1
    )
    tiles = col_sum.reshape(col_sum.shape[0], tile_count, total_snaps // tile_count)
    tiles = jnp.transpose(jnp.take(tiles, inverse, axis=1), (1, 2, 0))
    mine = all_to_all_sum(tiles, "space")
    return mine[None]


def solution(mesh):
    return jax.shard_map(
        body,
        mesh=mesh,
        in_specs=(P("snap", None, "space", None, None), P(), P()),
        out_specs=P("space", None, "snap"),
        check_vma=False,
    )
```

time: 119 us -> 127 us (1.067)
  waiting for transfers between devices: 42.4 us -> 59 us
  other arithmetic: 11.9 us -> 1.05 us
  Pallas kernels: 0 us -> 10.7 us
  local copies, waits for them, and re-layouts: 14.2 us -> 4.96 us
  matrix products: 5.74 us -> 7.08 us
    ppermute x2, waiting for transfers between devices: 5.84 us -> 26.9 us  [the longest x1 26.9 us: body(): low = lax.ppermute(velocity[:, 1:3, cells_x - 2:], 'space', forward)]
    pallas_call x0 -> x2, Pallas kernels: none -> 10.7 us  [curl_call(): pl.pallas_call(kernel, grid=(snaps_dev // block,), in_specs=[vel_spec] +...]
    convert_element_type x4 -> x0, other arithmetic: 9.31 us -> none  [the longest x1 4.2 us: per_device(): omega_y.astype(jnp.bfloat16)]
    all_to_all x2, waiting for transfers between devices: 29.4 us -> 24.8 us  [exchange(): lax.all_to_all(parts, 'snap', split_axis=0, concat_axis=0, tiled=True)]
    squeeze x2 -> x0, local copies, waits for them, and re-layouts: 3.18 us -> none  [the longest x1 2.39 us: per_device(): u, v, w = (frame[:, 0], frame[:, 1], frame[:, 2])]
    reshape x5 -> x2, local copies, waits for them, and re-layouts: 3.15 us -> 0.14 us  [body(): col_sum.reshape(col_sum.shape[0], tile_count, total_snaps // tile_count)]
    all_to_all x2, starting transfers between devices: 13.7 us -> 16.2 us  [exchange(): lax.all_to_all(parts, 'snap', split_axis=0, concat_axis=0, tiled=True)]
    ppermute x2, starting transfers between devices: 8.44 us -> 6.22 us  [the longest x1 4.93 us: body(): low = lax.ppermute(velocity[:, 1:3, cells_x - 2:], 'space', forward)]
  transfers between devices with their start and end apart: 5 -> 5, of which waited for: 4 -> 3; matrix products, arithmetic and copies ran while one was open for 17% -> 3% of each run, Pallas kernels for 0% -> 5%
where the time goes in v5:
time: 127 us; the launch traced here: 126 us
  waiting for transfers between devices  59 us (46%)
  starting transfers between devices  26.7 us (21%)
  blocking collectives  16.7 us (13%)
  Pallas kernels  10.7 us (8%)
  matrix products  7.08 us (6%)
  local copies, waits for them, and re-layouts  4.96 us (4%)
    ppermute x1, waiting for transfers between devices, body(): low = lax.ppermute(velocity[:, 1:3, cells_x - 2:], 'space', forward)  26.9 us
    all_to_all x2, waiting for transfers between devices, exchange(): lax.all_to_all(parts, 'snap', split_axis=0, concat_axis=0, tiled=True)  24.8 us
    all_to_all x1, blocking collectives, all_to_all_sum(): got = lax.all_to_all(x, axis, split_axis=0, concat_axis=0, tiled=True)  16.7 us
    all_to_all x2, starting transfers between devices, exchange(): lax.all_to_all(parts, 'snap', split_axis=0, concat_axis=0, tiled=True)  16.2 us
    pallas_call x2, Pallas kernels, curl_call(): pl.pallas_call(kernel, grid=(snaps_dev // block,), in_specs=[vel_spec] +...  10.7 us
    all_to_all x1, waiting for transfers between devices, all_to_all_sum(): got = lax.all_to_all(x, axis, split_axis=0, concat_axis=0, tiled=True)  7.22 us
    ppermute x1, starting transfers between devices, body(): low = lax.ppermute(velocity[:, 1:3, cells_x - 2:], 'space', forward)  4.93 us
    all_to_all x1, starting transfers between devices, all_to_all_sum(): got = lax.all_to_all(x, axis, split_axis=0, concat_axis=0, tiled=True)  4.29 us
  transfers between devices with their start and end apart: 5, of which 3 were waited for; matrix products, arithmetic and copies ran while one was open for 3% of the time, Pallas kernels for 5%

profile of v5, /device:TPU:1, one launch (start us, length us, event | category | flops | bytes accessed | tf_op | source)
XLA Modules:
  0.0 126.3 jit_solution(9528350104513213675)
XLA Ops:
  0.0 4.9 %shard_map.37 = bf16[16,16,1,16,128]{4,3,2,1,0:T(8,128)(2,1)} custom-call(bf16[16,3,8,32,128]{4,3,2,1,0:T(8,128)(2,1)} %vel_ref.3), custom_call_target="tpu_custom_call" | custom-call | tf_op jit(solution)/shard_map/pallas_call | solution.py:75
  4.9 7.3 %all-to-all-start = ((bf16[16,16,1,16,128]{4,3,2,1,0:T(8,128)(2,1)}), bf16[16,16,1,16,128]{4,3,2,1,0:T(8,128)(2,1)S(1)}, u32[]{:S(2)}, u32[]{:S(2)}) async-start(bf16[16,16,1,16,128]{4,3,2,1,0:T(8,128)(2,1)} %shard_map.37), calls=%async_computation | async-start | bytes 2097152 | tf_op jit(solution)/shard_map/all_to_all | solution.py:90
  12.2 1.3 %fusion.22 = (bf16[16,2,2,32,128]{4,3,2,1,0:T(8,128)(2,1)S(1)}, bf16[16,2,2,32,128]{4,3,2,1,0:T(8,128)(2,1)S(1)}) fusion(bf16[16,3,8,32,128]{4,3,2,1,0:T(8,128)(2,1)} %vel_ref.3), kind=kLoop, calls=%fused_computation.30 | loop fusion | bytes 2097152 | tf_op jit(solution)/shard_map/slice | solution.py:118
  13.5 4.9 %collective-permute-start = (bf16[16,2,2,32,128]{4,3,2,1,0:T(8,128)(2,1)S(1)}, bf16[16,2,2,32,128]{4,3,2,1,0:T(8,128)(2,1)S(1)}, u32[]{:S(2)}, u32[]{:S(2)}) collective-permute-start(bf16[16,2,2,32,128]{4,3,2,1,0:T(8,128)(2,1)S(1)} %get-tuple-element.6), channel_id=1, source_target_pairs={{0,16},{16,32},{32,48},{48,64},{64,80},{80,96},{96,112},{112,128},... | collective-permute-start | bytes 1572872 | tf_op jit(solution)/shard_map/ppermute | solution.py:117
  18.4 1.3 %collective-permute-start.1 = (bf16[16,2,2,32,128]{4,3,2,1,0:T(8,128)(2,1)S(1)}, bf16[16,2,2,32,128]{4,3,2,1,0:T(8,128)(2,1)S(1)}, u32[]{:S(2)}, u32[]{:S(2)}) collective-permute-start(bf16[16,2,2,32,128]{4,3,2,1,0:T(8,128)(2,1)S(1)} %get-tuple-element.5), channel_id=1, source_target_pairs={{16,0},{32,16},{48,32},{64,48},{80,64},{96,80},{112,96},{128,112},... | collective-permute-start | bytes 1572872 | tf_op jit(solution)/shard_map/ppermute | solution.py:118
  19.7 26.9 %collective-permute-done.low_ref = bf16[16,2,2,32,128]{4,3,2,1,0:T(8,128)(2,1)S(1)} collective-permute-done((bf16[16,2,2,32,128]{4,3,2,1,0:T(8,128)(2,1)S(1)}, bf16[16,2,2,32,128]{4,3,2,1,0:T(8,128)(2,1)S(1)}, u32[]{:S(2)}, u32[]{:S(2)}) %collective-permute-start) | collective-permute-done | bytes 524320 | tf_op jit(solution)/shard_map/ppermute | solution.py:117
  46.6 0.0 copy-start
  46.6 0.0 collective-permute-done.1.high_ref
  46.6 0.8 copy-done
  47.4 0.0 copy-start.1
  47.4 0.8 copy-done.1
  48.2 5.9 %shard_map.38 = bf16[16,16,2,16,128]{4,3,2,1,0:T(8,128)(2,1)} custom-call(bf16[16,3,8,32,128]{4,3,2,1,0:T(8,128)(2,1)} %vel_ref.3, bf16[16,2,2,32,128]{4,3,2,1,0:T(8,128)(2,1)} %copy-done, bf16[16,2,2,32,128]{4,3,2,1,0:T(8,128)(2,1)} %copy-done.1), custom_call_target="tpu_custom_call" | custom-call | tf_op jit(solution)/shard_map/pallas_call | solution.py:75
  54.1 0.0 copy-start.3
  54.1 0.0 copy-start.2
  54.1 0.0 all-to-all-done
  54.1 8.8 %all-to-all-start.1 = ((bf16[16,16,2,16,128]{4,3,2,1,0:T(8,128)(2,1)}), bf16[16,16,2,16,128]{4,3,2,1,0:T(8,128)(2,1)S(1)}, u32[]{:S(2)}, u32[]{:S(2)}) async-start(bf16[16,16,2,16,128]{4,3,2,1,0:T(8,128)(2,1)} %shard_map.38), calls=%async_computation.1 | async-start | bytes 4194304 | tf_op jit(solution)/shard_map/all_to_all | solution.py:90
  63.0 0.0 copy-done.3
  63.0 0.1 select_reduce_fusion
  63.1 0.0 copy-done.2
  63.1 0.1 convert_reduce_fusion
  63.2 0.3 convolution_divide_fusion
  63.5 1.1 subtract_convert_fusion.2
  64.6 0.5 convolution_bitcast_fusion
  65.1 24.8 %all-to-all-done.1 = bf16[16,16,2,16,128]{4,3,2,1,0:T(8,128)(2,1)S(1)} async-done(((bf16[16,16,2,16,128]{4,3,2,1,0:T(8,128)(2,1)}), bf16[16,16,2,16,128]{4,3,2,1,0:T(8,128)(2,1)S(1)}, u32[]{:S(2)}, u32[]{:S(2)}) %all-to-all-start.1) | async-done | bytes 2097184 | tf_op jit(solution)/shard_map/all_to_all | solution.py:90
  89.9 0.7 fusion.4
  90.6 1.8 %fusion.12 = f32[256,32,128]{2,0,1:T(8,128)S(1)} fusion(f32[24,32,128]{2,0,1:T(8,128)S(1)} %fusion.4, s32[256]{0:T(256)S(1)} %copy-done.2), kind=kOutput, calls=%fused_computation.18 | convolution fusion | flops 301996032 | bytes 4588544 | tf_op jit(solution)/shard_map/sb,bkz->skz/dot_general | solution.py:100
  92.4 2.7 %fusion.9 = f32[256,256]{1,0:T(8,128)} fusion(f32[256,256]{1,0:T(8,128)S(1)} %convolution_bitcast_fusion, f32[256,32,128]{2,0,1:T(8,128)S(1)} %fusion.12, bf16[256,32,128]{2,1,0:T(8,128)(2,1)S(1)} %bitcast.35), kind=kOutput, calls=%fused_computation.11 | convolution fusion | flops 540147712 | bytes 6815744 | tf_op jit(solution)/shard_map/skz,tkz->st/dot_general | solution.py:108
  95.1 4.3 %all-to-all-start.2 = ((f32[16,16,256]{2,1,0:T(8,128)}), f32[16,16,256]{2,1,0:T(8,128)S(1)}, u32[]{:S(2)}, u32[]{:S(2)}) async-start(f32[16,16,256]{2,1,0:T(8,128)} %bitcast.5), calls=%async_computation.2 | async-start | bytes 524288 | tf_op jit(solution)/shard_map/all_to_all | solution.py:85
  99.4 7.2 %all-to-all-done.2 = f32[16,16,256]{2,1,0:T(8,128)S(1)} async-done(((f32[16,16,256]{2,1,0:T(8,128)}), f32[16,16,256]{2,1,0:T(8,128)S(1)}, u32[]{:S(2)}, u32[]{:S(2)}) %all-to-all-start.2) | async-done | bytes 262176 | tf_op jit(solution)/shard_map/all_to_all | solution.py:85
  106.7 0.1 reshape.36
  106.8 0.6 gather_fusion
  107.4 0.1 fusion.23
  107.5 0.1 reshape.48
  107.6 16.7 %all_to_all.20 = f32[16,1,256]{2,1,0:T(1,128)S(1)} all-to-all(f32[16,1,256]{2,1,0:T(1,128)S(1)} %reshape.48), channel_id=1, replica_groups=mesh['space'=16,'snap'=16] {'space'}, dimensions={0} | all-to-all | bytes 32768 | tf_op jit(solution)/shard_map/all_to_all | solution.py:85
  124.3 0.5 broadcast.59
  124.8 0.7 reduce
  125.5 0.1 reshape.49
  125.6 0.7 copy.24
  (6 shorter events, 0.1 us)
Async XLA Ops:
  4.9 49.3 %all-to-all-start = ((bf16[16,16,1,16,128]{4,3,2,1,0:T(8,128)(2,1)}), bf16[16,16,1,16,128]{4,3,2,1,0:T(8,128)(2,1)S(1)}, u32[]{:S(2)}, u32[]{:S(2)}) async-start(bf16[16,16,1,16,128]{4,3,2,1,0:T(8,128)(2,1)} %shard_map.37), calls=%async_computation | async-start | bytes 2097152 | tf_op jit(solution)/shard_map/all_to_all | solution.py:90
  13.5 33.1 %collective-permute-start = (bf16[16,2,2,32,128]{4,3,2,1,0:T(8,128)(2,1)S(1)}, bf16[16,2,2,32,128]{4,3,2,1,0:T(8,128)(2,1)S(1)}, u32[]{:S(2)}, u32[]{:S(2)}) collective-permute-start(bf16[16,2,2,32,128]{4,3,2,1,0:T(8,128)(2,1)S(1)} %get-tuple-element.6), channel_id=1, source_target_pairs={{0,16},{16,32},{32,48},{48,64},{64,80},{80,96},{96,112},{112,128},... | collective-permute-start | bytes 1572872 | tf_op jit(solution)/shard_map/ppermute | solution.py:117
  18.4 28.2 %collective-permute-start.1 = (bf16[16,2,2,32,128]{4,3,2,1,0:T(8,128)(2,1)S(1)}, bf16[16,2,2,32,128]{4,3,2,1,0:T(8,128)(2,1)S(1)}, u32[]{:S(2)}, u32[]{:S(2)}) collective-permute-start(bf16[16,2,2,32,128]{4,3,2,1,0:T(8,128)(2,1)S(1)} %get-tuple-element.5), channel_id=1, source_target_pairs={{16,0},{32,16},{48,32},{64,48},{80,64},{96,80},{112,96},{128,112},... | collective-permute-start | bytes 1572872 | tf_op jit(solution)/shard_map/ppermute | solution.py:118
  46.6 0.8 copy-start
  47.4 0.8 copy-start.1
  54.1 8.9 %copy-start.3 = (s32[16]{0:T(128)S(1)}, s32[16]{0:T(128)}, u32[]{:S(2)}) copy-start(s32[16]{0:T(128)} %param.5) | copy-start | bytes 196
  54.1 9.0 %copy-start.2 = (s32[256]{0:T(256)S(1)}, s32[256]{0:T(256)}, u32[]{:S(2)}) copy-start(s32[256]{0:T(256)} %param.4) | copy-start | bytes 3076
  54.1 35.8 %all-to-all-start.1 = ((bf16[16,16,2,16,128]{4,3,2,1,0:T(8,128)(2,1)}), bf16[16,16,2,16,128]{4,3,2,1,0:T(8,128)(2,1)S(1)}, u32[]{:S(2)}, u32[]{:S(2)}) async-start(bf16[16,16,2,16,128]{4,3,2,1,0:T(8,128)(2,1)} %shard_map.38), calls=%async_computation.1 | async-start | bytes 4194304 | tf_op jit(solution)/shard_map/all_to_all | solution.py:90
  95.1 11.6 %all-to-all-start.2 = ((f32[16,16,256]{2,1,0:T(8,128)}), f32[16,16,256]{2,1,0:T(8,128)S(1)}, u32[]{:S(2)}, u32[]{:S(2)}) async-start(f32[16,16,256]{2,1,0:T(8,128)} %bitcast.5), calls=%async_computation.2 | async-start | bytes 524288 | tf_op jit(solution)/shard_map/all_to_all | solution.py:85

commit v6 on v5

--- a/solution.py
+++ b/solution.py
@@ -30,23 +30,35 @@
     return d_in
 
 
-def curl_x_kernel(vel_ref, out_ref):
+def curl_early_kernel(vel_ref, out_ref):
     snaps, _, cells_x, cells_y, _ = vel_ref.shape
     rows = out_ref.shape[3]
+    halves = cells_y // rows
+    inner = cells_x - 4
     d_in = shifters(vel_ref.shape[3:])
     for s in range(snaps):
+        planes = [[vel_ref[s, c, i].astype(jnp.float32) for i in range(cells_x)] for c in range(3)]
+        u, v, w = planes
         for x in range(cells_x):
-            v = vel_ref[s, 1, x].astype(jnp.float32)
-            w = vel_ref[s, 2, x].astype(jnp.float32)
-            omega = (d_in(w, 0) - d_in(v, 1)).astype(out_ref.dtype)
-            for h in range(cells_y // rows):
-                out_ref[x * (cells_y // rows) + h, s, 0] = omega[h * rows : (h + 1) * rows]
+            omega = (d_in(w[x], 0) - d_in(v[x], 1)).astype(out_ref.dtype)
+            for h in range(halves):
+                out_ref[x * halves + h, s, 0] = omega[h * rows : (h + 1) * rows]
+            if 2 <= x < cells_x - 2:
+                dxw = stencil(lambda o: w[x + o - 2])
+                dxv = stencil(lambda o: v[x + o - 2])
+                omega_y = (d_in(u[x], 1) - dxw).astype(out_ref.dtype)
+                omega_z = (dxv - d_in(u[x], 0)).astype(out_ref.dtype)
+                for h in range(halves):
+                    out_ref[(x - 2) * halves + h, s, 1] = omega_y[h * rows : (h + 1) * rows]
+                    out_ref[(inner + x - 2) * halves + h, s, 1] = omega_z[h * rows : (h + 1) * rows]
 
 
-def curl_yz_kernel(vel_ref, low_ref, high_ref, out_ref):
+def curl_edge_kernel(vel_ref, low_ref, high_ref, out_ref):
     snaps, _, cells_x, cells_y, _ = vel_ref.shape
     rows = out_ref.shape[3]
+    halves = cells_y // rows
     d_in = shifters(vel_ref.shape[3:])
+    edges = [0, 1, cells_x - 2, cells_x - 1]
     for s in range(snaps):
         wide = []
         for c in (1, 2):
@@ -55,15 +67,15 @@
             planes += [high_ref[s, c - 1, i] for i in range(2)]
             wide.append([p.astype(jnp.float32) for p in planes])
         v_wide, w_wide = wide
-        for x in range(cells_x):
+        for e, x in enumerate(edges):
             u = vel_ref[s, 0, x].astype(jnp.float32)
             dxw = stencil(lambda o: w_wide[x + o])
             dxv = stencil(lambda o: v_wide[x + o])
             omega_y = (d_in(u, 1) - dxw).astype(out_ref.dtype)
             omega_z = (dxv - d_in(u, 0)).astype(out_ref.dtype)
-            for h in range(cells_y // rows):
-                out_ref[x * (cells_y // rows) + h, s, 0] = omega_y[h * rows : (h + 1) * rows]
-                out_ref[x * (cells_y // rows) + h, s, 1] = omega_z[h * rows : (h + 1) * rows]
+            for h in range(halves):
+                out_ref[e * halves + h, s, 0] = omega_y[h * rows : (h + 1) * rows]
+                out_ref[(len(edges) + e) * halves + h, s, 0] = omega_z[h * rows : (h + 1) * rows]
 
 
 def curl_call(kernel, comps, velocity, halos, n_snap):
@@ -117,9 +129,10 @@
     low = lax.ppermute(velocity[:, 1:3, cells_x - 2 :], "space", forward)
     high = lax.ppermute(velocity[:, 1:3, :2], "space", backward)
 
-    parts_x = curl_call(curl_x_kernel, 1, velocity, [], n_snap)
+    parts_x = curl_call(curl_early_kernel, 2, velocity, [], n_snap)
     cols_x = exchange(parts_x)
-    cols_yz = exchange(curl_call(curl_yz_kernel, 2, velocity, [low, high], n_snap))
+    low, high, cols_x = lax.optimization_barrier((low, high, cols_x))
+    cols_yz = exchange(curl_call(curl_edge_kernel, 1, velocity, [low, high], n_snap))
     total_snaps = cols_x.shape[0]
 
     onehot = (phase_bins[None, :] == jnp.arange(NB, dtype=jnp.int32)[:, None])

time: 127 us -> 128 us (level)
  matrix products: 7.08 us -> 9 us
  waiting for transfers between devices: 59 us -> 57.2 us
    all_to_all x2, waiting for transfers between devices: 24.8 us -> 11 us  [exchange(): lax.all_to_all(parts, 'snap', split_axis=0, concat_axis=0, tiled=True)]
    ppermute x1, waiting for transfers between devices: 26.9 us -> 39 us  [body(): low = lax.ppermute(velocity[:, 1:3, cells_x - 2:], 'space', forward)]
    dot_general x2, matrix products: 2.98 us -> 4.91 us  [fluctuation_of(): jnp.einsum('sb,bkz->skz', onehot.T.astype(jnp.float32), bin_means, precis...]
  transfers between devices with their start and end apart: 5 -> 5, of which waited for: 3 -> 3; matrix products, arithmetic and copies ran while one was open for 3% -> 5% of each run, Pallas kernels for 5% -> 0%
where the time goes in v6:
time: 128 us; the launch traced here: 127 us
  waiting for transfers between devices  57.2 us (45%)
  starting transfers between devices  27.1 us (21%)
  blocking collectives  16.7 us (13%)
  Pallas kernels  10.8 us (8%)
  matrix products  9 us (7%)
  local copies, waits for them, and re-layouts  4.92 us (4%)
    ppermute x1, waiting for transfers between devices, body(): low = lax.ppermute(velocity[:, 1:3, cells_x - 2:], 'space', forward)  39 us
    all_to_all x1, blocking collectives, all_to_all_sum(): got = lax.all_to_all(x, axis, split_axis=0, concat_axis=0, tiled=True)  16.7 us
    all_to_all x2, starting transfers between devices, exchange(): lax.all_to_all(parts, 'snap', split_axis=0, concat_axis=0, tiled=True)  16.6 us
    all_to_all x2, waiting for transfers between devices, exchange(): lax.all_to_all(parts, 'snap', split_axis=0, concat_axis=0, tiled=True)  11 us
    pallas_call x2, Pallas kernels, curl_call(): pl.pallas_call(kernel, grid=(snaps_dev // block,), in_specs=[vel_spec] +...  10.8 us
    all_to_all x1, waiting for transfers between devices, all_to_all_sum(): got = lax.all_to_all(x, axis, split_axis=0, concat_axis=0, tiled=True)  7.22 us
    ppermute x1, starting transfers between devices, body(): low = lax.ppermute(velocity[:, 1:3, cells_x - 2:], 'space', forward)  4.93 us
    dot_general x2, matrix products, fluctuation_of(): jnp.einsum('sb,bkz->skz', onehot.T.astype(jnp.float32), bin_means, precis...  4.91 us
  transfers between devices with their start and end apart: 5, of which 3 were waited for; matrix products, arithmetic and copies ran while one was open for 5% of the time, Pallas kernels for 0%

profile of v6, /device:TPU:1, one launch (start us, length us, event | category | flops | bytes accessed | tf_op | source)
XLA Modules:
  0.0 126.9 jit_solution(13708503252863182192)
XLA Ops:
  0.0 6.0 %shard_map.37 = bf16[16,16,2,16,128]{4,3,2,1,0:T(8,128)(2,1)} custom-call(bf16[16,3,8,32,128]{4,3,2,1,0:T(8,128)(2,1)} %vel_ref.3), custom_call_target="tpu_custom_call" | custom-call | tf_op jit(solution)/shard_map/pallas_call | solution.py:87
  6.0 7.3 %all-to-all-start = ((bf16[16,16,2,16,128]{4,3,2,1,0:T(8,128)(2,1)}), bf16[16,16,2,16,128]{4,3,2,1,0:T(8,128)(2,1)S(1)}, u32[]{:S(2)}, u32[]{:S(2)}) async-start(bf16[16,16,2,16,128]{4,3,2,1,0:T(8,128)(2,1)} %shard_map.37), calls=%async_computation | async-start | bytes 4194304 | tf_op jit(solution)/shard_map/all_to_all | solution.py:102
  13.4 1.3 %fusion.22 = (bf16[16,2,2,32,128]{4,3,2,1,0:T(8,128)(2,1)S(1)}, bf16[16,2,2,32,128]{4,3,2,1,0:T(8,128)(2,1)S(1)}) fusion(bf16[16,3,8,32,128]{4,3,2,1,0:T(8,128)(2,1)} %vel_ref.3), kind=kLoop, calls=%fused_computation.30 | loop fusion | bytes 2097152 | tf_op jit(solution)/shard_map/slice | solution.py:130
  14.7 4.9 %collective-permute-start = (bf16[16,2,2,32,128]{4,3,2,1,0:T(8,128)(2,1)S(1)}, bf16[16,2,2,32,128]{4,3,2,1,0:T(8,128)(2,1)S(1)}, u32[]{:S(2)}, u32[]{:S(2)}) collective-permute-start(bf16[16,2,2,32,128]{4,3,2,1,0:T(8,128)(2,1)S(1)} %get-tuple-element.12), channel_id=1, source_target_pairs={{0,16},{16,32},{32,48},{48,64},{64,80},{80,96},{96,112},{112,128},... | collective-permute-start | bytes 1572872 | tf_op jit(solution)/shard_map/ppermute | solution.py:129
  19.6 1.3 %collective-permute-start.1 = (bf16[16,2,2,32,128]{4,3,2,1,0:T(8,128)(2,1)S(1)}, bf16[16,2,2,32,128]{4,3,2,1,0:T(8,128)(2,1)S(1)}, u32[]{:S(2)}, u32[]{:S(2)}) collective-permute-start(bf16[16,2,2,32,128]{4,3,2,1,0:T(8,128)(2,1)S(1)} %get-tuple-element.11), channel_id=1, source_target_pairs={{16,0},{32,16},{48,32},{64,48},{80,64},{96,80},{112,96},{128,112},... | collective-permute-start | bytes 1572872 | tf_op jit(solution)/shard_map/ppermute | solution.py:130
  20.9 39.0 %collective-permute-done.low_ref = bf16[16,2,2,32,128]{4,3,2,1,0:T(8,128)(2,1)S(1)} collective-permute-done((bf16[16,2,2,32,128]{4,3,2,1,0:T(8,128)(2,1)S(1)}, bf16[16,2,2,32,128]{4,3,2,1,0:T(8,128)(2,1)S(1)}, u32[]{:S(2)}, u32[]{:S(2)}) %collective-permute-start) | collective-permute-done | bytes 524320 | tf_op jit(solution)/shard_map/ppermute | solution.py:129
  59.9 0.0 copy-start.1
  59.9 0.0 collective-permute-done.1.high_ref
  59.9 0.0 copy-start.2
  59.9 0.0 all-to-all-done
  60.0 0.8 copy-done.1
  60.7 0.2 copy-done.2
  60.9 4.7 %shard_map.38 = bf16[16,16,1,16,128]{4,3,2,1,0:T(8,128)(2,1)} custom-call(bf16[16,3,8,32,128]{4,3,2,1,0:T(8,128)(2,1)} %vel_ref.3, bf16[16,2,2,32,128]{4,3,2,1,0:T(8,128)(2,1)} %copy-done.1, bf16[16,2,2,32,128]{4,3,2,1,0:T(8,128)(2,1)} %copy-done.2), custom_call_target="tpu_custom_call" | custom-call | tf_op jit(solution)/shard_map/pallas_call | solution.py:87
  65.6 0.0 copy-start.4
  65.6 0.0 copy-start.3
  65.6 9.2 %all-to-all-start.1 = ((bf16[16,16,1,16,128]{4,3,2,1,0:T(8,128)(2,1)}), bf16[16,16,1,16,128]{4,3,2,1,0:T(8,128)(2,1)S(1)}, u32[]{:S(2)}, u32[]{:S(2)}) async-start(bf16[16,16,1,16,128]{4,3,2,1,0:T(8,128)(2,1)} %shard_map.38), calls=%async_computation.1 | async-start | bytes 2097152 | tf_op jit(solution)/shard_map/all_to_all | solution.py:102
  74.9 0.0 copy-done.4
  74.9 0.1 select_reduce_fusion
  75.0 0.0 copy-done.3
  75.0 0.1 convert_reduce_fusion
  75.1 0.7 fusion.4
  75.8 3.8 %fusion.14 = f32[256,32,128]{2,0,1:T(8,128)} fusion(f32[24,32,128]{2,0,1:T(8,128)S(1)} %fusion.4, s32[256]{0:T(256)S(1)} %copy-done.3), kind=kOutput, calls=%fused_computation.18 | convolution fusion | flops 301996032 | bytes 4588544 | tf_op jit(solution)/shard_map/sb,bkz->skz/dot_general | solution.py:112
  79.6 11.0 %all-to-all-done.1 = bf16[16,16,1,16,128]{4,3,2,1,0:T(8,128)(2,1)S(1)} async-done(((bf16[16,16,1,16,128]{4,3,2,1,0:T(8,128)(2,1)}), bf16[16,16,1,16,128]{4,3,2,1,0:T(8,128)(2,1)S(1)}, u32[]{:S(2)}, u32[]{:S(2)}) %all-to-all-start.1) | async-done | bytes 1048608 | tf_op jit(solution)/shard_map/all_to_all | solution.py:102
  90.6 0.3 convolution_divide_fusion
  90.8 0.0 copy-start
  90.8 1.1 subtract_convert_fusion.2
  92.0 0.5 convolution_bitcast_fusion
  92.4 0.6 copy-done
  93.0 2.7 %fusion.9 = f32[256,256]{1,0:T(8,128)} fusion(f32[256,256]{1,0:T(8,128)S(1)} %convolution_bitcast_fusion, f32[256,32,128]{2,0,1:T(8,128)S(1)} %copy-done, bf16[256,32,128]{2,1,0:T(8,128)(2,1)S(1)} %bitcast.35), kind=kOutput, calls=%fused_computation.11 | convolution fusion | flops 540147712 | bytes 6815744 | tf_op jit(solution)/shard_map/skz,tkz->st/dot_general | solution.py:120
  95.7 4.3 %all-to-all-start.2 = ((f32[16,16,256]{2,1,0:T(8,128)}), f32[16,16,256]{2,1,0:T(8,128)S(1)}, u32[]{:S(2)}, u32[]{:S(2)}) async-start(f32[16,16,256]{2,1,0:T(8,128)} %bitcast.5), calls=%async_computation.2 | async-start | bytes 524288 | tf_op jit(solution)/shard_map/all_to_all | solution.py:97
  100.0 7.2 %all-to-all-done.2 = f32[16,16,256]{2,1,0:T(8,128)S(1)} async-done(((f32[16,16,256]{2,1,0:T(8,128)}), f32[16,16,256]{2,1,0:T(8,128)S(1)}, u32[]{:S(2)}, u32[]{:S(2)}) %all-to-all-start.2) | async-done | bytes 262176 | tf_op jit(solution)/shard_map/all_to_all | solution.py:97
  107.3 0.1 reshape.36
  107.4 0.6 gather_fusion
  108.0 0.1 fusion.23
  108.1 0.1 reshape.48
  108.2 16.7 %all_to_all.20 = f32[16,1,256]{2,1,0:T(1,128)S(1)} all-to-all(f32[16,1,256]{2,1,0:T(1,128)S(1)} %reshape.48), channel_id=1, replica_groups=mesh['space'=16,'snap'=16] {'space'}, dimensions={0} | all-to-all | bytes 32768 | tf_op jit(solution)/shard_map/all_to_all | solution.py:97
  124.9 0.5 broadcast.59
  125.4 0.7 reduce
  126.1 0.1 reshape.49
  126.2 0.7 copy.24
  (6 shorter events, 0.1 us)
Async XLA Ops:
  6.0 53.9 %all-to-all-start = ((bf16[16,16,2,16,128]{4,3,2,1,0:T(8,128)(2,1)}), bf16[16,16,2,16,128]{4,3,2,1,0:T(8,128)(2,1)S(1)}, u32[]{:S(2)}, u32[]{:S(2)}) async-start(bf16[16,16,2,16,128]{4,3,2,1,0:T(8,128)(2,1)} %shard_map.37), calls=%async_computation | async-start | bytes 4194304 | tf_op jit(solution)/shard_map/all_to_all | solution.py:102
  14.7 45.3 %collective-permute-start = (bf16[16,2,2,32,128]{4,3,2,1,0:T(8,128)(2,1)S(1)}, bf16[16,2,2,32,128]{4,3,2,1,0:T(8,128)(2,1)S(1)}, u32[]{:S(2)}, u32[]{:S(2)}) collective-permute-start(bf16[16,2,2,32,128]{4,3,2,1,0:T(8,128)(2,1)S(1)} %get-tuple-element.12), channel_id=1, source_target_pairs={{0,16},{16,32},{32,48},{48,64},{64,80},{80,96},{96,112},{112,128},... | collective-permute-start | bytes 1572872 | tf_op jit(solution)/shard_map/ppermute | solution.py:129
  19.6 40.3 %collective-permute-start.1 = (bf16[16,2,2,32,128]{4,3,2,1,0:T(8,128)(2,1)S(1)}, bf16[16,2,2,32,128]{4,3,2,1,0:T(8,128)(2,1)S(1)}, u32[]{:S(2)}, u32[]{:S(2)}) collective-permute-start(bf16[16,2,2,32,128]{4,3,2,1,0:T(8,128)(2,1)S(1)} %get-tuple-element.11), channel_id=1, source_target_pairs={{16,0},{32,16},{48,32},{64,48},{80,64},{96,80},{112,96},{128,112},... | collective-permute-start | bytes 1572872 | tf_op jit(solution)/shard_map/ppermute | solution.py:130
  59.9 0.8 copy-start.1
  59.9 1.0 copy-start.2
  65.6 9.3 %copy-start.4 = (s32[16]{0:T(128)S(1)}, s32[16]{0:T(128)}, u32[]{:S(2)}) copy-start(s32[16]{0:T(128)} %param.5) | copy-start | bytes 196
  65.6 9.4 %copy-start.3 = (s32[256]{0:T(256)S(1)}, s32[256]{0:T(256)}, u32[]{:S(2)}) copy-start(s32[256]{0:T(256)} %param.4) | copy-start | bytes 3076
  65.6 24.9 %all-to-all-start.1 = ((bf16[16,16,1,16,128]{4,3,2,1,0:T(8,128)(2,1)}), bf16[16,16,1,16,128]{4,3,2,1,0:T(8,128)(2,1)S(1)}, u32[]{:S(2)}, u32[]{:S(2)}) async-start(bf16[16,16,1,16,128]{4,3,2,1,0:T(8,128)(2,1)} %shard_map.38), calls=%async_computation.1 | async-start | bytes 2097152 | tf_op jit(solution)/shard_map/all_to_all | solution.py:102
  90.8 2.2 %copy-start = (f32[256,32,128]{2,0,1:T(8,128)S(1)}, f32[256,32,128]{2,0,1:T(8,128)}, u32[]{:S(2)}) copy-start(f32[256,32,128]{2,0,1:T(8,128)} %fusion.14) | copy-start | bytes 12582916
  95.7 11.5 %all-to-all-start.2 = ((f32[16,16,256]{2,1,0:T(8,128)}), f32[16,16,256]{2,1,0:T(8,128)S(1)}, u32[]{:S(2)}, u32[]{:S(2)}) async-start(f32[16,16,256]{2,1,0:T(8,128)} %bitcast.5), calls=%async_computation.2 | async-start | bytes 524288 | tf_op jit(solution)/shard_map/all_to_all | solution.py:97

commit v7 on v6

--- a/solution.py
+++ b/solution.py
@@ -53,7 +53,7 @@
                     out_ref[(inner + x - 2) * halves + h, s, 1] = omega_z[h * rows : (h + 1) * rows]
 
 
-def curl_edge_kernel(vel_ref, low_ref, high_ref, out_ref):
+def curl_edge_kernel(vel_ref, low_ref, high_ref, _, out_ref):
     snaps, _, cells_x, cells_y, _ = vel_ref.shape
     rows = out_ref.shape[3]
     halves = cells_y // rows
@@ -78,19 +78,27 @@
                 out_ref[(len(edges) + e) * halves + h, s, 0] = omega_z[h * rows : (h + 1) * rows]
 
 
-def curl_call(kernel, comps, velocity, halos, n_snap):
+def curl_call(kernel, comps, velocity, halos, n_snap, slot=0, into=None):
     snaps_dev, _, cells_x, cells_y, cells_z = velocity.shape
     rows = cells_y * cells_x // n_snap
-    block = 4
+    block = 8
     vel_spec = pl.BlockSpec((block,) + velocity.shape[1:], lambda s: (s, 0, 0, 0, 0))
     halo_specs = [pl.BlockSpec((block,) + h.shape[1:], lambda s: (s, 0, 0, 0, 0)) for h in halos]
+    operands = [velocity, *halos]
+    in_specs = [vel_spec] + halo_specs
+    aliases = {}
+    if into is not None:
+        operands.append(into)
+        in_specs.append(pl.BlockSpec(memory_space=pl.ANY))
+        aliases = {len(operands) - 1: 0}
     return pl.pallas_call(
         kernel,
         grid=(snaps_dev // block,),
-        in_specs=[vel_spec] + halo_specs,
-        out_specs=pl.BlockSpec((n_snap, block, comps, rows, cells_z), lambda s: (0, s, 0, 0, 0)),
-        out_shape=jax.ShapeDtypeStruct((n_snap, snaps_dev, comps, rows, cells_z), jnp.bfloat16),
-    )(velocity, *halos)
+        in_specs=in_specs,
+        out_specs=pl.BlockSpec((n_snap, block, comps, rows, cells_z), lambda s: (0, s, slot, 0, 0)),
+        out_shape=jax.ShapeDtypeStruct((n_snap, snaps_dev, 3, rows, cells_z), jnp.bfloat16),
+        input_output_aliases=aliases,
+    )(*operands)
 
 
 def all_to_all_sum(x, axis):
@@ -129,17 +137,16 @@
     low = lax.ppermute(velocity[:, 1:3, cells_x - 2 :], "space", forward)
     high = lax.ppermute(velocity[:, 1:3, :2], "space", backward)
 
-    parts_x = curl_call(curl_early_kernel, 2, velocity, [], n_snap)
-    cols_x = exchange(parts_x)
-    low, high, cols_x = lax.optimization_barrier((low, high, cols_x))
-    cols_yz = exchange(curl_call(curl_edge_kernel, 1, velocity, [low, high], n_snap))
-    total_snaps = cols_x.shape[0]
+    parts = curl_call(curl_early_kernel, 2, velocity, [], n_snap)
+    parts = curl_call(curl_edge_kernel, 1, velocity, [low, high], n_snap, slot=2, into=parts)
+    columns = exchange(parts)
+    total_snaps = columns.shape[0]
 
     onehot = (phase_bins[None, :] == jnp.arange(NB, dtype=jnp.int32)[:, None])
     bin_counts = jnp.sum(onehot.astype(jnp.float32), axis=1)
     voxel_total = lax.axis_size("space") * cells_x * cells_y * cells_z
     partial_gram = (
-        fluctuation_of(cols_x, onehot, bin_counts) + fluctuation_of(cols_yz, onehot, bin_counts)
+        fluctuation_of(columns, onehot, bin_counts)
     ) / voxel_total
 
     row_blocks = partial_gram.reshape(n_snap, total_snaps // n_snap, total_snaps)

time: 128 us -> 121 us (0.945)
  starting transfers between devices: 27.1 us -> 16.9 us
  waiting for transfers between devices: 57.2 us -> 67.1 us
  matrix products: 9 us -> 5.42 us
    ppermute x1, waiting for transfers between devices: 39 us -> 6.78 us  [body(): low = lax.ppermute(velocity[:, 1:3, cells_x - 2:], 'space', forward)]
    all_to_all x2 -> x1, waiting for transfers between devices: 11 us -> 37.9 us  [exchange(): lax.all_to_all(parts, 'snap', split_axis=0, concat_axis=0, tiled=True)]
    ppermute x1, waiting for transfers between devices: 0.01 us -> 15.2 us  [body(): high = lax.ppermute(velocity[:, 1:3, :2], 'space', backward)]
    all_to_all x2 -> x1, starting transfers between devices: 16.6 us -> 5.56 us  [exchange(): lax.all_to_all(parts, 'snap', split_axis=0, concat_axis=0, tiled=True)]
    dot_general x2 -> x1, matrix products: 4.91 us -> 2.66 us  [fluctuation_of(): jnp.einsum('sb,bkz->skz', onehot.T.astype(jnp.float32), bin_means, precis...]
    dot_general x2 -> x1, matrix products: 3.15 us -> 2.2 us  [fluctuation_of(): jnp.einsum('skz,tkz->st', fluct, fluct, preferred_element_type=jnp.float32)]
  transfers between devices with their start and end apart: 5 -> 4, of which waited for: 3 -> 4; matrix products, arithmetic and copies ran while one was open for 5% -> 0% of each run, Pallas kernels for 0% -> 5%
where the time goes in v7:
time: 121 us
  waiting for transfers between devices  67.1 us (55%)
  starting transfers between devices  16.9 us (14%)
  blocking collectives  16 us (13%)
  Pallas kernels  9.99 us (8%)
  matrix products  5.42 us (4%)
  local copies, waits for them, and re-layouts  4.18 us (3%)
    all_to_all x1, waiting for transfers between devices, exchange(): lax.all_to_all(parts, 'snap', split_axis=0, concat_axis=0, tiled=True)  37.9 us
    all_to_all x1, blocking collectives, all_to_all_sum(): got = lax.all_to_all(x, axis, split_axis=0, concat_axis=0, tiled=True)  16 us
    ppermute x1, waiting for transfers between devices, body(): high = lax.ppermute(velocity[:, 1:3, :2], 'space', backward)  15.2 us
    pallas_call x2, Pallas kernels, curl_call(): pl.pallas_call(kernel, grid=(snaps_dev // block,), in_specs=in_specs, out...  9.99 us
    all_to_all x1, waiting for transfers between devices, all_to_all_sum(): got = lax.all_to_all(x, axis, split_axis=0, concat_axis=0, tiled=True)  7.22 us
    ppermute x1, waiting for transfers between devices, body(): low = lax.ppermute(velocity[:, 1:3, cells_x - 2:], 'space', forward)  6.78 us
    ppermute x1, starting transfers between devices, body(): low = lax.ppermute(velocity[:, 1:3, cells_x - 2:], 'space', forward)  5.75 us
    all_to_all x1, starting transfers between devices, exchange(): lax.all_to_all(parts, 'snap', split_axis=0, concat_axis=0, tiled=True)  5.56 us
  transfers between devices with their start and end apart: 4, of which 4 were waited for; matrix products, arithmetic and copies ran while one was open for 0% of the time, Pallas kernels for 5%

profile of v7, /device:TPU:1, one launch (start us, length us, event | category | flops | bytes accessed | tf_op | source)
XLA Modules:
  0.0 120.8 jit_solution(1595507530510345450)
XLA Ops:
  0.0 1.3 %fusion.16 = (bf16[16,2,2,32,128]{4,3,2,1,0:T(8,128)(2,1)S(1)}, bf16[16,2,2,32,128]{4,3,2,1,0:T(8,128)(2,1)S(1)}) fusion(bf16[16,3,8,32,128]{4,3,2,1,0:T(8,128)(2,1)} %vel_ref.3), kind=kLoop, calls=%fused_computation.23 | loop fusion | bytes 2097152 | tf_op jit(solution)/shard_map/slice | solution.py:138
  1.3 5.7 %collective-permute-start = (bf16[16,2,2,32,128]{4,3,2,1,0:T(8,128)(2,1)S(1)}, bf16[16,2,2,32,128]{4,3,2,1,0:T(8,128)(2,1)S(1)}, u32[]{:S(2)}, u32[]{:S(2)}) collective-permute-start(bf16[16,2,2,32,128]{4,3,2,1,0:T(8,128)(2,1)S(1)} %get-tuple-element.6), channel_id=1, source_target_pairs={{0,16},{16,32},{32,48},{48,64},{64,80},{80,96},{96,112},{112,128},... | collective-permute-start | bytes 1572872 | tf_op jit(solution)/shard_map/ppermute | solution.py:137
  7.0 1.3 %collective-permute-start.1 = (bf16[16,2,2,32,128]{4,3,2,1,0:T(8,128)(2,1)S(1)}, bf16[16,2,2,32,128]{4,3,2,1,0:T(8,128)(2,1)S(1)}, u32[]{:S(2)}, u32[]{:S(2)}) collective-permute-start(bf16[16,2,2,32,128]{4,3,2,1,0:T(8,128)(2,1)S(1)} %get-tuple-element.5), channel_id=1, source_target_pairs={{16,0},{32,16},{48,32},{64,48},{80,64},{96,80},{112,96},{128,112},... | collective-permute-start | bytes 1572872 | tf_op jit(solution)/shard_map/ppermute | solution.py:138
  8.3 6.0 %shard_map.37._ = bf16[16,16,3,16,128]{4,3,2,1,0:T(8,128)(2,1)} custom-call(bf16[16,3,8,32,128]{4,3,2,1,0:T(8,128)(2,1)} %vel_ref.3), custom_call_target="tpu_custom_call" | custom-call | tf_op jit(solution)/shard_map/pallas_call | solution.py:94
  14.3 6.8 %collective-permute-done.low_ref = bf16[16,2,2,32,128]{4,3,2,1,0:T(8,128)(2,1)S(1)} collective-permute-done((bf16[16,2,2,32,128]{4,3,2,1,0:T(8,128)(2,1)S(1)}, bf16[16,2,2,32,128]{4,3,2,1,0:T(8,128)(2,1)S(1)}, u32[]{:S(2)}, u32[]{:S(2)}) %collective-permute-start) | collective-permute-done | bytes 524320 | tf_op jit(solution)/shard_map/ppermute | solution.py:137
  21.1 0.0 copy-start
  21.1 15.2 %collective-permute-done.1.high_ref = bf16[16,2,2,32,128]{4,3,2,1,0:T(8,128)(2,1)S(1)} collective-permute-done((bf16[16,2,2,32,128]{4,3,2,1,0:T(8,128)(2,1)S(1)}, bf16[16,2,2,32,128]{4,3,2,1,0:T(8,128)(2,1)S(1)}, u32[]{:S(2)}, u32[]{:S(2)}) %collective-permute-start.1) | collective-permute-done | bytes 524320 | tf_op jit(solution)/shard_map/ppermute | solution.py:138
  36.3 0.0 copy-done
  36.3 0.0 copy-start.1
  36.3 0.8 copy-done.1
  37.1 4.0 %shard_map.38 = bf16[16,16,3,16,128]{4,3,2,1,0:T(8,128)(2,1)} custom-call(bf16[16,3,8,32,128]{4,3,2,1,0:T(8,128)(2,1)} %vel_ref.3, bf16[16,2,2,32,128]{4,3,2,1,0:T(8,128)(2,1)} %copy-done, bf16[16,2,2,32,128]{4,3,2,1,0:T(8,128)(2,1)} %copy-done.1, bf16[16,16,3,16,128]{4,3,2,1,0:T(8,128)(2,1)} %shard_map.37._), custom_call_target="tpu_custom_call", output_to_operand_aliasing={{}: (3, {})} | custom-call | tf_op jit(solution)/shard_map/pallas_call | solution.py:94
  41.1 0.0 copy-start.3
  41.1 0.0 copy-start.2
  41.1 5.6 %all-to-all-start = ((bf16[16,16,3,16,128]{4,3,2,1,0:T(8,128)(2,1)}), bf16[16,16,3,16,128]{4,3,2,1,0:T(8,128)(2,1)S(1)}, u32[]{:S(2)}, u32[]{:S(2)}) async-start(bf16[16,16,3,16,128]{4,3,2,1,0:T(8,128)(2,1)} %shard_map.38), calls=%async_computation | async-start | bytes 6291456 | tf_op jit(solution)/shard_map/all_to_all | solution.py:110
  46.7 0.0 copy-done.3
  46.7 0.1 select_reduce_fusion
  46.8 0.0 copy-done.2
  46.8 0.1 convert_reduce_fusion
  46.9 37.9 %all-to-all-done = bf16[16,16,3,16,128]{4,3,2,1,0:T(8,128)(2,1)S(1)} async-done(((bf16[16,16,3,16,128]{4,3,2,1,0:T(8,128)(2,1)}), bf16[16,16,3,16,128]{4,3,2,1,0:T(8,128)(2,1)S(1)}, u32[]{:S(2)}, u32[]{:S(2)}) %all-to-all-start) | async-done | bytes 3145760 | tf_op jit(solution)/shard_map/all_to_all | solution.py:110
  84.9 0.6 fusion.4
  85.4 2.7 %fusion.10 = f32[256,48,128]{2,0,1:T(8,128)S(1)} fusion(f32[24,48,128]{2,0,1:T(8,128)S(1)} %fusion.4, s32[256]{0:T(256)S(1)} %copy-done.2), kind=kOutput, calls=%fused_computation.13 | convolution fusion | flops 452990976 | bytes 6882304 | tf_op jit(solution)/shard_map/sb,bkz->skz/dot_general | solution.py:120
  88.1 2.2 %fusion.8 = f32[256,256]{1,0:T(8,128)} fusion(f32[256,48,128]{2,0,1:T(8,128)S(1)} %fusion.10, bf16[256,48,128]{2,1,0:T(8,128)(2,1)S(1)} %bitcast.25), kind=kOutput, calls=%fused_computation.8 | convolution fusion | flops 810090496 | bytes 9699328 | tf_op jit(solution)/shard_map/skz,tkz->st/dot_general | solution.py:128
  90.3 4.3 %all-to-all-start.1 = ((f32[16,16,256]{2,1,0:T(8,128)}), f32[16,16,256]{2,1,0:T(8,128)S(1)}, u32[]{:S(2)}, u32[]{:S(2)}) async-start(f32[16,16,256]{2,1,0:T(8,128)} %bitcast.3), calls=%async_computation.1 | async-start | bytes 524288 | tf_op jit(solution)/shard_map/all_to_all | solution.py:105
  94.6 7.2 %all-to-all-done.1 = f32[16,16,256]{2,1,0:T(8,128)S(1)} async-done(((f32[16,16,256]{2,1,0:T(8,128)}), f32[16,16,256]{2,1,0:T(8,128)S(1)}, u32[]{:S(2)}, u32[]{:S(2)}) %all-to-all-start.1) | async-done | bytes 262176 | tf_op jit(solution)/shard_map/all_to_all | solution.py:105
  101.9 0.1 reshape.32
  102.0 0.6 gather_fusion
  102.6 0.1 fusion.17
  102.7 0.1 reshape.43
  102.8 16.0 %all_to_all.15 = f32[16,1,256]{2,1,0:T(1,128)S(1)} all-to-all(f32[16,1,256]{2,1,0:T(1,128)S(1)} %reshape.43), channel_id=1, replica_groups=mesh['space'=16,'snap'=16] {'space'}, dimensions={0} | all-to-all | bytes 32768 | tf_op jit(solution)/shard_map/all_to_all | solution.py:105
  118.8 0.5 broadcast.59
  119.4 0.7 reduce
  120.0 0.1 reshape.44
  120.2 0.7 copy.17
  (6 shorter events, 0.1 us)
Async XLA Ops:
  1.3 19.8 %collective-permute-start = (bf16[16,2,2,32,128]{4,3,2,1,0:T(8,128)(2,1)S(1)}, bf16[16,2,2,32,128]{4,3,2,1,0:T(8,128)(2,1)S(1)}, u32[]{:S(2)}, u32[]{:S(2)}) collective-permute-start(bf16[16,2,2,32,128]{4,3,2,1,0:T(8,128)(2,1)S(1)} %get-tuple-element.6), channel_id=1, source_target_pairs={{0,16},{16,32},{32,48},{48,64},{64,80},{80,96},{96,112},{112,128},... | collective-permute-start | bytes 1572872 | tf_op jit(solution)/shard_map/ppermute | solution.py:137
  7.0 29.2 %collective-permute-start.1 = (bf16[16,2,2,32,128]{4,3,2,1,0:T(8,128)(2,1)S(1)}, bf16[16,2,2,32,128]{4,3,2,1,0:T(8,128)(2,1)S(1)}, u32[]{:S(2)}, u32[]{:S(2)}) collective-permute-start(bf16[16,2,2,32,128]{4,3,2,1,0:T(8,128)(2,1)S(1)} %get-tuple-element.5), channel_id=1, source_target_pairs={{16,0},{32,16},{48,32},{64,48},{80,64},{96,80},{112,96},{128,112},... | collective-permute-start | bytes 1572872 | tf_op jit(solution)/shard_map/ppermute | solution.py:138
  21.1 15.2 %copy-start = (bf16[16,2,2,32,128]{4,3,2,1,0:T(8,128)(2,1)}, bf16[16,2,2,32,128]{4,3,2,1,0:T(8,128)(2,1)S(1)}, u32[]{:S(2)}) copy-start(bf16[16,2,2,32,128]{4,3,2,1,0:T(8,128)(2,1)S(1)} %collective-permute-done.low_ref) | copy-start | bytes 1572868
  36.3 0.8 copy-start.1
  41.1 5.6 %copy-start.3 = (s32[16]{0:T(128)S(1)}, s32[16]{0:T(128)}, u32[]{:S(2)}) copy-start(s32[16]{0:T(128)} %param.5) | copy-start | bytes 196
  41.1 5.7 %copy-start.2 = (s32[256]{0:T(256)S(1)}, s32[256]{0:T(256)}, u32[]{:S(2)}) copy-start(s32[256]{0:T(256)} %param.4) | copy-start | bytes 3076
  41.1 43.7 %all-to-all-start = ((bf16[16,16,3,16,128]{4,3,2,1,0:T(8,128)(2,1)}), bf16[16,16,3,16,128]{4,3,2,1,0:T(8,128)(2,1)S(1)}, u32[]{:S(2)}, u32[]{:S(2)}) async-start(bf16[16,16,3,16,128]{4,3,2,1,0:T(8,128)(2,1)} %shard_map.38), calls=%async_computation | async-start | bytes 6291456 | tf_op jit(solution)/shard_map/all_to_all | solution.py:110
  90.3 11.5 %all-to-all-start.1 = ((f32[16,16,256]{2,1,0:T(8,128)}), f32[16,16,256]{2,1,0:T(8,128)S(1)}, u32[]{:S(2)}, u32[]{:S(2)}) async-start(f32[16,16,256]{2,1,0:T(8,128)} %bitcast.3), calls=%async_computation.1 | async-start | bytes 524288 | tf_op jit(solution)/shard_map/all_to_all | solution.py:105

commit v8 on v5

--- a/solution.py
+++ b/solution.py
@@ -69,7 +69,7 @@
 def curl_call(kernel, comps, velocity, halos, n_snap):
     snaps_dev, _, cells_x, cells_y, cells_z = velocity.shape
     rows = cells_y * cells_x // n_snap
-    block = 4
+    block = 8
     vel_spec = pl.BlockSpec((block,) + velocity.shape[1:], lambda s: (s, 0, 0, 0, 0))
     halo_specs = [pl.BlockSpec((block,) + h.shape[1:], lambda s: (s, 0, 0, 0, 0)) for h in halos]
     return pl.pallas_call(
@@ -105,7 +105,8 @@
         preferred_element_type=jnp.float32,
     )
     fluct = (columns.astype(jnp.float32) - selected).astype(jnp.bfloat16)
-    return jnp.einsum("skz,tkz->st", fluct, fluct, preferred_element_type=jnp.float32)
+    fluct = fluct.reshape(fluct.shape[0], -1)
+    return jnp.einsum("sk,tk->st", fluct, fluct, preferred_element_type=jnp.float32)
 
 
 def body(velocity, phase_bins, tile_owner):

time: 127 us -> 126 us (level)
  no operation moved by 1% of the time
where the time goes in v8:
time: 126 us
  waiting for transfers between devices  58.9 us (47%)
  starting transfers between devices  26.7 us (21%)
  blocking collectives  16.7 us (13%)
  Pallas kernels  10 us (8%)
  matrix products  7.08 us (6%)
  local copies, waits for them, and re-layouts  4.96 us (4%)
    ppermute x1, waiting for transfers between devices, body(): low = lax.ppermute(velocity[:, 1:3, cells_x - 2:], 'space', forward)  26.9 us
    all_to_all x2, waiting for transfers between devices, exchange(): lax.all_to_all(parts, 'snap', split_axis=0, concat_axis=0, tiled=True)  24.8 us
    all_to_all x1, blocking collectives, all_to_all_sum(): got = lax.all_to_all(x, axis, split_axis=0, concat_axis=0, tiled=True)  16.7 us
    all_to_all x2, starting transfers between devices, exchange(): lax.all_to_all(parts, 'snap', split_axis=0, concat_axis=0, tiled=True)  16.2 us
    pallas_call x2, Pallas kernels, curl_call(): pl.pallas_call(kernel, grid=(snaps_dev // block,), in_specs=[vel_spec] +...  10 us
    all_to_all x1, waiting for transfers between devices, all_to_all_sum(): got = lax.all_to_all(x, axis, split_axis=0, concat_axis=0, tiled=True)  7.22 us
    ppermute x1, starting transfers between devices, body(): low = lax.ppermute(velocity[:, 1:3, cells_x - 2:], 'space', forward)  4.93 us
    all_to_all x1, starting transfers between devices, all_to_all_sum(): got = lax.all_to_all(x, axis, split_axis=0, concat_axis=0, tiled=True)  4.29 us
  transfers between devices with their start and end apart: 5, of which 3 were waited for; matrix products, arithmetic and copies ran while one was open for 3% of the time, Pallas kernels for 5%

profile of v8, /device:TPU:1, one launch (start us, length us, event | category | flops | bytes accessed | tf_op | source)
XLA Modules:
  0.0 125.6 jit_solution(13103905309495445391)
XLA Ops:
  0.0 4.4 %shard_map.37 = bf16[16,16,1,16,128]{4,3,2,1,0:T(8,128)(2,1)} custom-call(bf16[16,3,8,32,128]{4,3,2,1,0:T(8,128)(2,1)} %vel_ref.3), custom_call_target="tpu_custom_call" | custom-call | tf_op jit(solution)/shard_map/pallas_call | solution.py:75
  4.4 7.3 %all-to-all-start = ((bf16[16,16,1,16,128]{4,3,2,1,0:T(8,128)(2,1)}), bf16[16,16,1,16,128]{4,3,2,1,0:T(8,128)(2,1)S(1)}, u32[]{:S(2)}, u32[]{:S(2)}) async-start(bf16[16,16,1,16,128]{4,3,2,1,0:T(8,128)(2,1)} %shard_map.37), calls=%async_computation | async-start | bytes 2097152 | tf_op jit(solution)/shard_map/all_to_all | solution.py:90
  11.7 1.3 %fusion.22 = (bf16[16,2,2,32,128]{4,3,2,1,0:T(8,128)(2,1)S(1)}, bf16[16,2,2,32,128]{4,3,2,1,0:T(8,128)(2,1)S(1)}) fusion(bf16[16,3,8,32,128]{4,3,2,1,0:T(8,128)(2,1)} %vel_ref.3), kind=kLoop, calls=%fused_computation.30 | loop fusion | bytes 2097152 | tf_op jit(solution)/shard_map/slice | solution.py:119
  13.0 4.9 %collective-permute-start = (bf16[16,2,2,32,128]{4,3,2,1,0:T(8,128)(2,1)S(1)}, bf16[16,2,2,32,128]{4,3,2,1,0:T(8,128)(2,1)S(1)}, u32[]{:S(2)}, u32[]{:S(2)}) collective-permute-start(bf16[16,2,2,32,128]{4,3,2,1,0:T(8,128)(2,1)S(1)} %get-tuple-element.6), channel_id=1, source_target_pairs={{0,16},{16,32},{32,48},{48,64},{64,80},{80,96},{96,112},{112,128},... | collective-permute-start | bytes 1572872 | tf_op jit(solution)/shard_map/ppermute | solution.py:118
  17.9 1.3 %collective-permute-start.1 = (bf16[16,2,2,32,128]{4,3,2,1,0:T(8,128)(2,1)S(1)}, bf16[16,2,2,32,128]{4,3,2,1,0:T(8,128)(2,1)S(1)}, u32[]{:S(2)}, u32[]{:S(2)}) collective-permute-start(bf16[16,2,2,32,128]{4,3,2,1,0:T(8,128)(2,1)S(1)} %get-tuple-element.5), channel_id=1, source_target_pairs={{16,0},{32,16},{48,32},{64,48},{80,64},{96,80},{112,96},{128,112},... | collective-permute-start | bytes 1572872 | tf_op jit(solution)/shard_map/ppermute | solution.py:119
  19.2 26.9 %collective-permute-done.low_ref = bf16[16,2,2,32,128]{4,3,2,1,0:T(8,128)(2,1)S(1)} collective-permute-done((bf16[16,2,2,32,128]{4,3,2,1,0:T(8,128)(2,1)S(1)}, bf16[16,2,2,32,128]{4,3,2,1,0:T(8,128)(2,1)S(1)}, u32[]{:S(2)}, u32[]{:S(2)}) %collective-permute-start) | collective-permute-done | bytes 524320 | tf_op jit(solution)/shard_map/ppermute | solution.py:118
  46.1 0.0 copy-start
  46.1 0.0 collective-permute-done.1.high_ref
  46.1 0.8 copy-done
  46.9 0.0 copy-start.1
  46.9 0.8 copy-done.1
  47.7 5.7 %shard_map.38 = bf16[16,16,2,16,128]{4,3,2,1,0:T(8,128)(2,1)} custom-call(bf16[16,3,8,32,128]{4,3,2,1,0:T(8,128)(2,1)} %vel_ref.3, bf16[16,2,2,32,128]{4,3,2,1,0:T(8,128)(2,1)} %copy-done, bf16[16,2,2,32,128]{4,3,2,1,0:T(8,128)(2,1)} %copy-done.1), custom_call_target="tpu_custom_call" | custom-call | tf_op jit(solution)/shard_map/pallas_call | solution.py:75
  53.4 0.0 copy-start.3
  53.4 0.0 copy-start.2
  53.4 0.0 all-to-all-done
  53.4 8.8 %all-to-all-start.1 = ((bf16[16,16,2,16,128]{4,3,2,1,0:T(8,128)(2,1)}), bf16[16,16,2,16,128]{4,3,2,1,0:T(8,128)(2,1)S(1)}, u32[]{:S(2)}, u32[]{:S(2)}) async-start(bf16[16,16,2,16,128]{4,3,2,1,0:T(8,128)(2,1)} %shard_map.38), calls=%async_computation.1 | async-start | bytes 4194304 | tf_op jit(solution)/shard_map/all_to_all | solution.py:90
  62.2 0.0 copy-done.3
  62.2 0.1 select_reduce_fusion
  62.4 0.0 copy-done.2
  62.4 0.1 convert_reduce_fusion
  62.5 0.3 convolution_divide_fusion
  62.8 1.1 subtract_convert_fusion.2
  63.9 0.5 convolution_bitcast_fusion
  64.4 24.8 %all-to-all-done.1 = bf16[16,16,2,16,128]{4,3,2,1,0:T(8,128)(2,1)S(1)} async-done(((bf16[16,16,2,16,128]{4,3,2,1,0:T(8,128)(2,1)}), bf16[16,16,2,16,128]{4,3,2,1,0:T(8,128)(2,1)S(1)}, u32[]{:S(2)}, u32[]{:S(2)}) %all-to-all-start.1) | async-done | bytes 2097184 | tf_op jit(solution)/shard_map/all_to_all | solution.py:90
  89.2 0.7 fusion.4
  89.9 1.8 %fusion.12 = f32[256,32,128]{2,0,1:T(8,128)S(1)} fusion(f32[24,32,128]{2,0,1:T(8,128)S(1)} %fusion.4, s32[256]{0:T(256)S(1)} %copy-done.2), kind=kOutput, calls=%fused_computation.18 | convolution fusion | flops 301996032 | bytes 4588544 | tf_op jit(solution)/shard_map/sb,bkz->skz/dot_general | solution.py:100
  91.7 2.7 %fusion.9 = f32[256,256]{1,0:T(8,128)} fusion(f32[256,256]{1,0:T(8,128)S(1)} %convolution_bitcast_fusion, f32[256,32,128]{2,0,1:T(8,128)S(1)} %fusion.12, bf16[256,32,128]{2,1,0:T(8,128)(2,1)S(1)} %bitcast.35), kind=kOutput, calls=%fused_computation.11 | convolution fusion | flops 540147712 | bytes 6815744 | tf_op jit(solution)/shard_map/sk,tk->st/dot_general | solution.py:109
  94.4 4.3 %all-to-all-start.2 = ((f32[16,16,256]{2,1,0:T(8,128)}), f32[16,16,256]{2,1,0:T(8,128)S(1)}, u32[]{:S(2)}, u32[]{:S(2)}) async-start(f32[16,16,256]{2,1,0:T(8,128)} %bitcast.5), calls=%async_computation.2 | async-start | bytes 524288 | tf_op jit(solution)/shard_map/all_to_all | solution.py:85
  98.7 7.2 %all-to-all-done.2 = f32[16,16,256]{2,1,0:T(8,128)S(1)} async-done(((f32[16,16,256]{2,1,0:T(8,128)}), f32[16,16,256]{2,1,0:T(8,128)S(1)}, u32[]{:S(2)}, u32[]{:S(2)}) %all-to-all-start.2) | async-done | bytes 262176 | tf_op jit(solution)/shard_map/all_to_all | solution.py:85
  106.0 0.1 reshape.38
  106.1 0.6 gather_fusion
  106.7 0.1 fusion.23
  106.8 0.1 reshape.50
  106.9 16.7 %all_to_all.20 = f32[16,1,256]{2,1,0:T(1,128)S(1)} all-to-all(f32[16,1,256]{2,1,0:T(1,128)S(1)} %reshape.50), channel_id=1, replica_groups=mesh['space'=16,'snap'=16] {'space'}, dimensions={0} | all-to-all | bytes 32768 | tf_op jit(solution)/shard_map/all_to_all | solution.py:85
  123.6 0.5 broadcast.59
  124.1 0.7 reduce
  124.8 0.1 reshape.51
  124.9 0.7 copy.24
  (6 shorter events, 0.1 us)
Async XLA Ops:
  4.4 49.0 %all-to-all-start = ((bf16[16,16,1,16,128]{4,3,2,1,0:T(8,128)(2,1)}), bf16[16,16,1,16,128]{4,3,2,1,0:T(8,128)(2,1)S(1)}, u32[]{:S(2)}, u32[]{:S(2)}) async-start(bf16[16,16,1,16,128]{4,3,2,1,0:T(8,128)(2,1)} %shard_map.37), calls=%async_computation | async-start | bytes 2097152 | tf_op jit(solution)/shard_map/all_to_all | solution.py:90
  13.0 33.1 %collective-permute-start = (bf16[16,2,2,32,128]{4,3,2,1,0:T(8,128)(2,1)S(1)}, bf16[16,2,2,32,128]{4,3,2,1,0:T(8,128)(2,1)S(1)}, u32[]{:S(2)}, u32[]{:S(2)}) collective-permute-start(bf16[16,2,2,32,128]{4,3,2,1,0:T(8,128)(2,1)S(1)} %get-tuple-element.6), channel_id=1, source_target_pairs={{0,16},{16,32},{32,48},{48,64},{64,80},{80,96},{96,112},{112,128},... | collective-permute-start | bytes 1572872 | tf_op jit(solution)/shard_map/ppermute | solution.py:118
  17.9 28.2 %collective-permute-start.1 = (bf16[16,2,2,32,128]{4,3,2,1,0:T(8,128)(2,1)S(1)}, bf16[16,2,2,32,128]{4,3,2,1,0:T(8,128)(2,1)S(1)}, u32[]{:S(2)}, u32[]{:S(2)}) collective-permute-start(bf16[16,2,2,32,128]{4,3,2,1,0:T(8,128)(2,1)S(1)} %get-tuple-element.5), channel_id=1, source_target_pairs={{16,0},{32,16},{48,32},{64,48},{80,64},{96,80},{112,96},{128,112},... | collective-permute-start | bytes 1572872 | tf_op jit(solution)/shard_map/ppermute | solution.py:119
  46.1 0.8 copy-start
  46.9 0.8 copy-start.1
  53.4 8.9 %copy-start.3 = (s32[16]{0:T(128)S(1)}, s32[16]{0:T(128)}, u32[]{:S(2)}) copy-start(s32[16]{0:T(128)} %param.5) | copy-start | bytes 196
  53.4 9.0 %copy-start.2 = (s32[256]{0:T(256)S(1)}, s32[256]{0:T(256)}, u32[]{:S(2)}) copy-start(s32[256]{0:T(256)} %param.4) | copy-start | bytes 3076
  53.4 35.8 %all-to-all-start.1 = ((bf16[16,16,2,16,128]{4,3,2,1,0:T(8,128)(2,1)}), bf16[16,16,2,16,128]{4,3,2,1,0:T(8,128)(2,1)S(1)}, u32[]{:S(2)}, u32[]{:S(2)}) async-start(bf16[16,16,2,16,128]{4,3,2,1,0:T(8,128)(2,1)} %shard_map.38), calls=%async_computation.1 | async-start | bytes 4194304 | tf_op jit(solution)/shard_map/all_to_all | solution.py:90
  94.4 11.5 %all-to-all-start.2 = ((f32[16,16,256]{2,1,0:T(8,128)}), f32[16,16,256]{2,1,0:T(8,128)S(1)}, u32[]{:S(2)}, u32[]{:S(2)}) async-start(f32[16,16,256]{2,1,0:T(8,128)} %bitcast.5), calls=%async_computation.2 | async-start | bytes 524288 | tf_op jit(solution)/shard_map/all_to_all | solution.py:85

commit v9 on v5

--- a/solution.py
+++ b/solution.py
@@ -69,7 +69,7 @@
 def curl_call(kernel, comps, velocity, halos, n_snap):
     snaps_dev, _, cells_x, cells_y, cells_z = velocity.shape
     rows = cells_y * cells_x // n_snap
-    block = 4
+    block = 8
     vel_spec = pl.BlockSpec((block,) + velocity.shape[1:], lambda s: (s, 0, 0, 0, 0))
     halo_specs = [pl.BlockSpec((block,) + h.shape[1:], lambda s: (s, 0, 0, 0, 0)) for h in halos]
     return pl.pallas_call(
@@ -133,11 +133,11 @@
     col_sum = all_to_all_sum(row_blocks, "snap")
     tile_count = lax.axis_size("space")
     tile_ids = jnp.arange(tile_count, dtype=jnp.int32)
-    inverse = jnp.sum(
-        tile_ids[None, :] * (tile_owner[None, :] == tile_ids[:, None]).astype(jnp.int32), axis=1
+    owned = (tile_owner[None, :] == tile_ids[:, None]).astype(jnp.float32)
+    tiles = col_sum.reshape(col_sum.shape[0], tile_count, total_snaps // tile_count)
+    tiles = jnp.einsum(
+        "kt,atr->kra", owned, tiles, precision=lax.Precision.HIGHEST, preferred_element_type=jnp.float32
     )
-    tiles = col_sum.reshape(col_sum.shape[0], tile_count, total_snaps // tile_count)
-    tiles = jnp.transpose(jnp.take(tiles, inverse, axis=1), (1, 2, 0))
     mine = all_to_all_sum(tiles, "space")
     return mine[None]
 

time: 127 us -> 124 us (0.976)
  blocking collectives: 16.7 us -> 27.7 us
  waiting for transfers between devices: 59 us -> 51.8 us
  starting transfers between devices: 26.7 us -> 22.4 us
    all_to_all x1 -> x2, blocking collectives: 16.7 us -> 27.7 us  [all_to_all_sum(): got = lax.all_to_all(x, axis, split_axis=0, concat_axis=0, tiled=True)]
    all_to_all x1 -> x0, waiting for transfers between devices: 7.22 us -> none  [all_to_all_sum(): got = lax.all_to_all(x, axis, split_axis=0, concat_axis=0, tiled=True)]
    all_to_all x1 -> x0, starting transfers between devices: 4.29 us -> none  [all_to_all_sum(): got = lax.all_to_all(x, axis, split_axis=0, concat_axis=0, tiled=True)]
  transfers between devices with their start and end apart: 5 -> 4, of which waited for: 3 -> 2; matrix products, arithmetic and copies ran while one was open for 3% -> 3% of each run, Pallas kernels for 5% -> 5%
where the time goes in v9:
time: 124 us
  waiting for transfers between devices  51.8 us (42%)
  blocking collectives  27.7 us (22%)
  starting transfers between devices  22.4 us (18%)
  Pallas kernels  10 us (8%)
  matrix products  6.67 us (5%)
  local copies, waits for them, and re-layouts  4.47 us (4%)
    all_to_all x2, blocking collectives, all_to_all_sum(): got = lax.all_to_all(x, axis, split_axis=0, concat_axis=0, tiled=True)  27.7 us
    ppermute x1, waiting for transfers between devices, body(): low = lax.ppermute(velocity[:, 1:3, cells_x - 2:], 'space', forward)  26.9 us
    all_to_all x2, waiting for transfers between devices, exchange(): lax.all_to_all(parts, 'snap', split_axis=0, concat_axis=0, tiled=True)  24.9 us
    all_to_all x2, starting transfers between devices, exchange(): lax.all_to_all(parts, 'snap', split_axis=0, concat_axis=0, tiled=True)  16.2 us
    pallas_call x2, Pallas kernels, curl_call(): pl.pallas_call(kernel, grid=(snaps_dev // block,), in_specs=[vel_spec] +...  10 us
    ppermute x1, starting transfers between devices, body(): low = lax.ppermute(velocity[:, 1:3, cells_x - 2:], 'space', forward)  4.93 us
    dot_general x2, matrix products, fluctuation_of(): jnp.einsum('sb,bkz->skz', onehot.T.astype(jnp.float32), bin_means, precis...  2.98 us
  transfers between devices with their start and end apart: 4, of which 2 were waited for; matrix products, arithmetic and copies ran while one was open for 3% of the time, Pallas kernels for 5%

profile of v9, /device:TPU:1, one launch (start us, length us, event | category | flops | bytes accessed | tf_op | source)
XLA Modules:
  0.0 124.0 jit_solution(8787149286285352307)
XLA Ops:
  0.0 4.4 %shard_map.37 = bf16[16,16,1,16,128]{4,3,2,1,0:T(8,128)(2,1)} custom-call(bf16[16,3,8,32,128]{4,3,2,1,0:T(8,128)(2,1)} %vel_ref.3), custom_call_target="tpu_custom_call" | custom-call | tf_op jit(solution)/shard_map/pallas_call | solution.py:75
  4.4 7.3 %all-to-all-start = ((bf16[16,16,1,16,128]{4,3,2,1,0:T(8,128)(2,1)}), bf16[16,16,1,16,128]{4,3,2,1,0:T(8,128)(2,1)S(1)}, u32[]{:S(2)}, u32[]{:S(2)}) async-start(bf16[16,16,1,16,128]{4,3,2,1,0:T(8,128)(2,1)} %shard_map.37), calls=%async_computation | async-start | bytes 2097152 | tf_op jit(solution)/shard_map/all_to_all | solution.py:90
  11.7 1.3 %fusion.24 = (bf16[16,2,2,32,128]{4,3,2,1,0:T(8,128)(2,1)S(1)}, bf16[16,2,2,32,128]{4,3,2,1,0:T(8,128)(2,1)S(1)}) fusion(bf16[16,3,8,32,128]{4,3,2,1,0:T(8,128)(2,1)} %vel_ref.3), kind=kLoop, calls=%fused_computation.25 | loop fusion | bytes 2097152 | tf_op jit(solution)/shard_map/slice | solution.py:118
  13.0 4.9 %collective-permute-start = (bf16[16,2,2,32,128]{4,3,2,1,0:T(8,128)(2,1)S(1)}, bf16[16,2,2,32,128]{4,3,2,1,0:T(8,128)(2,1)S(1)}, u32[]{:S(2)}, u32[]{:S(2)}) collective-permute-start(bf16[16,2,2,32,128]{4,3,2,1,0:T(8,128)(2,1)S(1)} %get-tuple-element.6), channel_id=1, source_target_pairs={{0,16},{16,32},{32,48},{48,64},{64,80},{80,96},{96,112},{112,128},... | collective-permute-start | bytes 1572872 | tf_op jit(solution)/shard_map/ppermute | solution.py:117
  17.9 1.3 %collective-permute-start.1 = (bf16[16,2,2,32,128]{4,3,2,1,0:T(8,128)(2,1)S(1)}, bf16[16,2,2,32,128]{4,3,2,1,0:T(8,128)(2,1)S(1)}, u32[]{:S(2)}, u32[]{:S(2)}) collective-permute-start(bf16[16,2,2,32,128]{4,3,2,1,0:T(8,128)(2,1)S(1)} %get-tuple-element.5), channel_id=1, source_target_pairs={{16,0},{32,16},{48,32},{64,48},{80,64},{96,80},{112,96},{128,112},... | collective-permute-start | bytes 1572872 | tf_op jit(solution)/shard_map/ppermute | solution.py:118
  19.2 26.9 %collective-permute-done.low_ref = bf16[16,2,2,32,128]{4,3,2,1,0:T(8,128)(2,1)S(1)} collective-permute-done((bf16[16,2,2,32,128]{4,3,2,1,0:T(8,128)(2,1)S(1)}, bf16[16,2,2,32,128]{4,3,2,1,0:T(8,128)(2,1)S(1)}, u32[]{:S(2)}, u32[]{:S(2)}) %collective-permute-start) | collective-permute-done | bytes 524320 | tf_op jit(solution)/shard_map/ppermute | solution.py:117
  46.1 0.0 copy-start
  46.1 0.0 collective-permute-done.1.high_ref
  46.1 0.8 copy-done
  46.9 0.0 copy-start.1
  46.9 0.8 copy-done.1
  47.7 5.7 %shard_map.38 = bf16[16,16,2,16,128]{4,3,2,1,0:T(8,128)(2,1)} custom-call(bf16[16,3,8,32,128]{4,3,2,1,0:T(8,128)(2,1)} %vel_ref.3, bf16[16,2,2,32,128]{4,3,2,1,0:T(8,128)(2,1)} %copy-done, bf16[16,2,2,32,128]{4,3,2,1,0:T(8,128)(2,1)} %copy-done.1), custom_call_target="tpu_custom_call" | custom-call | tf_op jit(solution)/shard_map/pallas_call | solution.py:75
  53.4 0.0 copy-start.2
  53.4 0.0 all-to-all-done
  53.4 8.8 %all-to-all-start.1 = ((bf16[16,16,2,16,128]{4,3,2,1,0:T(8,128)(2,1)}), bf16[16,16,2,16,128]{4,3,2,1,0:T(8,128)(2,1)S(1)}, u32[]{:S(2)}, u32[]{:S(2)}) async-start(bf16[16,16,2,16,128]{4,3,2,1,0:T(8,128)(2,1)} %shard_map.38), calls=%async_computation.1 | async-start | bytes 4194304 | tf_op jit(solution)/shard_map/all_to_all | solution.py:90
  62.2 0.0 copy-done.2
  62.2 0.1 convert_reduce_fusion
  62.4 0.3 convolution_divide_fusion
  62.6 1.1 subtract_convert_fusion.2
  63.8 0.5 convolution_bitcast_fusion
  64.2 24.9 %all-to-all-done.1 = bf16[16,16,2,16,128]{4,3,2,1,0:T(8,128)(2,1)S(1)} async-done(((bf16[16,16,2,16,128]{4,3,2,1,0:T(8,128)(2,1)}), bf16[16,16,2,16,128]{4,3,2,1,0:T(8,128)(2,1)S(1)}, u32[]{:S(2)}, u32[]{:S(2)}) %all-to-all-start.1) | async-done | bytes 2097184 | tf_op jit(solution)/shard_map/all_to_all | solution.py:90
  89.2 0.7 fusion.4
  89.9 1.8 %fusion.12 = f32[256,32,128]{2,0,1:T(8,128)S(1)} fusion(f32[24,32,128]{2,0,1:T(8,128)S(1)} %fusion.4, s32[256]{0:T(256)S(1)} %copy-done.2), kind=kOutput, calls=%fused_computation.17 | convolution fusion | flops 301996032 | bytes 4588544 | tf_op jit(solution)/shard_map/sb,bkz->skz/dot_general | solution.py:100
  91.7 0.0 copy-start.3
  91.7 2.0 %fusion.9 = f32[256,256]{1,0:T(8,128)S(1)} fusion(f32[256,256]{1,0:T(8,128)S(1)} %convolution_bitcast_fusion, f32[256,32,128]{2,0,1:T(8,128)S(1)} %fusion.12, bf16[256,32,128]{2,1,0:T(8,128)(2,1)S(1)} %bitcast.32), kind=kOutput, calls=%fused_computation.10 | convolution fusion | flops 540147712 | bytes 6815744 | tf_op jit(solution)/shard_map/skz,tkz->st/dot_general | solution.py:108
  93.7 11.0 %all_to_all.20 = f32[16,16,256]{2,1,0:T(8,128)S(1)} all-to-all(f32[16,16,256]{2,1,0:T(8,128)S(1)} %bitcast.35), channel_id=1, replica_groups=mesh['space'=16,'snap'=16] {'snap'}, dimensions={0} | all-to-all | bytes 524288 | tf_op jit(solution)/shard_map/all_to_all | solution.py:85
  104.7 0.1 reshape.18
  104.8 0.0 copy-done.3
  104.8 0.3 convolution_bitcast_fusion.1
  105.1 0.1 copy.14
  105.2 0.1 reshape.23
  105.3 16.7 %all_to_all.21 = f32[16,1,256]{2,1,0:T(1,128)S(1)} all-to-all(f32[16,1,256]{2,1,0:T(1,128)S(1)} %reshape.23), channel_id=1, replica_groups=mesh['space'=16,'snap'=16] {'space'}, dimensions={0} | all-to-all | bytes 32768 | tf_op jit(solution)/shard_map/all_to_all | solution.py:85
  122.0 0.5 broadcast.4
  122.6 0.7 reduce
  123.2 0.1 reshape.24
  123.4 0.7 copy.16
  (2 shorter events, 0.0 us)
Async XLA Ops:
  4.4 49.0 %all-to-all-start = ((bf16[16,16,1,16,128]{4,3,2,1,0:T(8,128)(2,1)}), bf16[16,16,1,16,128]{4,3,2,1,0:T(8,128)(2,1)S(1)}, u32[]{:S(2)}, u32[]{:S(2)}) async-start(bf16[16,16,1,16,128]{4,3,2,1,0:T(8,128)(2,1)} %shard_map.37), calls=%async_computation | async-start | bytes 2097152 | tf_op jit(solution)/shard_map/all_to_all | solution.py:90
  13.0 33.1 %collective-permute-start = (bf16[16,2,2,32,128]{4,3,2,1,0:T(8,128)(2,1)S(1)}, bf16[16,2,2,32,128]{4,3,2,1,0:T(8,128)(2,1)S(1)}, u32[]{:S(2)}, u32[]{:S(2)}) collective-permute-start(bf16[16,2,2,32,128]{4,3,2,1,0:T(8,128)(2,1)S(1)} %get-tuple-element.6), channel_id=1, source_target_pairs={{0,16},{16,32},{32,48},{48,64},{64,80},{80,96},{96,112},{112,128},... | collective-permute-start | bytes 1572872 | tf_op jit(solution)/shard_map/ppermute | solution.py:117
  17.9 28.2 %collective-permute-start.1 = (bf16[16,2,2,32,128]{4,3,2,1,0:T(8,128)(2,1)S(1)}, bf16[16,2,2,32,128]{4,3,2,1,0:T(8,128)(2,1)S(1)}, u32[]{:S(2)}, u32[]{:S(2)}) collective-permute-start(bf16[16,2,2,32,128]{4,3,2,1,0:T(8,128)(2,1)S(1)} %get-tuple-element.5), channel_id=1, source_target_pairs={{16,0},{32,16},{48,32},{64,48},{80,64},{96,80},{112,96},{128,112},... | collective-permute-start | bytes 1572872 | tf_op jit(solution)/shard_map/ppermute | solution.py:118
  46.1 0.8 copy-start
  46.9 0.8 copy-start.1
  53.4 8.8 %copy-start.2 = (s32[256]{0:T(256)S(1)}, s32[256]{0:T(256)}, u32[]{:S(2)}) copy-start(s32[256]{0:T(256)} %param.4) | copy-start | bytes 3076
  53.4 35.8 %all-to-all-start.1 = ((bf16[16,16,2,16,128]{4,3,2,1,0:T(8,128)(2,1)}), bf16[16,16,2,16,128]{4,3,2,1,0:T(8,128)(2,1)S(1)}, u32[]{:S(2)}, u32[]{:S(2)}) async-start(bf16[16,16,2,16,128]{4,3,2,1,0:T(8,128)(2,1)} %shard_map.38), calls=%async_computation.1 | async-start | bytes 4194304 | tf_op jit(solution)/shard_map/all_to_all | solution.py:90
  91.7 13.1 %copy-start.3 = (s32[16]{0:T(128)S(1)}, s32[16]{0:T(128)}, u32[]{:S(2)}) copy-start(s32[16]{0:T(128)} %param.5) | copy-start | bytes 196

commit v10 on v9

--- a/solution.py
+++ b/solution.py
@@ -138,8 +138,9 @@
     tiles = jnp.einsum(
         "kt,atr->kra", owned, tiles, precision=lax.Precision.HIGHEST, preferred_element_type=jnp.float32
     )
-    mine = all_to_all_sum(tiles, "space")
-    return mine[None]
+    lanes = 128
+    mine = all_to_all_sum(tiles.reshape(tile_count, -1, lanes), "space")
+    return mine.reshape(1, total_snaps // tile_count, -1)
 
 
 def solution(mesh):

time: 124 us -> 124 us (level)
  starting transfers between devices: 22.4 us -> 24.3 us
  local copies, waits for them, and re-layouts: 4.47 us -> 3.09 us
    ppermute x1, waiting for transfers between devices: 26.9 us -> 16.2 us  [body(): low = lax.ppermute(velocity[:, 1:3, cells_x - 2:], 'space', forward)]
    ppermute x1, waiting for transfers between devices: 0.01 us -> 10.3 us  [body(): high = lax.ppermute(velocity[:, 1:3, :2], 'space', backward)]
    all_to_all x2, starting transfers between devices: 16.2 us -> 17.5 us  [exchange(): lax.all_to_all(parts, 'snap', split_axis=0, concat_axis=0, tiled=True)]
  transfers between devices with their start and end apart: 4 -> 4, of which waited for: 2 -> 3; matrix products, arithmetic and copies ran while one was open for 3% -> 3% of each run, Pallas kernels for 5% -> 5%
where the time goes in v10:
time: 124 us; the launch traced here: 123 us
  waiting for transfers between devices  51.4 us (41%)
  blocking collectives  27.7 us (22%)
  starting transfers between devices  24.3 us (20%)
  Pallas kernels  10 us (8%)
  matrix products  6.67 us (5%)
  local copies, waits for them, and re-layouts  3.09 us (2%)
    all_to_all x2, blocking collectives, all_to_all_sum(): got = lax.all_to_all(x, axis, split_axis=0, concat_axis=0, tiled=True)  27.7 us
    all_to_all x2, waiting for transfers between devices, exchange(): lax.all_to_all(parts, 'snap', split_axis=0, concat_axis=0, tiled=True)  24.9 us
    all_to_all x2, starting transfers between devices, exchange(): lax.all_to_all(parts, 'snap', split_axis=0, concat_axis=0, tiled=True)  17.5 us
    ppermute x1, waiting for transfers between devices, body(): low = lax.ppermute(velocity[:, 1:3, cells_x - 2:], 'space', forward)  16.2 us
    ppermute x1, waiting for transfers between devices, body(): high = lax.ppermute(velocity[:, 1:3, :2], 'space', backward)  10.3 us
    pallas_call x2, Pallas kernels, curl_call(): pl.pallas_call(kernel, grid=(snaps_dev // block,), in_specs=[vel_spec] +...  10 us
    ppermute x1, starting transfers between devices, body(): low = lax.ppermute(velocity[:, 1:3, cells_x - 2:], 'space', forward)  5.56 us
    dot_general x2, matrix products, fluctuation_of(): jnp.einsum('sb,bkz->skz', onehot.T.astype(jnp.float32), bin_means, precis...  2.98 us
  transfers between devices with their start and end apart: 4, of which 3 were waited for; matrix products, arithmetic and copies ran while one was open for 3% of the time, Pallas kernels for 5%

profile of v10, /device:TPU:1, one launch (start us, length us, event | category | flops | bytes accessed | tf_op | source)
XLA Modules:
  0.0 123.5 jit_solution(12589142718225180526)
XLA Ops:
  0.0 4.4 %shard_map.37 = bf16[16,16,1,16,128]{4,3,2,1,0:T(8,128)(2,1)} custom-call(bf16[16,3,8,32,128]{4,3,2,1,0:T(8,128)(2,1)} %vel_ref.3), custom_call_target="tpu_custom_call" | custom-call | tf_op jit(solution)/shard_map/pallas_call | solution.py:75
  4.4 7.3 %all-to-all-start = ((bf16[16,16,1,16,128]{4,3,2,1,0:T(8,128)(2,1)}), bf16[16,16,1,16,128]{4,3,2,1,0:T(8,128)(2,1)S(1)}, u32[]{:S(2)}, u32[]{:S(2)}) async-start(bf16[16,16,1,16,128]{4,3,2,1,0:T(8,128)(2,1)} %shard_map.37), calls=%async_computation | async-start | bytes 2097152 | tf_op jit(solution)/shard_map/all_to_all | solution.py:90
  11.7 1.3 %fusion.24 = (bf16[16,2,2,32,128]{4,3,2,1,0:T(8,128)(2,1)S(1)}, bf16[16,2,2,32,128]{4,3,2,1,0:T(8,128)(2,1)S(1)}) fusion(bf16[16,3,8,32,128]{4,3,2,1,0:T(8,128)(2,1)} %vel_ref.3), kind=kLoop, calls=%fused_computation.25 | loop fusion | bytes 2097152 | tf_op jit(solution)/shard_map/slice | solution.py:118
  13.0 1.3 %collective-permute-start.1 = (bf16[16,2,2,32,128]{4,3,2,1,0:T(8,128)(2,1)S(1)}, bf16[16,2,2,32,128]{4,3,2,1,0:T(8,128)(2,1)S(1)}, u32[]{:S(2)}, u32[]{:S(2)}) collective-permute-start(bf16[16,2,2,32,128]{4,3,2,1,0:T(8,128)(2,1)S(1)} %get-tuple-element.5), channel_id=1, source_target_pairs={{16,0},{32,16},{48,32},{64,48},{80,64},{96,80},{112,96},{128,112},... | collective-permute-start | bytes 1572872 | tf_op jit(solution)/shard_map/ppermute | solution.py:118
  14.3 5.6 %collective-permute-start = (bf16[16,2,2,32,128]{4,3,2,1,0:T(8,128)(2,1)S(1)}, bf16[16,2,2,32,128]{4,3,2,1,0:T(8,128)(2,1)S(1)}, u32[]{:S(2)}, u32[]{:S(2)}) collective-permute-start(bf16[16,2,2,32,128]{4,3,2,1,0:T(8,128)(2,1)S(1)} %get-tuple-element.6), channel_id=1, source_target_pairs={{0,16},{16,32},{32,48},{48,64},{64,80},{80,96},{96,112},{112,128},... | collective-permute-start | bytes 1572872 | tf_op jit(solution)/shard_map/ppermute | solution.py:117
  19.9 10.3 %collective-permute-done.1.high_ref = bf16[16,2,2,32,128]{4,3,2,1,0:T(8,128)(2,1)S(1)} collective-permute-done((bf16[16,2,2,32,128]{4,3,2,1,0:T(8,128)(2,1)S(1)}, bf16[16,2,2,32,128]{4,3,2,1,0:T(8,128)(2,1)S(1)}, u32[]{:S(2)}, u32[]{:S(2)}) %collective-permute-start.1) | collective-permute-done | bytes 524320 | tf_op jit(solution)/shard_map/ppermute | solution.py:118
  30.1 0.0 copy-start
  30.1 16.2 %collective-permute-done.low_ref = bf16[16,2,2,32,128]{4,3,2,1,0:T(8,128)(2,1)S(1)} collective-permute-done((bf16[16,2,2,32,128]{4,3,2,1,0:T(8,128)(2,1)S(1)}, bf16[16,2,2,32,128]{4,3,2,1,0:T(8,128)(2,1)S(1)}, u32[]{:S(2)}, u32[]{:S(2)}) %collective-permute-start) | collective-permute-done | bytes 524320 | tf_op jit(solution)/shard_map/ppermute | solution.py:117
  46.3 0.0 copy-done
  46.3 0.0 copy-start.1
  46.3 0.8 copy-done.1
  47.1 5.6 %shard_map.38 = bf16[16,16,2,16,128]{4,3,2,1,0:T(8,128)(2,1)} custom-call(bf16[16,3,8,32,128]{4,3,2,1,0:T(8,128)(2,1)} %vel_ref.3, bf16[16,2,2,32,128]{4,3,2,1,0:T(8,128)(2,1)} %copy-done.1, bf16[16,2,2,32,128]{4,3,2,1,0:T(8,128)(2,1)} %copy-done), custom_call_target="tpu_custom_call" | custom-call | tf_op jit(solution)/shard_map/pallas_call | solution.py:75
  52.8 0.0 copy-start.2
  52.8 0.0 all-to-all-done
  52.8 10.2 %all-to-all-start.1 = ((bf16[16,16,2,16,128]{4,3,2,1,0:T(8,128)(2,1)}), bf16[16,16,2,16,128]{4,3,2,1,0:T(8,128)(2,1)S(1)}, u32[]{:S(2)}, u32[]{:S(2)}) async-start(bf16[16,16,2,16,128]{4,3,2,1,0:T(8,128)(2,1)} %shard_map.38), calls=%async_computation.1 | async-start | bytes 4194304 | tf_op jit(solution)/shard_map/all_to_all | solution.py:90
  62.9 0.0 copy-done.2
  62.9 0.1 convert_reduce_fusion
  63.1 0.3 convolution_divide_fusion
  63.3 1.1 subtract_convert_fusion.2
  64.5 0.5 convolution_bitcast_fusion
  64.9 24.9 %all-to-all-done.1 = bf16[16,16,2,16,128]{4,3,2,1,0:T(8,128)(2,1)S(1)} async-done(((bf16[16,16,2,16,128]{4,3,2,1,0:T(8,128)(2,1)}), bf16[16,16,2,16,128]{4,3,2,1,0:T(8,128)(2,1)S(1)}, u32[]{:S(2)}, u32[]{:S(2)}) %all-to-all-start.1) | async-done | bytes 2097184 | tf_op jit(solution)/shard_map/all_to_all | solution.py:90
  89.9 0.7 fusion.4
  90.6 1.8 %fusion.12 = f32[256,32,128]{2,0,1:T(8,128)S(1)} fusion(f32[24,32,128]{2,0,1:T(8,128)S(1)} %fusion.4, s32[256]{0:T(256)S(1)} %copy-done.2), kind=kOutput, calls=%fused_computation.17 | convolution fusion | flops 301996032 | bytes 4588544 | tf_op jit(solution)/shard_map/sb,bkz->skz/dot_general | solution.py:100
  92.4 0.0 copy-start.3
  92.4 2.0 %fusion.9 = f32[256,256]{1,0:T(8,128)S(1)} fusion(f32[256,256]{1,0:T(8,128)S(1)} %convolution_bitcast_fusion, f32[256,32,128]{2,0,1:T(8,128)S(1)} %fusion.12, bf16[256,32,128]{2,1,0:T(8,128)(2,1)S(1)} %bitcast.28), kind=kOutput, calls=%fused_computation.10 | convolution fusion | flops 540147712 | bytes 6815744 | tf_op jit(solution)/shard_map/skz,tkz->st/dot_general | solution.py:108
  94.4 11.0 %all_to_all.20 = f32[16,16,256]{2,1,0:T(8,128)S(1)} all-to-all(f32[16,16,256]{2,1,0:T(8,128)S(1)} %bitcast.31), channel_id=1, replica_groups=mesh['space'=16,'snap'=16] {'snap'}, dimensions={0} | all-to-all | bytes 524288 | tf_op jit(solution)/shard_map/all_to_all | solution.py:85
  105.4 0.1 reshape.24
  105.5 0.0 copy-done.3
  105.5 0.3 convolution_bitcast_fusion.1
  105.8 0.1 copy.15
  105.9 0.1 reshape.25
  106.0 16.7 %all_to_all.21 = f32[16,2,128]{2,1,0:T(2,128)S(1)} all-to-all(f32[16,2,128]{2,1,0:T(2,128)S(1)} %reshape.25), channel_id=1, replica_groups=mesh['space'=16,'snap'=16] {'space'}, dimensions={0} | all-to-all | bytes 32768 | tf_op jit(solution)/shard_map/all_to_all | solution.py:85
  122.8 0.7 reshape.26
  (2 shorter events, 0.0 us)
Async XLA Ops:
  4.4 48.4 %all-to-all-start = ((bf16[16,16,1,16,128]{4,3,2,1,0:T(8,128)(2,1)}), bf16[16,16,1,16,128]{4,3,2,1,0:T(8,128)(2,1)S(1)}, u32[]{:S(2)}, u32[]{:S(2)}) async-start(bf16[16,16,1,16,128]{4,3,2,1,0:T(8,128)(2,1)} %shard_map.37), calls=%async_computation | async-start | bytes 2097152 | tf_op jit(solution)/shard_map/all_to_all | solution.py:90
  13.0 17.1 %collective-permute-start.1 = (bf16[16,2,2,32,128]{4,3,2,1,0:T(8,128)(2,1)S(1)}, bf16[16,2,2,32,128]{4,3,2,1,0:T(8,128)(2,1)S(1)}, u32[]{:S(2)}, u32[]{:S(2)}) collective-permute-start(bf16[16,2,2,32,128]{4,3,2,1,0:T(8,128)(2,1)S(1)} %get-tuple-element.5), channel_id=1, source_target_pairs={{16,0},{32,16},{48,32},{64,48},{80,64},{96,80},{112,96},{128,112},... | collective-permute-start | bytes 1572872 | tf_op jit(solution)/shard_map/ppermute | solution.py:118
  14.3 32.0 %collective-permute-start = (bf16[16,2,2,32,128]{4,3,2,1,0:T(8,128)(2,1)S(1)}, bf16[16,2,2,32,128]{4,3,2,1,0:T(8,128)(2,1)S(1)}, u32[]{:S(2)}, u32[]{:S(2)}) collective-permute-start(bf16[16,2,2,32,128]{4,3,2,1,0:T(8,128)(2,1)S(1)} %get-tuple-element.6), channel_id=1, source_target_pairs={{0,16},{16,32},{32,48},{48,64},{64,80},{80,96},{96,112},{112,128},... | collective-permute-start | bytes 1572872 | tf_op jit(solution)/shard_map/ppermute | solution.py:117
  30.1 16.2 %copy-start = (bf16[16,2,2,32,128]{4,3,2,1,0:T(8,128)(2,1)}, bf16[16,2,2,32,128]{4,3,2,1,0:T(8,128)(2,1)S(1)}, u32[]{:S(2)}) copy-start(bf16[16,2,2,32,128]{4,3,2,1,0:T(8,128)(2,1)S(1)} %collective-permute-done.1.high_ref) | copy-start | bytes 1572868
  46.3 0.8 copy-start.1
  52.8 10.2 %copy-start.2 = (s32[256]{0:T(256)S(1)}, s32[256]{0:T(256)}, u32[]{:S(2)}) copy-start(s32[256]{0:T(256)} %param.4) | copy-start | bytes 3076
  52.8 37.1 %all-to-all-start.1 = ((bf16[16,16,2,16,128]{4,3,2,1,0:T(8,128)(2,1)}), bf16[16,16,2,16,128]{4,3,2,1,0:T(8,128)(2,1)S(1)}, u32[]{:S(2)}, u32[]{:S(2)}) async-start(bf16[16,16,2,16,128]{4,3,2,1,0:T(8,128)(2,1)} %shard_map.38), calls=%async_computation.1 | async-start | bytes 4194304 | tf_op jit(solution)/shard_map/all_to_all | solution.py:90
  92.4 13.1 %copy-start.3 = (s32[16]{0:T(128)S(1)}, s32[16]{0:T(128)}, u32[]{:S(2)}) copy-start(s32[16]{0:T(128)} %param.5) | copy-start | bytes 196

commit v11 on v10

--- a/solution.py
+++ b/solution.py
@@ -97,11 +97,14 @@
         "bs,skz->bkz", onehot.astype(jnp.bfloat16), columns, preferred_element_type=jnp.float32
     )
     bin_means = bin_sums / bin_counts[:, None, None]
+    high = lax.reduce_precision(bin_means, exponent_bits=8, mantissa_bits=7)
+    rest = bin_means - high
+    middle = lax.reduce_precision(rest, exponent_bits=8, mantissa_bits=7)
+    split = jnp.concatenate([high, middle, rest - middle], axis=0).astype(jnp.bfloat16)
     selected = jnp.einsum(
         "sb,bkz->skz",
-        onehot.T.astype(jnp.float32),
-        bin_means,
-        precision=lax.Precision.HIGHEST,
+        jnp.tile(onehot.T.astype(jnp.bfloat16), (1, 3)),
+        split,
         preferred_element_type=jnp.float32,
     )
     fluct = (columns.astype(jnp.float32) - selected).astype(jnp.bfloat16)
@@ -139,8 +142,10 @@
         "kt,atr->kra", owned, tiles, precision=lax.Precision.HIGHEST, preferred_element_type=jnp.float32
     )
     lanes = 128
-    mine = all_to_all_sum(tiles.reshape(tile_count, -1, lanes), "space")
-    return mine.reshape(1, total_snaps // tile_count, -1)
+    cols = tiles.shape[2]
+    padded = jnp.pad(tiles, ((0, 0), (0, 0), (0, lanes - cols)))
+    mine = all_to_all_sum(padded, "space")
+    return mine[None, :, :cols]
 
 
 def solution(mesh):

time: 124 us -> 124 us (level)
    dot_general x2 -> x0, matrix products: 2.98 us -> none  [fluctuation_of(): jnp.einsum('sb,bkz->skz', onehot.T.astype(jnp.float32), bin_means, precis...]
    dot_general x2, matrix products: 2.45 us -> 5.26 us  [fluctuation_of(): jnp.einsum('skz,tkz->st', fluct, fluct, preferred_element_type=jnp.float32)]
where the time goes in v11:
time: 124 us
  waiting for transfers between devices  50.9 us (41%)
  blocking collectives  28.7 us (23%)
  starting transfers between devices  24.3 us (20%)
  Pallas kernels  10 us (8%)
  matrix products  6.54 us (5%)
  local copies, waits for them, and re-layouts  3.07 us (2%)
    all_to_all x2, blocking collectives, all_to_all_sum(): got = lax.all_to_all(x, axis, split_axis=0, concat_axis=0, tiled=True)  28.7 us
    all_to_all x2, waiting for transfers between devices, exchange(): lax.all_to_all(parts, 'snap', split_axis=0, concat_axis=0, tiled=True)  24.4 us
    all_to_all x2, starting transfers between devices, exchange(): lax.all_to_all(parts, 'snap', split_axis=0, concat_axis=0, tiled=True)  17.5 us
    ppermute x1, waiting for transfers between devices, body(): low = lax.ppermute(velocity[:, 1:3, cells_x - 2:], 'space', forward)  16.2 us
    ppermute x1, waiting for transfers between devices, body(): high = lax.ppermute(velocity[:, 1:3, :2], 'space', backward)  10.3 us
    pallas_call x2, Pallas kernels, curl_call(): pl.pallas_call(kernel, grid=(snaps_dev // block,), in_specs=[vel_spec] +...  10 us
    ppermute x1, starting transfers between devices, body(): low = lax.ppermute(velocity[:, 1:3, cells_x - 2:], 'space', forward)  5.56 us
    dot_general x2, matrix products, fluctuation_of(): jnp.einsum('skz,tkz->st', fluct, fluct, preferred_element_type=jnp.float32)  5.26 us
  transfers between devices with their start and end apart: 4, of which 3 were waited for; matrix products, arithmetic and copies ran while one was open for 3% of the time, Pallas kernels for 5%

profile of v11, /device:TPU:1, one launch (start us, length us, event | category | flops | bytes accessed | tf_op | source)
XLA Modules:
  0.0 123.9 jit_solution(1045875508908907219)
XLA Ops:
  0.0 4.4 %shard_map.37 = bf16[16,16,1,16,128]{4,3,2,1,0:T(8,128)(2,1)} custom-call(bf16[16,3,8,32,128]{4,3,2,1,0:T(8,128)(2,1)} %vel_ref.3), custom_call_target="tpu_custom_call" | custom-call | tf_op jit(solution)/shard_map/pallas_call | solution.py:75
  4.4 7.3 %all-to-all-start = ((bf16[16,16,1,16,128]{4,3,2,1,0:T(8,128)(2,1)}), bf16[16,16,1,16,128]{4,3,2,1,0:T(8,128)(2,1)S(1)}, u32[]{:S(2)}, u32[]{:S(2)}) async-start(bf16[16,16,1,16,128]{4,3,2,1,0:T(8,128)(2,1)} %shard_map.37), calls=%async_computation | async-start | bytes 2097152 | tf_op jit(solution)/shard_map/all_to_all | solution.py:90
  11.7 1.3 %fusion.51 = (bf16[16,2,2,32,128]{4,3,2,1,0:T(8,128)(2,1)S(1)}, bf16[16,2,2,32,128]{4,3,2,1,0:T(8,128)(2,1)S(1)}) fusion(bf16[16,3,8,32,128]{4,3,2,1,0:T(8,128)(2,1)} %vel_ref.3), kind=kLoop, calls=%fused_computation.49 | loop fusion | bytes 2097152 | tf_op jit(solution)/shard_map/slice | solution.py:121
  13.0 1.3 %collective-permute-start.1 = (bf16[16,2,2,32,128]{4,3,2,1,0:T(8,128)(2,1)S(1)}, bf16[16,2,2,32,128]{4,3,2,1,0:T(8,128)(2,1)S(1)}, u32[]{:S(2)}, u32[]{:S(2)}) collective-permute-start(bf16[16,2,2,32,128]{4,3,2,1,0:T(8,128)(2,1)S(1)} %get-tuple-element.5), channel_id=1, source_target_pairs={{16,0},{32,16},{48,32},{64,48},{80,64},{96,80},{112,96},{128,112},... | collective-permute-start | bytes 1572872 | tf_op jit(solution)/shard_map/ppermute | solution.py:121
  14.3 5.6 %collective-permute-start = (bf16[16,2,2,32,128]{4,3,2,1,0:T(8,128)(2,1)S(1)}, bf16[16,2,2,32,128]{4,3,2,1,0:T(8,128)(2,1)S(1)}, u32[]{:S(2)}, u32[]{:S(2)}) collective-permute-start(bf16[16,2,2,32,128]{4,3,2,1,0:T(8,128)(2,1)S(1)} %get-tuple-element.6), channel_id=1, source_target_pairs={{0,16},{16,32},{32,48},{48,64},{64,80},{80,96},{96,112},{112,128},... | collective-permute-start | bytes 1572872 | tf_op jit(solution)/shard_map/ppermute | solution.py:120
  19.9 10.3 %collective-permute-done.1.high_ref = bf16[16,2,2,32,128]{4,3,2,1,0:T(8,128)(2,1)S(1)} collective-permute-done((bf16[16,2,2,32,128]{4,3,2,1,0:T(8,128)(2,1)S(1)}, bf16[16,2,2,32,128]{4,3,2,1,0:T(8,128)(2,1)S(1)}, u32[]{:S(2)}, u32[]{:S(2)}) %collective-permute-start.1) | collective-permute-done | bytes 524320 | tf_op jit(solution)/shard_map/ppermute | solution.py:121
  30.1 0.0 copy-start
  30.1 16.2 %collective-permute-done.low_ref = bf16[16,2,2,32,128]{4,3,2,1,0:T(8,128)(2,1)S(1)} collective-permute-done((bf16[16,2,2,32,128]{4,3,2,1,0:T(8,128)(2,1)S(1)}, bf16[16,2,2,32,128]{4,3,2,1,0:T(8,128)(2,1)S(1)}, u32[]{:S(2)}, u32[]{:S(2)}) %collective-permute-start) | collective-permute-done | bytes 524320 | tf_op jit(solution)/shard_map/ppermute | solution.py:120
  46.3 0.0 copy-done
  46.3 0.0 copy-start.1
  46.3 0.8 copy-done.1
  47.1 5.6 %shard_map.38 = bf16[16,16,2,16,128]{4,3,2,1,0:T(8,128)(2,1)} custom-call(bf16[16,3,8,32,128]{4,3,2,1,0:T(8,128)(2,1)} %vel_ref.3, bf16[16,2,2,32,128]{4,3,2,1,0:T(8,128)(2,1)} %copy-done.1, bf16[16,2,2,32,128]{4,3,2,1,0:T(8,128)(2,1)} %copy-done), custom_call_target="tpu_custom_call" | custom-call | tf_op jit(solution)/shard_map/pallas_call | solution.py:75
  52.8 0.0 copy-start.2
  52.8 0.0 all-to-all-done
  52.8 10.2 %all-to-all-start.1 = ((bf16[16,16,2,16,128]{4,3,2,1,0:T(8,128)(2,1)}), bf16[16,16,2,16,128]{4,3,2,1,0:T(8,128)(2,1)S(1)}, u32[]{:S(2)}, u32[]{:S(2)}) async-start(bf16[16,16,2,16,128]{4,3,2,1,0:T(8,128)(2,1)} %shard_map.38), calls=%async_computation.1 | async-start | bytes 4194304 | tf_op jit(solution)/shard_map/all_to_all | solution.py:90
  63.0 0.0 copy-done.2
  63.0 0.1 convert_reduce_fusion
  63.1 0.3 reduce-precision_convert_fusion.3
  63.4 2.1 %fusion.11 = f32[256,256]{1,0:T(8,128)} fusion(bf16[256,72,1]{0,1,2:T(8,128)(2,1)S(1)} %bitcast.37, bf16[256,16,128]{2,1,0:T(8,128)(2,1)S(1)} %bitcast.35, bf16[24,16,128]{2,0,1:T(8,128)(2,1)S(1)} %get-tuple-element.11, bf16[24,16,128]{2,0,1:T(8,128)(2,1)S(1)} %get-tuple-element.12, bf16[24,16,128]{2,0,1:T(8,128)(2,1)S(1)} %get-tuple-element.10), kind=kOutput, calls=%fused_computation.10 | convolution fusion | flops 346390528 | bytes 1642496 | tf_op jit(solution)/shard_map/skz,tkz->st/dot_general | solution.py:111
  65.5 0.0 copy-start.4
  65.5 24.4 %all-to-all-done.1 = bf16[16,16,2,16,128]{4,3,2,1,0:T(8,128)(2,1)S(1)} async-done(((bf16[16,16,2,16,128]{4,3,2,1,0:T(8,128)(2,1)}), bf16[16,16,2,16,128]{4,3,2,1,0:T(8,128)(2,1)S(1)}, u32[]{:S(2)}, u32[]{:S(2)}) %all-to-all-start.1) | async-done | bytes 2097184 | tf_op jit(solution)/shard_map/all_to_all | solution.py:90
  89.9 0.7 reduce-precision_convert_fusion.1
  90.6 0.0 copy-done.4
  90.6 0.0 copy-start.3
  90.6 3.2 %fusion.13 = f32[256,256]{1,0:T(8,128)S(1)} fusion(f32[256,256]{1,0:T(8,128)S(1)} %copy-done.4, bf16[256,72,1]{0,1,2:T(8,128)(2,1)S(1)} %bitcast.38, bf16[256,32,128]{2,1,0:T(8,128)(2,1)S(1)} %bitcast.33, bf16[24,32,128]{2,0,1:T(8,128)(2,1)S(1)} %get-tuple-element.8, bf16[24,32,128]{2,0,1:T(8,128)(2,1)S(1)} %get-tuple-element.9, ...), kind=kOutput, calls=%fused_computation.12 | convolution fusion | flops 692912128 | bytes 3248128 | tf_op jit(solution)/shard_map/skz,tkz->st/dot_general | solution.py:111
  93.8 11.0 %all_to_all.20 = f32[16,16,256]{2,1,0:T(8,128)S(1)} all-to-all(f32[16,16,256]{2,1,0:T(8,128)S(1)} %bitcast.36), channel_id=1, replica_groups=mesh['space'=16,'snap'=16] {'snap'}, dimensions={0} | all-to-all | bytes 524288 | tf_op jit(solution)/shard_map/all_to_all | solution.py:85
  104.8 0.1 reshape.39
  104.9 0.0 copy-done.3
  104.9 0.3 convolution_bitcast_fusion
  105.2 0.1 copy.24
  105.3 17.8 %all_to_all.21 = f32[16,16,128]{2,1,0:T(8,128)S(1)} all-to-all(f32[16,16,128]{2,1,0:T(8,128)S(1)} %pad.4.clone), channel_id=1, replica_groups=mesh['space'=16,'snap'=16] {'space'}, dimensions={0} | all-to-all | bytes 262144 | tf_op jit(solution)/shard_map/all_to_all | solution.py:85
  123.1 0.1 copy.23
  123.2 0.7 copy.20
  (5 shorter events, 0.1 us)
Async XLA Ops:
  4.4 48.4 %all-to-all-start = ((bf16[16,16,1,16,128]{4,3,2,1,0:T(8,128)(2,1)}), bf16[16,16,1,16,128]{4,3,2,1,0:T(8,128)(2,1)S(1)}, u32[]{:S(2)}, u32[]{:S(2)}) async-start(bf16[16,16,1,16,128]{4,3,2,1,0:T(8,128)(2,1)} %shard_map.37), calls=%async_computation | async-start | bytes 2097152 | tf_op jit(solution)/shard_map/all_to_all | solution.py:90
  13.0 17.1 %collective-permute-start.1 = (bf16[16,2,2,32,128]{4,3,2,1,0:T(8,128)(2,1)S(1)}, bf16[16,2,2,32,128]{4,3,2,1,0:T(8,128)(2,1)S(1)}, u32[]{:S(2)}, u32[]{:S(2)}) collective-permute-start(bf16[16,2,2,32,128]{4,3,2,1,0:T(8,128)(2,1)S(1)} %get-tuple-element.5), channel_id=1, source_target_pairs={{16,0},{32,16},{48,32},{64,48},{80,64},{96,80},{112,96},{128,112},... | collective-permute-start | bytes 1572872 | tf_op jit(solution)/shard_map/ppermute | solution.py:121
  14.3 32.0 %collective-permute-start = (bf16[16,2,2,32,128]{4,3,2,1,0:T(8,128)(2,1)S(1)}, bf16[16,2,2,32,128]{4,3,2,1,0:T(8,128)(2,1)S(1)}, u32[]{:S(2)}, u32[]{:S(2)}) collective-permute-start(bf16[16,2,2,32,128]{4,3,2,1,0:T(8,128)(2,1)S(1)} %get-tuple-element.6), channel_id=1, source_target_pairs={{0,16},{16,32},{32,48},{48,64},{64,80},{80,96},{96,112},{112,128},... | collective-permute-start | bytes 1572872 | tf_op jit(solution)/shard_map/ppermute | solution.py:120
  30.1 16.2 %copy-start = (bf16[16,2,2,32,128]{4,3,2,1,0:T(8,128)(2,1)}, bf16[16,2,2,32,128]{4,3,2,1,0:T(8,128)(2,1)S(1)}, u32[]{:S(2)}) copy-start(bf16[16,2,2,32,128]{4,3,2,1,0:T(8,128)(2,1)S(1)} %collective-permute-done.1.high_ref) | copy-start | bytes 1572868
  46.3 0.8 copy-start.1
  52.8 10.2 %copy-start.2 = (s32[256]{0:T(256)S(1)}, s32[256]{0:T(256)}, u32[]{:S(2)}) copy-start(s32[256]{0:T(256)} %param.4) | copy-start | bytes 3076
  52.8 37.1 %all-to-all-start.1 = ((bf16[16,16,2,16,128]{4,3,2,1,0:T(8,128)(2,1)}), bf16[16,16,2,16,128]{4,3,2,1,0:T(8,128)(2,1)S(1)}, u32[]{:S(2)}, u32[]{:S(2)}) async-start(bf16[16,16,2,16,128]{4,3,2,1,0:T(8,128)(2,1)} %shard_map.38), calls=%async_computation.1 | async-start | bytes 4194304 | tf_op jit(solution)/shard_map/all_to_all | solution.py:90
  65.5 25.1 %copy-start.4 = (f32[256,256]{1,0:T(8,128)S(1)}, f32[256,256]{1,0:T(8,128)}, u32[]{:S(2)}) copy-start(f32[256,256]{1,0:T(8,128)} %fusion.11) | copy-start | bytes 786436
  90.6 14.3 %copy-start.3 = (s32[16]{0:T(128)S(1)}, s32[16]{0:T(128)}, u32[]{:S(2)}) copy-start(s32[16]{0:T(128)} %param.5) | copy-start | bytes 196

commit v12 on v11

--- a/solution.py
+++ b/solution.py
@@ -138,14 +138,16 @@
     tile_ids = jnp.arange(tile_count, dtype=jnp.int32)
     owned = (tile_owner[None, :] == tile_ids[:, None]).astype(jnp.float32)
     tiles = col_sum.reshape(col_sum.shape[0], tile_count, total_snaps // tile_count)
+    high = lax.reduce_precision(tiles, exponent_bits=8, mantissa_bits=7)
+    rest = tiles - high
+    middle = lax.reduce_precision(rest, exponent_bits=8, mantissa_bits=7)
+    split = jnp.concatenate([high, middle, rest - middle], axis=1).astype(jnp.bfloat16)
     tiles = jnp.einsum(
-        "kt,atr->kra", owned, tiles, precision=lax.Precision.HIGHEST, preferred_element_type=jnp.float32
+        "kt,atr->kra", jnp.tile(owned.astype(jnp.bfloat16), (1, 3)), split, preferred_element_type=jnp.float32
     )
     lanes = 128
-    cols = tiles.shape[2]
-    padded = jnp.pad(tiles, ((0, 0), (0, 0), (0, lanes - cols)))
-    mine = all_to_all_sum(padded, "space")
-    return mine[None, :, :cols]
+    mine = all_to_all_sum(tiles.reshape(tile_count, -1, lanes), "space")
+    return mine.reshape(1, total_snaps // tile_count, -1)
 
 
 def solution(mesh):

time: 124 us -> 124 us (level)
  blocking collectives: 28.7 us -> 16.7 us
  waiting for transfers between devices: 50.9 us -> 58.5 us
  starting transfers between devices: 24.3 us -> 26.7 us
    all_to_all x2 -> x1, blocking collectives: 28.7 us -> 16.7 us  [all_to_all_sum(): got = lax.all_to_all(x, axis, split_axis=0, concat_axis=0, tiled=True)]
    ppermute x1, waiting for transfers between devices: 16.2 us -> 26.9 us  [body(): low = lax.ppermute(velocity[:, 1:3, cells_x - 2:], 'space', forward)]
    ppermute x1, waiting for transfers between devices: 10.3 us -> 0.01 us  [body(): high = lax.ppermute(velocity[:, 1:3, :2], 'space', backward)]
    all_to_all x0 -> x1, waiting for transfers between devices: none -> 7.13 us  [all_to_all_sum(): got = lax.all_to_all(x, axis, split_axis=0, concat_axis=0, tiled=True)]
    all_to_all x0 -> x1, starting transfers between devices: none -> 4.29 us  [all_to_all_sum(): got = lax.all_to_all(x, axis, split_axis=0, concat_axis=0, tiled=True)]
    all_to_all x2, starting transfers between devices: 17.5 us -> 16.2 us  [exchange(): lax.all_to_all(parts, 'snap', split_axis=0, concat_axis=0, tiled=True)]
  transfers between devices with their start and end apart: 4 -> 5, of which waited for: 3 -> 3; matrix products, arithmetic and copies ran while one was open for 3% -> 3% of each run, Pallas kernels for 5% -> 5%
where the time goes in v12:
time: 124 us; the launch traced here: 123 us
  waiting for transfers between devices  58.5 us (47%)
  starting transfers between devices  26.7 us (22%)
  blocking collectives  16.7 us (13%)
  Pallas kernels  10.1 us (8%)
  matrix products  7.18 us (6%)
  local copies, waits for them, and re-layouts  4.08 us (3%)
    ppermute x1, waiting for transfers between devices, body(): low = lax.ppermute(velocity[:, 1:3, cells_x - 2:], 'space', forward)  26.9 us
    all_to_all x2, waiting for transfers between devices, exchange(): lax.all_to_all(parts, 'snap', split_axis=0, concat_axis=0, tiled=True)  24.4 us
    all_to_all x1, blocking collectives, all_to_all_sum(): got = lax.all_to_all(x, axis, split_axis=0, concat_axis=0, tiled=True)  16.7 us
    all_to_all x2, starting transfers between devices, exchange(): lax.all_to_all(parts, 'snap', split_axis=0, concat_axis=0, tiled=True)  16.2 us
    pallas_call x2, Pallas kernels, curl_call(): pl.pallas_call(kernel, grid=(snaps_dev // block,), in_specs=[vel_spec] +...  10.1 us
    all_to_all x1, waiting for transfers between devices, all_to_all_sum(): got = lax.all_to_all(x, axis, split_axis=0, concat_axis=0, tiled=True)  7.13 us
    dot_general x2, matrix products, fluctuation_of(): jnp.einsum('skz,tkz->st', fluct, fluct, preferred_element_type=jnp.float32)  5.96 us
    ppermute x1, starting transfers between devices, body(): low = lax.ppermute(velocity[:, 1:3, cells_x - 2:], 'space', forward)  4.93 us
  transfers between devices with their start and end apart: 5, of which 3 were waited for; matrix products, arithmetic and copies ran while one was open for 3% of the time, Pallas kernels for 5%

profile of v12, /device:TPU:1, one launch (start us, length us, event | category | flops | bytes accessed | tf_op | source)
XLA Modules:
  0.0 123.5 jit_solution(4698464139388049175)
XLA Ops:
  0.0 4.4 %shard_map.37 = bf16[16,16,1,16,128]{4,3,2,1,0:T(8,128)(2,1)} custom-call(bf16[16,3,8,32,128]{4,3,2,1,0:T(8,128)(2,1)} %vel_ref.3), custom_call_target="tpu_custom_call" | custom-call | tf_op jit(solution)/shard_map/pallas_call | solution.py:75
  4.4 7.3 %all-to-all-start = ((bf16[16,16,1,16,128]{4,3,2,1,0:T(8,128)(2,1)}), bf16[16,16,1,16,128]{4,3,2,1,0:T(8,128)(2,1)S(1)}, u32[]{:S(2)}, u32[]{:S(2)}) async-start(bf16[16,16,1,16,128]{4,3,2,1,0:T(8,128)(2,1)} %shard_map.37), calls=%async_computation | async-start | bytes 2097152 | tf_op jit(solution)/shard_map/all_to_all | solution.py:90
  11.7 1.3 %fusion.55 = (bf16[16,2,2,32,128]{4,3,2,1,0:T(8,128)(2,1)S(1)}, bf16[16,2,2,32,128]{4,3,2,1,0:T(8,128)(2,1)S(1)}) fusion(bf16[16,3,8,32,128]{4,3,2,1,0:T(8,128)(2,1)} %vel_ref.3), kind=kLoop, calls=%fused_computation.59 | loop fusion | bytes 2097152 | tf_op jit(solution)/shard_map/slice | solution.py:121
  13.0 4.9 %collective-permute-start = (bf16[16,2,2,32,128]{4,3,2,1,0:T(8,128)(2,1)S(1)}, bf16[16,2,2,32,128]{4,3,2,1,0:T(8,128)(2,1)S(1)}, u32[]{:S(2)}, u32[]{:S(2)}) collective-permute-start(bf16[16,2,2,32,128]{4,3,2,1,0:T(8,128)(2,1)S(1)} %get-tuple-element.6), channel_id=1, source_target_pairs={{0,16},{16,32},{32,48},{48,64},{64,80},{80,96},{96,112},{112,128},... | collective-permute-start | bytes 1572872 | tf_op jit(solution)/shard_map/ppermute | solution.py:120
  17.9 1.3 %collective-permute-start.1 = (bf16[16,2,2,32,128]{4,3,2,1,0:T(8,128)(2,1)S(1)}, bf16[16,2,2,32,128]{4,3,2,1,0:T(8,128)(2,1)S(1)}, u32[]{:S(2)}, u32[]{:S(2)}) collective-permute-start(bf16[16,2,2,32,128]{4,3,2,1,0:T(8,128)(2,1)S(1)} %get-tuple-element.5), channel_id=1, source_target_pairs={{16,0},{32,16},{48,32},{64,48},{80,64},{96,80},{112,96},{128,112},... | collective-permute-start | bytes 1572872 | tf_op jit(solution)/shard_map/ppermute | solution.py:121
  19.2 26.9 %collective-permute-done.low_ref = bf16[16,2,2,32,128]{4,3,2,1,0:T(8,128)(2,1)S(1)} collective-permute-done((bf16[16,2,2,32,128]{4,3,2,1,0:T(8,128)(2,1)S(1)}, bf16[16,2,2,32,128]{4,3,2,1,0:T(8,128)(2,1)S(1)}, u32[]{:S(2)}, u32[]{:S(2)}) %collective-permute-start) | collective-permute-done | bytes 524320 | tf_op jit(solution)/shard_map/ppermute | solution.py:120
  46.1 0.0 copy-start
  46.1 0.0 collective-permute-done.1.high_ref
  46.1 0.8 copy-done
  46.9 0.0 copy-start.1
  46.9 0.8 copy-done.1
  47.7 5.7 %shard_map.38 = bf16[16,16,2,16,128]{4,3,2,1,0:T(8,128)(2,1)} custom-call(bf16[16,3,8,32,128]{4,3,2,1,0:T(8,128)(2,1)} %vel_ref.3, bf16[16,2,2,32,128]{4,3,2,1,0:T(8,128)(2,1)} %copy-done, bf16[16,2,2,32,128]{4,3,2,1,0:T(8,128)(2,1)} %copy-done.1), custom_call_target="tpu_custom_call" | custom-call | tf_op jit(solution)/shard_map/pallas_call | solution.py:75
  53.4 0.0 copy-start.2
  53.4 0.0 all-to-all-done
  53.4 8.8 %all-to-all-start.1 = ((bf16[16,16,2,16,128]{4,3,2,1,0:T(8,128)(2,1)}), bf16[16,16,2,16,128]{4,3,2,1,0:T(8,128)(2,1)S(1)}, u32[]{:S(2)}, u32[]{:S(2)}) async-start(bf16[16,16,2,16,128]{4,3,2,1,0:T(8,128)(2,1)} %shard_map.38), calls=%async_computation.1 | async-start | bytes 4194304 | tf_op jit(solution)/shard_map/all_to_all | solution.py:90
  62.2 0.0 copy-done.2
  62.3 0.1 convert_reduce_fusion
  62.4 0.3 reduce-precision_convert_fusion.3
  62.7 2.1 %fusion.11 = f32[256,256]{1,0:T(8,128)} fusion(bf16[256,72,1]{0,1,2:T(8,128)(2,1)S(1)} %bitcast.31, bf16[256,16,128]{2,1,0:T(8,128)(2,1)S(1)} %bitcast.30, bf16[24,16,128]{2,0,1:T(8,128)(2,1)S(1)} %get-tuple-element.11, bf16[24,16,128]{2,0,1:T(8,128)(2,1)S(1)} %get-tuple-element.12, bf16[24,16,128]{2,0,1:T(8,128)(2,1)S(1)} %get-tuple-element.10), kind=kOutput, calls=%fused_computation.10 | convolution fusion | flops 346390528 | bytes 1642496 | tf_op jit(solution)/shard_map/skz,tkz->st/dot_general | solution.py:111
  64.8 0.0 copy-start.4
  64.8 24.4 %all-to-all-done.1 = bf16[16,16,2,16,128]{4,3,2,1,0:T(8,128)(2,1)S(1)} async-done(((bf16[16,16,2,16,128]{4,3,2,1,0:T(8,128)(2,1)}), bf16[16,16,2,16,128]{4,3,2,1,0:T(8,128)(2,1)S(1)}, u32[]{:S(2)}, u32[]{:S(2)}) %all-to-all-start.1) | async-done | bytes 2097184 | tf_op jit(solution)/shard_map/all_to_all | solution.py:90
  89.2 0.7 reduce-precision_convert_fusion.1
  89.9 0.0 copy-done.4
  89.9 0.0 copy-start.3
  89.9 3.9 %fusion.13 = f32[256,256]{1,0:T(8,128)} fusion(f32[256,256]{1,0:T(8,128)S(1)} %copy-done.4, bf16[256,72,1]{0,1,2:T(8,128)(2,1)S(1)} %bitcast.32, bf16[256,32,128]{2,1,0:T(8,128)(2,1)S(1)} %bitcast.28, bf16[24,32,128]{2,0,1:T(8,128)(2,1)S(1)} %get-tuple-element.8, bf16[24,32,128]{2,0,1:T(8,128)(2,1)S(1)} %get-tuple-element.9, ...), kind=kOutput, calls=%fused_computation.12 | convolution fusion | flops 692912128 | bytes 3248128 | tf_op jit(solution)/shard_map/skz,tkz->st/dot_general | solution.py:111
  93.8 4.3 %all-to-all-start.2 = ((f32[16,16,256]{2,1,0:T(8,128)}), f32[16,16,256]{2,1,0:T(8,128)S(1)}, u32[]{:S(2)}, u32[]{:S(2)}) async-start(f32[16,16,256]{2,1,0:T(8,128)} %bitcast.8), calls=%async_computation.2 | async-start | bytes 524288 | tf_op jit(solution)/shard_map/all_to_all | solution.py:85
  98.1 0.0 copy-done.3
  98.1 0.1 reshape.76
  98.2 7.1 %all-to-all-done.2 = f32[16,16,256]{2,1,0:T(8,128)S(1)} async-done(((f32[16,16,256]{2,1,0:T(8,128)}), f32[16,16,256]{2,1,0:T(8,128)S(1)}, u32[]{:S(2)}, u32[]{:S(2)}) %all-to-all-start.2) | async-done | bytes 262176 | tf_op jit(solution)/shard_map/all_to_all | solution.py:85
  105.4 0.1 reshape.69
  105.5 0.1 copy.12
  105.6 0.2 convolution_bitcast_fusion
  105.8 0.1 copy.14
  106.0 0.1 reshape.70
  106.1 16.7 %all_to_all.20 = f32[16,2,128]{2,1,0:T(2,128)S(1)} all-to-all(f32[16,2,128]{2,1,0:T(2,128)S(1)} %reshape.70), channel_id=1, replica_groups=mesh['space'=16,'snap'=16] {'space'}, dimensions={0} | all-to-all | bytes 32768 | tf_op jit(solution)/shard_map/all_to_all | solution.py:85
  122.8 0.7 reshape.71
  (7 shorter events, 0.1 us)
Async XLA Ops:
  4.4 49.0 %all-to-all-start = ((bf16[16,16,1,16,128]{4,3,2,1,0:T(8,128)(2,1)}), bf16[16,16,1,16,128]{4,3,2,1,0:T(8,128)(2,1)S(1)}, u32[]{:S(2)}, u32[]{:S(2)}) async-start(bf16[16,16,1,16,128]{4,3,2,1,0:T(8,128)(2,1)} %shard_map.37), calls=%async_computation | async-start | bytes 2097152 | tf_op jit(solution)/shard_map/all_to_all | solution.py:90
  13.0 33.1 %collective-permute-start = (bf16[16,2,2,32,128]{4,3,2,1,0:T(8,128)(2,1)S(1)}, bf16[16,2,2,32,128]{4,3,2,1,0:T(8,128)(2,1)S(1)}, u32[]{:S(2)}, u32[]{:S(2)}) collective-permute-start(bf16[16,2,2,32,128]{4,3,2,1,0:T(8,128)(2,1)S(1)} %get-tuple-element.6), channel_id=1, source_target_pairs={{0,16},{16,32},{32,48},{48,64},{64,80},{80,96},{96,112},{112,128},... | collective-permute-start | bytes 1572872 | tf_op jit(solution)/shard_map/ppermute | solution.py:120
  17.9 28.2 %collective-permute-start.1 = (bf16[16,2,2,32,128]{4,3,2,1,0:T(8,128)(2,1)S(1)}, bf16[16,2,2,32,128]{4,3,2,1,0:T(8,128)(2,1)S(1)}, u32[]{:S(2)}, u32[]{:S(2)}) collective-permute-start(bf16[16,2,2,32,128]{4,3,2,1,0:T(8,128)(2,1)S(1)} %get-tuple-element.5), channel_id=1, source_target_pairs={{16,0},{32,16},{48,32},{64,48},{80,64},{96,80},{112,96},{128,112},... | collective-permute-start | bytes 1572872 | tf_op jit(solution)/shard_map/ppermute | solution.py:121
  46.1 0.8 copy-start
  46.9 0.8 copy-start.1
  53.4 8.8 %copy-start.2 = (s32[256]{0:T(256)S(1)}, s32[256]{0:T(256)}, u32[]{:S(2)}) copy-start(s32[256]{0:T(256)} %param.4) | copy-start | bytes 3076
  53.4 35.8 %all-to-all-start.1 = ((bf16[16,16,2,16,128]{4,3,2,1,0:T(8,128)(2,1)}), bf16[16,16,2,16,128]{4,3,2,1,0:T(8,128)(2,1)S(1)}, u32[]{:S(2)}, u32[]{:S(2)}) async-start(bf16[16,16,2,16,128]{4,3,2,1,0:T(8,128)(2,1)} %shard_map.38), calls=%async_computation.1 | async-start | bytes 4194304 | tf_op jit(solution)/shard_map/all_to_all | solution.py:90
  64.8 25.1 %copy-start.4 = (f32[256,256]{1,0:T(8,128)S(1)}, f32[256,256]{1,0:T(8,128)}, u32[]{:S(2)}) copy-start(f32[256,256]{1,0:T(8,128)} %fusion.11) | copy-start | bytes 786436
  89.9 8.2 %copy-start.3 = (s32[16]{0:T(128)S(1)}, s32[16]{0:T(128)}, u32[]{:S(2)}) copy-start(s32[16]{0:T(128)} %param.5) | copy-start | bytes 196
  93.8 11.5 %all-to-all-start.2 = ((f32[16,16,256]{2,1,0:T(8,128)}), f32[16,16,256]{2,1,0:T(8,128)S(1)}, u32[]{:S(2)}, u32[]{:S(2)}) async-start(f32[16,16,256]{2,1,0:T(8,128)} %bitcast.8), calls=%async_computation.2 | async-start | bytes 524288 | tf_op jit(solution)/shard_map/all_to_all | solution.py:85

commit v13 on v12

--- a/solution.py
+++ b/solution.py
@@ -138,12 +138,8 @@
     tile_ids = jnp.arange(tile_count, dtype=jnp.int32)
     owned = (tile_owner[None, :] == tile_ids[:, None]).astype(jnp.float32)
     tiles = col_sum.reshape(col_sum.shape[0], tile_count, total_snaps // tile_count)
-    high = lax.reduce_precision(tiles, exponent_bits=8, mantissa_bits=7)
-    rest = tiles - high
-    middle = lax.reduce_precision(rest, exponent_bits=8, mantissa_bits=7)
-    split = jnp.concatenate([high, middle, rest - middle], axis=1).astype(jnp.bfloat16)
     tiles = jnp.einsum(
-        "kt,atr->kra", jnp.tile(owned.astype(jnp.bfloat16), (1, 3)), split, preferred_element_type=jnp.float32
+        "kt,atr->kra", owned, tiles, precision=lax.Precision.HIGHEST, preferred_element_type=jnp.float32
     )
     lanes = 128
     mine = all_to_all_sum(tiles.reshape(tile_count, -1, lanes), "space")

time: 124 us -> 123 us (level)
  blocking collectives: 16.7 us -> 27.7 us
  waiting for transfers between devices: 58.5 us -> 50.9 us
  starting transfers between devices: 26.7 us -> 24.3 us
    all_to_all x1 -> x2, blocking collectives: 16.7 us -> 27.7 us  [all_to_all_sum(): got = lax.all_to_all(x, axis, split_axis=0, concat_axis=0, tiled=True)]
    ppermute x1, waiting for transfers between devices: 26.9 us -> 16.2 us  [body(): low = lax.ppermute(velocity[:, 1:3, cells_x - 2:], 'space', forward)]
    ppermute x1, waiting for transfers between devices: 0.01 us -> 10.3 us  [body(): high = lax.ppermute(velocity[:, 1:3, :2], 'space', backward)]
    all_to_all x1 -> x0, waiting for transfers between devices: 7.13 us -> none  [all_to_all_sum(): got = lax.all_to_all(x, axis, split_axis=0, concat_axis=0, tiled=True)]
    all_to_all x1 -> x0, starting transfers between devices: 4.29 us -> none  [all_to_all_sum(): got = lax.all_to_all(x, axis, split_axis=0, concat_axis=0, tiled=True)]
    all_to_all x2, starting transfers between devices: 16.2 us -> 17.5 us  [exchange(): lax.all_to_all(parts, 'snap', split_axis=0, concat_axis=0, tiled=True)]
  transfers between devices with their start and end apart: 5 -> 4, of which waited for: 3 -> 3; matrix products, arithmetic and copies ran while one was open for 3% -> 3% of each run, Pallas kernels for 5% -> 5%
where the time goes in v13:
time: 123 us
  waiting for transfers between devices  50.9 us (41%)
  blocking collectives  27.7 us (23%)
  starting transfers between devices  24.3 us (20%)
  Pallas kernels  10 us (8%)
  matrix products  6.54 us (5%)
  local copies, waits for them, and re-layouts  3.1 us (3%)
    all_to_all x2, blocking collectives, all_to_all_sum(): got = lax.all_to_all(x, axis, split_axis=0, concat_axis=0, tiled=True)  27.7 us
    all_to_all x2, waiting for transfers between devices, exchange(): lax.all_to_all(parts, 'snap', split_axis=0, concat_axis=0, tiled=True)  24.4 us
    all_to_all x2, starting transfers between devices, exchange(): lax.all_to_all(parts, 'snap', split_axis=0, concat_axis=0, tiled=True)  17.5 us
    ppermute x1, waiting for transfers between devices, body(): low = lax.ppermute(velocity[:, 1:3, cells_x - 2:], 'space', forward)  16.2 us
    ppermute x1, waiting for transfers between devices, body(): high = lax.ppermute(velocity[:, 1:3, :2], 'space', backward)  10.3 us
    pallas_call x2, Pallas kernels, curl_call(): pl.pallas_call(kernel, grid=(snaps_dev // block,), in_specs=[vel_spec] +...  10 us
    ppermute x1, starting transfers between devices, body(): low = lax.ppermute(velocity[:, 1:3, cells_x - 2:], 'space', forward)  5.56 us
    dot_general x2, matrix products, fluctuation_of(): jnp.einsum('skz,tkz->st', fluct, fluct, preferred_element_type=jnp.float32)  5.26 us
  transfers between devices with their start and end apart: 4, of which 3 were waited for; matrix products, arithmetic and copies ran while one was open for 3% of the time, Pallas kernels for 5%

profile of v13, /device:TPU:1, one launch (start us, length us, event | category | flops | bytes accessed | tf_op | source)
XLA Modules:
  0.0 122.8 jit_solution(10794483046750631336)
XLA Ops:
  0.0 4.4 %shard_map.37 = bf16[16,16,1,16,128]{4,3,2,1,0:T(8,128)(2,1)} custom-call(bf16[16,3,8,32,128]{4,3,2,1,0:T(8,128)(2,1)} %vel_ref.3), custom_call_target="tpu_custom_call" | custom-call | tf_op jit(solution)/shard_map/pallas_call | solution.py:75
  4.4 7.3 %all-to-all-start = ((bf16[16,16,1,16,128]{4,3,2,1,0:T(8,128)(2,1)}), bf16[16,16,1,16,128]{4,3,2,1,0:T(8,128)(2,1)S(1)}, u32[]{:S(2)}, u32[]{:S(2)}) async-start(bf16[16,16,1,16,128]{4,3,2,1,0:T(8,128)(2,1)} %shard_map.37), calls=%async_computation | async-start | bytes 2097152 | tf_op jit(solution)/shard_map/all_to_all | solution.py:90
  11.7 1.3 %fusion.51 = (bf16[16,2,2,32,128]{4,3,2,1,0:T(8,128)(2,1)S(1)}, bf16[16,2,2,32,128]{4,3,2,1,0:T(8,128)(2,1)S(1)}) fusion(bf16[16,3,8,32,128]{4,3,2,1,0:T(8,128)(2,1)} %vel_ref.3), kind=kLoop, calls=%fused_computation.49 | loop fusion | bytes 2097152 | tf_op jit(solution)/shard_map/slice | solution.py:121
  13.0 1.3 %collective-permute-start.1 = (bf16[16,2,2,32,128]{4,3,2,1,0:T(8,128)(2,1)S(1)}, bf16[16,2,2,32,128]{4,3,2,1,0:T(8,128)(2,1)S(1)}, u32[]{:S(2)}, u32[]{:S(2)}) collective-permute-start(bf16[16,2,2,32,128]{4,3,2,1,0:T(8,128)(2,1)S(1)} %get-tuple-element.5), channel_id=1, source_target_pairs={{16,0},{32,16},{48,32},{64,48},{80,64},{96,80},{112,96},{128,112},... | collective-permute-start | bytes 1572872 | tf_op jit(solution)/shard_map/ppermute | solution.py:121
  14.3 5.6 %collective-permute-start = (bf16[16,2,2,32,128]{4,3,2,1,0:T(8,128)(2,1)S(1)}, bf16[16,2,2,32,128]{4,3,2,1,0:T(8,128)(2,1)S(1)}, u32[]{:S(2)}, u32[]{:S(2)}) collective-permute-start(bf16[16,2,2,32,128]{4,3,2,1,0:T(8,128)(2,1)S(1)} %get-tuple-element.6), channel_id=1, source_target_pairs={{0,16},{16,32},{32,48},{48,64},{64,80},{80,96},{96,112},{112,128},... | collective-permute-start | bytes 1572872 | tf_op jit(solution)/shard_map/ppermute | solution.py:120
  19.9 10.3 %collective-permute-done.1.high_ref = bf16[16,2,2,32,128]{4,3,2,1,0:T(8,128)(2,1)S(1)} collective-permute-done((bf16[16,2,2,32,128]{4,3,2,1,0:T(8,128)(2,1)S(1)}, bf16[16,2,2,32,128]{4,3,2,1,0:T(8,128)(2,1)S(1)}, u32[]{:S(2)}, u32[]{:S(2)}) %collective-permute-start.1) | collective-permute-done | bytes 524320 | tf_op jit(solution)/shard_map/ppermute | solution.py:121
  30.1 0.0 copy-start
  30.1 16.2 %collective-permute-done.low_ref = bf16[16,2,2,32,128]{4,3,2,1,0:T(8,128)(2,1)S(1)} collective-permute-done((bf16[16,2,2,32,128]{4,3,2,1,0:T(8,128)(2,1)S(1)}, bf16[16,2,2,32,128]{4,3,2,1,0:T(8,128)(2,1)S(1)}, u32[]{:S(2)}, u32[]{:S(2)}) %collective-permute-start) | collective-permute-done | bytes 524320 | tf_op jit(solution)/shard_map/ppermute | solution.py:120
  46.3 0.0 copy-done
  46.3 0.0 copy-start.1
  46.3 0.8 copy-done.1
  47.1 5.6 %shard_map.38 = bf16[16,16,2,16,128]{4,3,2,1,0:T(8,128)(2,1)} custom-call(bf16[16,3,8,32,128]{4,3,2,1,0:T(8,128)(2,1)} %vel_ref.3, bf16[16,2,2,32,128]{4,3,2,1,0:T(8,128)(2,1)} %copy-done.1, bf16[16,2,2,32,128]{4,3,2,1,0:T(8,128)(2,1)} %copy-done), custom_call_target="tpu_custom_call" | custom-call | tf_op jit(solution)/shard_map/pallas_call | solution.py:75
  52.8 0.0 copy-start.2
  52.8 0.0 all-to-all-done
  52.8 10.2 %all-to-all-start.1 = ((bf16[16,16,2,16,128]{4,3,2,1,0:T(8,128)(2,1)}), bf16[16,16,2,16,128]{4,3,2,1,0:T(8,128)(2,1)S(1)}, u32[]{:S(2)}, u32[]{:S(2)}) async-start(bf16[16,16,2,16,128]{4,3,2,1,0:T(8,128)(2,1)} %shard_map.38), calls=%async_computation.1 | async-start | bytes 4194304 | tf_op jit(solution)/shard_map/all_to_all | solution.py:90
  63.0 0.0 copy-done.2
  63.0 0.1 convert_reduce_fusion
  63.1 0.3 reduce-precision_convert_fusion.3
  63.4 2.1 %fusion.11 = f32[256,256]{1,0:T(8,128)} fusion(bf16[256,72,1]{0,1,2:T(8,128)(2,1)S(1)} %bitcast.35, bf16[256,16,128]{2,1,0:T(8,128)(2,1)S(1)} %bitcast.33, bf16[24,16,128]{2,0,1:T(8,128)(2,1)S(1)} %get-tuple-element.11, bf16[24,16,128]{2,0,1:T(8,128)(2,1)S(1)} %get-tuple-element.12, bf16[24,16,128]{2,0,1:T(8,128)(2,1)S(1)} %get-tuple-element.10), kind=kOutput, calls=%fused_computation.10 | convolution fusion | flops 346390528 | bytes 1642496 | tf_op jit(solution)/shard_map/skz,tkz->st/dot_general | solution.py:111
  65.5 0.0 copy-start.4
  65.5 24.4 %all-to-all-done.1 = bf16[16,16,2,16,128]{4,3,2,1,0:T(8,128)(2,1)S(1)} async-done(((bf16[16,16,2,16,128]{4,3,2,1,0:T(8,128)(2,1)}), bf16[16,16,2,16,128]{4,3,2,1,0:T(8,128)(2,1)S(1)}, u32[]{:S(2)}, u32[]{:S(2)}) %all-to-all-start.1) | async-done | bytes 2097184 | tf_op jit(solution)/shard_map/all_to_all | solution.py:90
  89.9 0.7 reduce-precision_convert_fusion.1
  90.6 0.0 copy-done.4
  90.6 0.0 copy-start.3
  90.6 3.2 %fusion.13 = f32[256,256]{1,0:T(8,128)S(1)} fusion(f32[256,256]{1,0:T(8,128)S(1)} %copy-done.4, bf16[256,72,1]{0,1,2:T(8,128)(2,1)S(1)} %bitcast.36, bf16[256,32,128]{2,1,0:T(8,128)(2,1)S(1)} %bitcast.31, bf16[24,32,128]{2,0,1:T(8,128)(2,1)S(1)} %get-tuple-element.8, bf16[24,32,128]{2,0,1:T(8,128)(2,1)S(1)} %get-tuple-element.9, ...), kind=kOutput, calls=%fused_computation.12 | convolution fusion | flops 692912128 | bytes 3248128 | tf_op jit(solution)/shard_map/skz,tkz->st/dot_general | solution.py:111
  93.8 11.0 %all_to_all.20 = f32[16,16,256]{2,1,0:T(8,128)S(1)} all-to-all(f32[16,16,256]{2,1,0:T(8,128)S(1)} %bitcast.34), channel_id=1, replica_groups=mesh['space'=16,'snap'=16] {'snap'}, dimensions={0} | all-to-all | bytes 524288 | tf_op jit(solution)/shard_map/all_to_all | solution.py:85
  104.8 0.1 reshape.45
  104.9 0.0 copy-done.3
  104.9 0.3 convolution_bitcast_fusion
  105.2 0.1 copy.13
  105.3 0.1 reshape.46
  105.4 16.7 %all_to_all.21 = f32[16,2,128]{2,1,0:T(2,128)S(1)} all-to-all(f32[16,2,128]{2,1,0:T(2,128)S(1)} %reshape.46), channel_id=1, replica_groups=mesh['space'=16,'snap'=16] {'space'}, dimensions={0} | all-to-all | bytes 32768 | tf_op jit(solution)/shard_map/all_to_all | solution.py:85
  122.2 0.7 reshape.47
  (4 shorter events, 0.1 us)
Async XLA Ops:
  4.4 48.4 %all-to-all-start = ((bf16[16,16,1,16,128]{4,3,2,1,0:T(8,128)(2,1)}), bf16[16,16,1,16,128]{4,3,2,1,0:T(8,128)(2,1)S(1)}, u32[]{:S(2)}, u32[]{:S(2)}) async-start(bf16[16,16,1,16,128]{4,3,2,1,0:T(8,128)(2,1)} %shard_map.37), calls=%async_computation | async-start | bytes 2097152 | tf_op jit(solution)/shard_map/all_to_all | solution.py:90
  13.0 17.1 %collective-permute-start.1 = (bf16[16,2,2,32,128]{4,3,2,1,0:T(8,128)(2,1)S(1)}, bf16[16,2,2,32,128]{4,3,2,1,0:T(8,128)(2,1)S(1)}, u32[]{:S(2)}, u32[]{:S(2)}) collective-permute-start(bf16[16,2,2,32,128]{4,3,2,1,0:T(8,128)(2,1)S(1)} %get-tuple-element.5), channel_id=1, source_target_pairs={{16,0},{32,16},{48,32},{64,48},{80,64},{96,80},{112,96},{128,112},... | collective-permute-start | bytes 1572872 | tf_op jit(solution)/shard_map/ppermute | solution.py:121
  14.3 32.0 %collective-permute-start = (bf16[16,2,2,32,128]{4,3,2,1,0:T(8,128)(2,1)S(1)}, bf16[16,2,2,32,128]{4,3,2,1,0:T(8,128)(2,1)S(1)}, u32[]{:S(2)}, u32[]{:S(2)}) collective-permute-start(bf16[16,2,2,32,128]{4,3,2,1,0:T(8,128)(2,1)S(1)} %get-tuple-element.6), channel_id=1, source_target_pairs={{0,16},{16,32},{32,48},{48,64},{64,80},{80,96},{96,112},{112,128},... | collective-permute-start | bytes 1572872 | tf_op jit(solution)/shard_map/ppermute | solution.py:120
  30.1 16.2 %copy-start = (bf16[16,2,2,32,128]{4,3,2,1,0:T(8,128)(2,1)}, bf16[16,2,2,32,128]{4,3,2,1,0:T(8,128)(2,1)S(1)}, u32[]{:S(2)}) copy-start(bf16[16,2,2,32,128]{4,3,2,1,0:T(8,128)(2,1)S(1)} %collective-permute-done.1.high_ref) | copy-start | bytes 1572868
  46.3 0.8 copy-start.1
  52.8 10.2 %copy-start.2 = (s32[256]{0:T(256)S(1)}, s32[256]{0:T(256)}, u32[]{:S(2)}) copy-start(s32[256]{0:T(256)} %param.4) | copy-start | bytes 3076
  52.8 37.1 %all-to-all-start.1 = ((bf16[16,16,2,16,128]{4,3,2,1,0:T(8,128)(2,1)}), bf16[16,16,2,16,128]{4,3,2,1,0:T(8,128)(2,1)S(1)}, u32[]{:S(2)}, u32[]{:S(2)}) async-start(bf16[16,16,2,16,128]{4,3,2,1,0:T(8,128)(2,1)} %shard_map.38), calls=%async_computation.1 | async-start | bytes 4194304 | tf_op jit(solution)/shard_map/all_to_all | solution.py:90
  65.5 25.1 %copy-start.4 = (f32[256,256]{1,0:T(8,128)S(1)}, f32[256,256]{1,0:T(8,128)}, u32[]{:S(2)}) copy-start(f32[256,256]{1,0:T(8,128)} %fusion.11) | copy-start | bytes 786436
  90.6 14.3 %copy-start.3 = (s32[16]{0:T(128)S(1)}, s32[16]{0:T(128)}, u32[]{:S(2)}) copy-start(s32[16]{0:T(128)} %param.5) | copy-start | bytes 196
